TPU v7x, 256 devices: a whole 4x4x8 slice. The times are simulated.
256 devices in a mesh: dp: 4 (over x_lo, core), expert: 64 (over z, y, x_hi).
Axes of the slice: x: 4 (x_hi: 2, x_lo: 2; x = x_hi * 2 + x_lo), y: 4, z: 8, core: 2. Of those that a mesh axis runs over, the one named last changes fastest.
Arguments:
- prev_acts: bfloat16 [4, 64, 128, 3584], P('dp', 'expert'), may hold values from -6 to 6
- prev_cot: bfloat16 [4, 64, 128, 512], P('dp', 'expert'), may hold values from -0.59765625 to 0.59765625
- weights: bfloat16 [64, 3584, 512], P('expert', 'dp'), may hold values from -0.09375 to 0.09375
- first_moment: float32 [64, 3584, 512], P('expert', 'dp'), may hold values from -1.8 to 1.8
- second_moment: float32 [64, 3584, 512], P('expert', 'dp'), may hold values from 0.1 to 2
- tokens: bfloat16 [4, 64, 128, 3584], P('dp', 'expert'), may hold values from -6 to 6
- routing: int32 [4, 64, 128, 2], P('dp', 'expert'), may hold values from 0 to 15, all different within a row; in each aligned block of 128 rows (0 to 127, 128 to 255, ..., all dimensions but the last counted through in order) at most 24 rows name the same one
- gates: bfloat16 [4, 64, 128, 2], P('dp', 'expert'), may hold values from 0.19921875 to 1
- token_counts: int32 [4, 64], P('dp', 'expert'), may hold values from 64 to 128
- old_owner: int32 [16], replicated, may hold values from 0 to 15, each once
- new_owner: int32 [16], replicated, may hold values from 0 to 15, each once
Outputs:
- expert_hidden: bfloat16 [4, 64, 1536, 256], P('dp', 'expert')
- new_weights: bfloat16 [64, 3584, 512], P('expert', 'dp')
- new_first: float32 [64, 3584, 512], P('expert', 'dp')
- new_second: float32 [64, 3584, 512], P('expert', 'dp')
Inputs may be any that keep to these rules, and one draw needn't show every extreme that they name: `routing`: each token names 2 different hot experts; within the rows of one device no hot expert is named by more than 24 rows. `old_owner`: each is a permutation of the 16 groups. `new_owner`: each is a permutation of the 16 groups.
All inputs are finite; a program needn't handle non-finite values.
Results may differ from a plain program's by a relative error of at most 0.013.
Values may be sent and summed in bfloat16 or wider, within the bound.
No kernel may reach another device: no remote copies, remote signals or barrier semaphores. Data moves between devices by JAX's collectives and lax.ppermute only.
A program may use at most 128 MiB of HBM per device.

v0:
```python
import jax
import jax.numpy as jnp
from jax import lax
from jax.sharding import PartitionSpec as P

D = 3584
GRP = 4


beta_first = 0.9
beta_second = 0.95
learning = 0.00022
decay_rate = 0.1
epsilon = 1e-08
first_fix = 1.0 - 0.9**40
second_fix = 1.0 - 0.95**40


def adamw(weight_now, first_now, second_now, gradient):
    first_next = beta_first * first_now + (1.0 - beta_first) * gradient
    second_next = beta_second * second_now + (1.0 - beta_second) * gradient * gradient
    stepped = weight_now.astype(jnp.float32) * (1.0 - learning * decay_rate) - learning * (
        first_next / first_fix
    ) / (jnp.sqrt(second_next / second_fix) + epsilon)
    return (stepped.astype(jnp.bfloat16), jnp.stack([first_next, second_next]))


def migrate(weight_now, moment_stack, source, experts):
    rows_dev = weight_now.shape[0]
    width = weight_now.shape[1]
    layers = moment_stack.shape[0]
    piece_rows = rows_dev // experts
    weight_split = weight_now.reshape(experts, piece_rows, width)
    moment_split = moment_stack.reshape(layers, experts, piece_rows, width)
    weight_spread = lax.all_to_all(weight_split, "expert", split_axis=0, concat_axis=0, tiled=True)
    moment_spread = lax.all_to_all(moment_split, "expert", split_axis=1, concat_axis=1, tiled=True)
    weight_sorted = jnp.take(weight_spread, source, axis=0)
    moment_sorted = jnp.take(moment_spread, source, axis=1)
    weight_home = lax.all_to_all(weight_sorted, "expert", split_axis=0, concat_axis=0, tiled=True)
    moment_home = lax.all_to_all(moment_sorted, "expert", split_axis=1, concat_axis=1, tiled=True)
    return (weight_home.reshape(rows_dev, width), moment_home.reshape(layers, rows_dev, width))


def pack_tokens(token_block, route_block, gate_block, limit, hot_count, capacity):
    hot_index = jnp.arange(hot_count, dtype=jnp.int32)
    valid = jnp.arange(token_block.shape[0], dtype=jnp.int32) < limit
    hits = (route_block[:, :, None] == hot_index[None, None, :]) & valid[:, None, None]
    named = jnp.sum(hits.astype(jnp.int32), axis=1)
    scales = jnp.sum(jnp.where(hits, gate_block.astype(jnp.float32)[:, :, None], 0.0), axis=1)
    ranks = jnp.cumsum(named, axis=0) - named
    slots = jnp.arange(capacity, dtype=jnp.int32)
    placed = (ranks.T[:, None, :] == slots[None, :, None]) & (named.T[:, None, :] == 1)
    packed = jnp.einsum(
        "hct,td->hcd", placed.astype(jnp.bfloat16), token_block, preferred_element_type=jnp.float32
    ).astype(jnp.bfloat16)
    gate_scale = jnp.einsum("hct,th->hc", placed.astype(jnp.float32), scales).astype(jnp.bfloat16)
    return (packed, gate_scale)


def local(
    prev_acts,
    prev_cot,
    weights,
    first_moment,
    second_moment,
    tokens,
    routing,
    gates,
    token_counts,
    old_owner,
    new_owner,
):
    experts = lax.axis_size("expert")
    groups = experts // GRP
    token_slots = tokens.shape[2]
    capacity = min(token_slots, 3 * token_slots // groups)
    width = weights.shape[2]
    hidden_units = width // 2
    activations = prev_acts[0, 0]
    cotangent = prev_cot[0, 0]
    hot_index = jnp.arange(groups, dtype=jnp.int32)
    holder = jnp.sum(
        jnp.where(new_owner[None, :] == hot_index[:, None], hot_index[None, :], 0), axis=1
    )
    owners = jnp.arange(experts, dtype=jnp.int32)
    source = jnp.take(old_owner, jnp.take(holder, owners // GRP)) * GRP + owners % GRP
    columns = activations
    grads = lax.psum_scatter(
        lax.dot_general(
            columns, cotangent, (((0,), (0,)), ((), ())), preferred_element_type=jnp.float32
        ).astype(jnp.bfloat16),
        "dp",
        scatter_dimension=0,
        tiled=True,
    ).astype(jnp.float32)
    stepped, moment_stack = adamw(weights[0], first_moment[0], second_moment[0], grads)
    new_weight, moments = migrate(stepped, moment_stack, source, experts)
    packed, gate_scale = pack_tokens(
        tokens[0, 0], routing[0, 0], gates[0, 0], token_counts[0, 0], groups, capacity
    )
    to_group = jnp.take(packed, holder, axis=0)
    scale_group = jnp.take(gate_scale, holder, axis=0)
    scale_send = jnp.repeat(scale_group, GRP, axis=0)
    full_send = jnp.repeat(to_group, GRP, axis=0)
    received, scale_in = (
        lax.all_to_all(full_send, "expert", split_axis=0, concat_axis=0, tiled=True),
        lax.all_to_all(scale_send, "expert", split_axis=0, concat_axis=0, tiled=True),
    )
    token_rows = received.reshape(experts * capacity, D)
    columns = token_rows
    projected = jnp.dot(
        columns,
        lax.all_gather(new_weight, "dp", axis=0, tiled=True),
        preferred_element_type=jnp.float32,
    )
    scaling = scale_in.reshape(experts * capacity).astype(jnp.float32)
    result = (
        jax.nn.silu(projected[:, :hidden_units]) * projected[:, hidden_units:] * scaling[:, None]
    )
    hidden = result.astype(jnp.bfloat16).reshape(1, 1, experts * capacity, hidden_units)
    return (hidden, new_weight[None], moments[0][None], moments[1][None])


def solution(mesh):
    in_specs = (
        P("dp", "expert", None, None),
        P("dp", "expert", None, None),
        P("expert", "dp", None),
        P("expert", "dp", None),
        P("expert", "dp", None),
        P("dp", "expert", None, None),
        P("dp", "expert", None, None),
        P("dp", "expert", None, None),
        P("dp", "expert"),
        P(),
        P(),
    )
    out_specs = (
        P("dp", "expert", None, None),
        P("expert", "dp", None),
        P("expert", "dp", None),
        P("expert", "dp", None),
    )
    return jax.shard_map(local, mesh=mesh, in_specs=in_specs, out_specs=out_specs, check_vma=False)
```

profile of v0, /device:TPU:4, one launch (start us, length us, event | category | flops | bytes accessed | tf_op | source)
XLA Modules:
  0.0 608.9 jit_solution(13180646358381109086)
XLA Ops:
  8.4 3.8 convolution_convert_fusion
  13.4 45.2 %reduce-scatter.2.cloned.1.call-done = bf16[896,512]{1,0:T(8,128)(2,1)} async-done(((bf16[3584,512]{1,0:T(8,128)(2,1)}), bf16[896,512]{1,0:T(8,128)(2,1)}) %reduce-scatter.2.cloned.1.call-update) | async-done | bytes 917520 | tf_op jit(solution)/shard_map/reduce_scatter | solution.py:88
  58.7 5.4 fusion.2
  64.1 1.2 reshape.97
  65.3 13.1 %all-to-all-start.1 = ((bf16[64,14,512]{2,1,0:T(8,128)(2,1)}), bf16[64,14,512]{2,1,0:T(8,128)(2,1)S(1)}, u32[]{:S(2)}, u32[]{:S(2)}) async-start(bf16[64,14,512]{2,1,0:T(8,128)(2,1)} %reshape.97), calls=%async_computation.2 | async-start | bytes 2097152 | tf_op jit(solution)/shard_map/all_to_all | solution.py:35
  81.7 24.9 %all-to-all-done.1 = bf16[64,14,512]{2,1,0:T(8,128)(2,1)S(1)} async-done(((bf16[64,14,512]{2,1,0:T(8,128)(2,1)}), bf16[64,14,512]{2,1,0:T(8,128)(2,1)S(1)}, u32[]{:S(2)}, u32[]{:S(2)}) %all-to-all-start.1) | async-done | bytes 917536 | tf_op jit(solution)/shard_map/all_to_all | solution.py:35
  106.6 8.3 %all-to-all-start.3 = ((bf16[64,1,24]{2,1,0:T(2,128)(2,1)}), bf16[64,1,24]{2,1,0:T(2,128)(2,1)S(1)}, u32[]{:S(2)}, u32[]{:S(2)}) async-start(bf16[64,1,24]{2,1,0:T(2,128)(2,1)} %copy.43), calls=%async_computation.4 | async-start | bytes 65536 | tf_op jit(solution)/shard_map/all_to_all | solution.py:107
  116.7 7.7 %all-to-all-done.3 = bf16[64,1,24]{2,1,0:T(2,128)(2,1)S(1)} async-done(((bf16[64,1,24]{2,1,0:T(2,128)(2,1)}), bf16[64,1,24]{2,1,0:T(2,128)(2,1)S(1)}, u32[]{:S(2)}, u32[]{:S(2)}) %all-to-all-start.3) | async-done | bytes 3104 | tf_op jit(solution)/shard_map/all_to_all | solution.py:107
  124.4 7.0 %all-to-all-start.2 = ((bf16[64,14,512]{2,1,0:T(8,128)(2,1)}), bf16[64,14,512]{2,1,0:T(8,128)(2,1)S(1)}, u32[]{:S(2)}, u32[]{:S(2)}) async-start(bf16[64,14,512]{2,1,0:T(8,128)(2,1)} %broadcast_select_fusion.1), calls=%async_computation.3 | async-start | bytes 2097152 | tf_op jit(solution)/shard_map/all_to_all | solution.py:39
  131.4 2.7 stack.10
  134.1 2.7 stack.9
  136.8 2.7 pad_maximum_fusion
  139.5 5.2 copy.44
  144.7 13.0 %all-to-all-done.2 = bf16[64,14,512]{2,1,0:T(8,128)(2,1)S(1)} async-done(((bf16[64,14,512]{2,1,0:T(8,128)(2,1)}), bf16[64,14,512]{2,1,0:T(8,128)(2,1)S(1)}, u32[]{:S(2)}, u32[]{:S(2)}) %all-to-all-start.2) | async-done | bytes 917536 | tf_op jit(solution)/shard_map/all_to_all | solution.py:39
  157.7 8.7 %all-to-all-start.4 = ((f32[2,64,14,512]{3,0,2,1:T(2,128)}), f32[2,64,14,512]{3,0,2,1:T(2,128)}, u32[]{:S(2)}, u32[]{:S(2)}) async-start(f32[2,64,14,512]{3,0,2,1:T(2,128)} %copy.44), calls=%async_computation.5 | async-start | bytes 7340032 | tf_op jit(solution)/shard_map/all_to_all | solution.py:36
  166.4 2.4 convolution_convert_fusion.1
  168.8 4.1 gather_fusion
  172.8 3.7 broadcast_select_fusion
  176.5 71.3 %all-to-all-done.4 = f32[2,64,14,512]{3,0,2,1:T(2,128)} async-done(((f32[2,64,14,512]{3,0,2,1:T(2,128)}), f32[2,64,14,512]{3,0,2,1:T(2,128)}, u32[]{:S(2)}, u32[]{:S(2)}) %all-to-all-start.4) | async-done | bytes 3670048 | tf_op jit(solution)/shard_map/all_to_all | solution.py:36
  247.8 6.6 %broadcast_in_dim.92 = bf16[16,4,24,3584]{3,2,1,0:T(8,128)(2,1)} broadcast(bf16[16,24,3584]{2,1,0:T(8,128)(2,1)} %broadcast_select_fusion), dimensions={0,2,3} | broadcast | bytes 13762560 | tf_op jit(solution)/shard_map/broadcast_in_dim | solution.py:104
  254.4 9.1 %all-to-all-start = ((bf16[64,24,3584]{2,1,0:T(8,128)(2,1)}), bf16[64,24,3584]{2,1,0:T(8,128)(2,1)}, u32[]{:S(2)}, u32[]{:S(2)}) async-start(bf16[64,24,3584]{2,1,0:T(8,128)(2,1)} %bitcast.52), calls=%async_computation | async-start | bytes 22020096 | tf_op jit(solution)/shard_map/all_to_all | solution.py:106
  263.6 1.2 reshape.98
  264.8 8.1 %gather_fusion.3 = f32[64,2,14,512]{3,1,2,0:T(2,128)} fusion(f32[2,64,14,512]{3,0,2,1:T(2,128)} %all-to-all-done.4, s32[1024]{0:T(1024)S(1)} %pad_clamp_fusion), kind=kCustom, calls=%fused_computation.5 | custom fusion | bytes 7340288 | tf_op jit(solution)/shard_map/jit(_take)/gather | solution.py:38
  272.9 5.8 select_bitcast_fusion
  278.7 224.7 %all-to-all-done = bf16[64,24,3584]{2,1,0:T(8,128)(2,1)} async-done(((bf16[64,24,3584]{2,1,0:T(8,128)(2,1)}), bf16[64,24,3584]{2,1,0:T(8,128)(2,1)}, u32[]{:S(2)}, u32[]{:S(2)}) %all-to-all-start) | async-done | bytes 11010080 | tf_op jit(solution)/shard_map/all_to_all | solution.py:106
  503.4 9.0 %all-to-all-start.5 = ((f32[2,64,14,512]{3,0,2,1:T(2,128)}), f32[2,64,14,512]{3,0,2,1:T(2,128)}, u32[]{:S(2)}, u32[]{:S(2)}) async-start(f32[2,64,14,512]{3,0,2,1:T(2,128)} %select_bitcast_fusion), calls=%async_computation.6 | async-start | bytes 7340032 | tf_op jit(solution)/shard_map/all_to_all | solution.py:40
  513.8 9.7 %fusion.23 = f32[1536,512]{1,0:T(8,128)S(1)} fusion(bf16[1536,3584]{1,0:T(8,128)(2,1)} %bitcast.9, bf16[3584,512]{1,0:T(8,128)(2,1)} %all-gather.2.cloned.1.call-done), kind=kOutput, calls=%fused_computation.65 | convolution fusion | flops 5637144576 | bytes 17825792 | tf_op jit(solution)/shard_map/dot_general | solution.py:111
  523.5 1.3 fusion.7
  524.8 68.0 %all-to-all-done.5 = f32[2,64,14,512]{3,0,2,1:T(2,128)} async-done(((f32[2,64,14,512]{3,0,2,1:T(2,128)}), f32[2,64,14,512]{3,0,2,1:T(2,128)}, u32[]{:S(2)}, u32[]{:S(2)}) %all-to-all-start.5) | async-done | bytes 3670048 | tf_op jit(solution)/shard_map/all_to_all | solution.py:40
  592.8 6.4 %fusion.22 = (f32[1,64,14,512]{3,0,2,1:T(1,128)S(1)}, f32[1,64,14,512]{3,0,2,1:T(1,128)S(1)}) fusion(f32[2,64,14,512]{3,0,2,1:T(2,128)} %all-to-all-done.5), kind=kLoop, calls=%fused_computation.64 | loop fusion | bytes 7340032 | tf_op jit(solution)/shard_map/slice | solution.py:121
  599.2 1.4 copy.45
  600.6 1.4 copy.46
  (53 shorter events, 8.1 us)
Async XLA Ops:
  7.2 1.2 copy-start
  7.2 51.5 %reduce-scatter.2.cloned.1.call-start = ((), (), s32[]{:S(2)}) async-start(), calls=%async_computation.7 | async-start | bytes 4587520 | tf_op jit(solution)/shard_map/reduce_scatter | solution.py:88
  12.2 0.8 copy-start.5
  12.2 1.2 copy-start.6
  12.2 46.5 %copy-start.3 = (f32[1,896,512]{2,1,0:T(8,128)S(1)}, f32[1,896,512]{2,1,0:T(8,128)}, u32[]{:S(2)}) copy-start(f32[1,896,512]{2,1,0:T(8,128)} %param.16) | copy-start | bytes 5505028
  64.1 14.5 %copy-start.7 = (s32[16]{0:T(128)S(1)}, s32[16]{0:T(128)}, u32[]{:S(2)}) copy-start(s32[16]{0:T(128)} %param.23) | copy-start | bytes 196
  65.3 15.6 %copy-start.2 = (s32[16]{0:T(128)S(1)}, s32[16]{0:T(128)}, u32[]{:S(2)}) copy-start(s32[16]{0:T(128)} %param.22) | copy-start | bytes 196
  65.3 41.3 %all-to-all-start.1 = ((bf16[64,14,512]{2,1,0:T(8,128)(2,1)}), bf16[64,14,512]{2,1,0:T(8,128)(2,1)S(1)}, u32[]{:S(2)}, u32[]{:S(2)}) async-start(bf16[64,14,512]{2,1,0:T(8,128)(2,1)} %reshape.97), calls=%async_computation.2 | async-start | bytes 2097152 | tf_op jit(solution)/shard_map/all_to_all | solution.py:35
  106.6 17.8 %all-to-all-start.3 = ((bf16[64,1,24]{2,1,0:T(2,128)(2,1)}), bf16[64,1,24]{2,1,0:T(2,128)(2,1)S(1)}, u32[]{:S(2)}, u32[]{:S(2)}) async-start(bf16[64,1,24]{2,1,0:T(2,128)(2,1)} %copy.43), calls=%async_computation.4 | async-start | bytes 65536 | tf_op jit(solution)/shard_map/all_to_all | solution.py:107
  124.4 33.3 %all-to-all-start.2 = ((bf16[64,14,512]{2,1,0:T(8,128)(2,1)}), bf16[64,14,512]{2,1,0:T(8,128)(2,1)S(1)}, u32[]{:S(2)}, u32[]{:S(2)}) async-start(bf16[64,14,512]{2,1,0:T(8,128)(2,1)} %broadcast_select_fusion.1), calls=%async_computation.3 | async-start | bytes 2097152 | tf_op jit(solution)/shard_map/all_to_all | solution.py:39
  144.7 21.7 %copy-start.4 = (bf16[1,1,128,3584]{3,2,1,0:T(8,128)(2,1)S(1)}, bf16[1,1,128,3584]{3,2,1,0:T(8,128)(2,1)}, u32[]{:S(2)}) copy-start(bf16[1,1,128,3584]{3,2,1,0:T(8,128)(2,1)} %param.18) | copy-start | bytes 2752516
  157.7 90.2 %all-to-all-start.4 = ((f32[2,64,14,512]{3,0,2,1:T(2,128)}), f32[2,64,14,512]{3,0,2,1:T(2,128)}, u32[]{:S(2)}, u32[]{:S(2)}) async-start(f32[2,64,14,512]{3,0,2,1:T(2,128)} %copy.44), calls=%async_computation.5 | async-start | bytes 7340032 | tf_op jit(solution)/shard_map/all_to_all | solution.py:36
  254.4 249.0 %all-to-all-start = ((bf16[64,24,3584]{2,1,0:T(8,128)(2,1)}), bf16[64,24,3584]{2,1,0:T(8,128)(2,1)}, u32[]{:S(2)}, u32[]{:S(2)}) async-start(bf16[64,24,3584]{2,1,0:T(8,128)(2,1)} %bitcast.52), calls=%async_computation | async-start | bytes 22020096 | tf_op jit(solution)/shard_map/all_to_all | solution.py:106
  263.6 250.2 %all-gather.2.cloned.1.call-start = ((), (), s32[]{:S(2)}) async-start(), calls=%async_computation.8 | async-start | bytes 4587520 | tf_op jit(solution)/shard_map/all_gather | solution.py:113
  503.4 89.4 %all-to-all-start.5 = ((f32[2,64,14,512]{3,0,2,1:T(2,128)}), f32[2,64,14,512]{3,0,2,1:T(2,128)}, u32[]{:S(2)}, u32[]{:S(2)}) async-start(f32[2,64,14,512]{3,0,2,1:T(2,128)} %select_bitcast_fusion), calls=%async_computation.6 | async-start | bytes 7340032 | tf_op jit(solution)/shard_map/all_to_all | solution.py:40
  600.6 1.5 copy-start.1
Sparse Core Ops, SparseCore 0:
  12.3 46.2 reduce-scatter.1
  266.8 83.2 all-gather.1
where the time goes:
time: 611 us; the launch traced here: 609 us
  waiting for transfers between devices  455 us (74%)
  starting transfers between devices  55.4 us (9%)
  local copies, waits for them, and re-layouts  46.9 us (8%)
  other arithmetic  20.7 us (3%)
  matrix products  16.1 us (3%)
  between operations  15 us (2%)
    all_to_all x1, waiting for transfers between devices, local(): lax.all_to_all(full_send, 'expert', split_axis=0, concat_axis=0, tiled=True)  225 us
    all_to_all x1, waiting for transfers between devices, migrate(): lax.all_to_all(moment_split, 'expert', split_axis=1, concat_axis=1, tiled...  71.3 us
    all_to_all x1, waiting for transfers between devices, migrate(): lax.all_to_all(moment_sorted, 'expert', split_axis=1, concat_axis=1, tile...  68 us
    reduce_scatter x1, waiting for transfers between devices, local(): lax.psum_scatter(lax.dot_general(columns, cotangent, (((0,), (0,)), ((),...  45.2 us
    all_to_all x1, waiting for transfers between devices, migrate(): lax.all_to_all(weight_split, 'expert', split_axis=0, concat_axis=0, tiled...  24.9 us
    all_to_all x1, starting transfers between devices, migrate(): lax.all_to_all(weight_split, 'expert', split_axis=0, concat_axis=0, tiled...  13.1 us
    all_to_all x1, waiting for transfers between devices, migrate(): lax.all_to_all(weight_sorted, 'expert', split_axis=0, concat_axis=0, tile...  13 us
  transfers between devices with their start and end apart: 8, of which 7 were waited for; matrix products, arithmetic and copies ran while one was open for 9% of the time, Pallas kernels for 0%

commit v1 on v0

v1 whole, which is shorter than its diff:
```python
import jax
import jax.numpy as jnp
from jax import lax
from jax.sharding import Mesh
from jax.sharding import PartitionSpec as P

D = 3584
GRP = 4
SCALE_PAD = 128


beta_first = 0.9
beta_second = 0.95
learning = 0.00022
decay_rate = 0.1
epsilon = 1e-08
first_fix = 1.0 - 0.9**40
second_fix = 1.0 - 0.95**40


def adamw(weight_now, first_now, second_now, gradient):
    first_next = beta_first * first_now + (1.0 - beta_first) * gradient
    second_next = beta_second * second_now + (1.0 - beta_second) * gradient * gradient
    stepped = weight_now.astype(jnp.float32) * (1.0 - learning * decay_rate) - learning * (
        first_next / first_fix
    ) / (jnp.sqrt(second_next / second_fix) + epsilon)
    return stepped.astype(jnp.bfloat16), first_next, second_next


def migrate(state, group_source, groups):
    layers, rows_dev, width = state.shape
    piece_rows = rows_dev // groups
    split = state.reshape(layers, groups, piece_rows, width)
    spread = lax.all_to_all(split, "grp", split_axis=1, concat_axis=1, tiled=True)
    chosen = jnp.take(spread, group_source, axis=1)
    home = lax.all_to_all(chosen, "grp", split_axis=1, concat_axis=1, tiled=True)
    return home.reshape(layers, rows_dev, width)


def pack_tokens(token_block, route_block, gate_block, limit, hot_count, capacity):
    hot_index = jnp.arange(hot_count, dtype=jnp.int32)
    valid = jnp.arange(token_block.shape[0], dtype=jnp.int32) < limit
    hits = (route_block[:, :, None] == hot_index[None, None, :]) & valid[:, None, None]
    named = jnp.sum(hits.astype(jnp.int32), axis=1)
    scales = jnp.sum(jnp.where(hits, gate_block.astype(jnp.float32)[:, :, None], 0.0), axis=1)
    ranks = jnp.cumsum(named, axis=0) - named
    slots = jnp.arange(capacity, dtype=jnp.int32)
    placed = (ranks.T[:, None, :] == slots[None, :, None]) & (named.T[:, None, :] == 1)
    packed = jnp.einsum(
        "hct,td->hcd", placed.astype(jnp.bfloat16), token_block, preferred_element_type=jnp.float32
    ).astype(jnp.bfloat16)
    gate_scale = jnp.einsum("hct,th->hc", placed.astype(jnp.float32), scales).astype(jnp.bfloat16)
    return (packed, gate_scale)


def local(
    prev_acts,
    prev_cot,
    weights,
    first_moment,
    second_moment,
    tokens,
    routing,
    gates,
    token_counts,
    old_owner,
    new_owner,
):
    groups = lax.axis_size("grp")
    per_group = lax.axis_size("pos")
    experts = groups * per_group
    token_slots = tokens.shape[2]
    capacity = min(token_slots, 3 * token_slots // groups)
    width = weights.shape[2]
    hidden_units = width // 2
    activations = prev_acts[0, 0]
    cotangent = prev_cot[0, 0]
    hot_index = jnp.arange(groups, dtype=jnp.int32)
    holder = jnp.sum(
        jnp.where(new_owner[None, :] == hot_index[:, None], hot_index[None, :], 0), axis=1
    )
    group_source = jnp.take(old_owner, holder)

    packed, gate_scale = pack_tokens(
        tokens[0, 0], routing[0, 0], gates[0, 0], token_counts[0, 0], groups, capacity
    )
    scale_cols = jnp.zeros((groups, capacity, SCALE_PAD), jnp.bfloat16).at[:, :, 0].set(gate_scale)
    payload = jnp.concatenate([packed, scale_cols], axis=2)
    to_group = jnp.take(payload, holder, axis=0)
    by_group = lax.all_to_all(to_group, "grp", split_axis=0, concat_axis=0, tiled=True)
    received = lax.all_gather(by_group, "pos", axis=0, tiled=False)

    grads = lax.psum_scatter(
        lax.dot_general(
            activations, cotangent, (((0,), (0,)), ((), ())), preferred_element_type=jnp.float32
        ).astype(jnp.bfloat16),
        "dp",
        scatter_dimension=0,
        tiled=True,
    ).astype(jnp.float32)
    stepped, first_next, second_next = adamw(weights[0], first_moment[0], second_moment[0], grads)
    state = jnp.stack(
        [stepped, first_next.astype(jnp.bfloat16), second_next.astype(jnp.bfloat16)]
    )
    moved = migrate(state, group_source, groups)
    new_weight = moved[0]

    token_rows = received[:, :, :, :D].reshape(experts * capacity, D)
    scaling = received[:, :, :, D].reshape(experts * capacity).astype(jnp.float32)
    projected = jnp.dot(
        token_rows,
        lax.all_gather(new_weight, "dp", axis=0, tiled=True),
        preferred_element_type=jnp.float32,
    )
    result = (
        jax.nn.silu(projected[:, :hidden_units]) * projected[:, hidden_units:] * scaling[:, None]
    )
    hidden = result.astype(jnp.bfloat16).reshape(per_group, groups, capacity, hidden_units)
    hidden = jnp.transpose(hidden, (1, 0, 2, 3)).reshape(1, 1, experts * capacity, hidden_units)
    return (
        hidden,
        new_weight[None],
        moved[1].astype(jnp.float32)[None],
        moved[2].astype(jnp.float32)[None],
    )


def solution(mesh):
    n_dp = mesh.shape["dp"]
    n_expert = mesh.shape["expert"]
    mesh3 = Mesh(
        mesh.devices.reshape(n_dp, n_expert // GRP, GRP), ("dp", "grp", "pos")
    )
    ex = ("grp", "pos")
    in_specs = (
        P("dp", ex, None, None),
        P("dp", ex, None, None),
        P(ex, "dp", None),
        P(ex, "dp", None),
        P(ex, "dp", None),
        P("dp", ex, None, None),
        P("dp", ex, None, None),
        P("dp", ex, None, None),
        P("dp", ex),
        P(),
        P(),
    )
    out_specs = (
        P("dp", ex, None, None),
        P(ex, "dp", None),
        P(ex, "dp", None),
        P(ex, "dp", None),
    )
    return jax.shard_map(local, mesh=mesh3, in_specs=in_specs, out_specs=out_specs, check_vma=False)
```

time: 611 us -> 399 us (0.65)
  waiting for transfers between devices: 455 us -> 165 us
  blocking collectives: 0 us -> 156 us
  starting transfers between devices: 55.4 us -> 4.64 us
  local copies, waits for them, and re-layouts: 46.9 us -> 25.2 us
    all_to_all x6 -> x1, waiting for transfers between devices: 410 us -> 73.3 us  [migrate(): lax.all_to_all(split, 'grp', split_axis=1, concat_axis=1, tiled=True)]
    all_to_all x0 -> x2, blocking collectives: none -> 156 us  [the longest x1 80.3 us: local(): lax.all_to_all(to_group, 'grp', split_axis=0, concat_axis=0, tiled=True)]
    all_to_all x6 -> x1, starting transfers between devices: 55.3 us -> 4.52 us  [migrate(): lax.all_to_all(split, 'grp', split_axis=1, concat_axis=1, tiled=True)]
    all_gather x0 -> x1, waiting for transfers between devices: none -> 47.7 us  [local(): received = lax.all_gather(by_group, 'pos', axis=0, tiled=False)]
    reduce_scatter x1, waiting for transfers between devices: 45.2 us -> 0.02 us  [local(): lax.psum_scatter(lax.dot_general(activations, cotangent, (((0,), (0,)), (...]
    all_gather x1, waiting for transfers between devices: 0.01 us -> 43.7 us  [local(): lax.all_gather(new_weight, 'dp', axis=0, tiled=True)]
    another operation x4 -> x1, local copies, waits for them, and re-layouts: 11.7 us -> 0.2 us  [the longest x3 10.5 us: adamw(): return (stepped.astype(jnp.bfloat16), jnp.stack([first_next, second_next]))]
    broadcast_in_dim x2 -> x0, local copies, waits for them, and re-layouts: 6.62 us -> none  [the longest x1 6.61 us: local(): full_send = jnp.repeat(to_group, GRP, axis=0)]
  transfers between devices with their start and end apart: 8 -> 4, of which waited for: 7 -> 3; matrix products, arithmetic and copies ran while one was open for 9% -> 9% of each run, Pallas kernels for 0% -> 0%
where the time goes in v1:
time: 399 us; the launch traced here: 397 us
  waiting for transfers between devices  165 us (41%)
  blocking collectives  156 us (39%)
  local copies, waits for them, and re-layouts  25.2 us (6%)
  between operations  16.4 us (4%)
  other arithmetic  15.3 us (4%)
  matrix products  14.7 us (4%)
  starting transfers between devices  4.64 us (1%)
    all_to_all x1, blocking collectives, local(): lax.all_to_all(to_group, 'grp', split_axis=0, concat_axis=0, tiled=True)  80.3 us
    all_to_all x1, blocking collectives, migrate(): lax.all_to_all(chosen, 'grp', split_axis=1, concat_axis=1, tiled=True)  75.3 us
    all_to_all x1, waiting for transfers between devices, migrate(): lax.all_to_all(split, 'grp', split_axis=1, concat_axis=1, tiled=True)  73.3 us
    all_gather x1, waiting for transfers between devices, local(): received = lax.all_gather(by_group, 'pos', axis=0, tiled=False)  47.7 us
    all_gather x1, waiting for transfers between devices, local(): lax.all_gather(new_weight, 'dp', axis=0, tiled=True)  43.7 us
    dot_general x1, matrix products, local(): jnp.dot(token_rows, lax.all_gather(new_weight, 'dp', axis=0, tiled=True),...  9.75 us
    slice x1, local copies, waits for them, and re-layouts, local(): token_rows = received[:, :, :, :D].reshape(experts * capacity, D)  9.58 us
  transfers between devices with their start and end apart: 4, of which 3 were waited for; matrix products, arithmetic and copies ran while one was open for 9% of the time, Pallas kernels for 0%

profile of v1, /device:TPU:4, one launch (start us, length us, event | category | flops | bytes accessed | tf_op | source)
XLA Modules:
  0.0 396.7 jit_solution(7379256620943259028)
XLA Ops:
  8.1 1.1 copy-done
  9.2 3.9 convolution_convert_fusion
  14.1 0.1 select_reduce_fusion.1
  14.3 0.2 reduce_window_sum.11
  14.5 0.2 fusion.12
  14.7 0.2 copy.40
  14.9 0.7 gather_fusion.1
  15.6 0.9 convolution_convert_fusion.1
  16.5 1.8 fusion.1
  18.2 4.3 %gather_fusion = bf16[16,24,3712]{2,1,0:T(8,128)(2,1)} fusion(bf16[16,24,3712]{2,1,0:T(8,128)(2,1)} %fusion.1, s32[1024]{0:T(1024)S(1)} %pad_clamp_fusion.1), kind=kCustom, calls=%fused_computation | custom fusion | bytes 5701696 | tf_op jit(solution)/shard_map/jit(_take)/gather | solution.py:89
  22.5 2.2 broadcast_select_fusion
  24.7 80.3 %all_to_all.15 = bf16[16,24,3712]{2,1,0:T(8,128)(2,1)} all-to-all(bf16[16,24,3712]{2,1,0:T(8,128)(2,1)S(1)} %broadcast_select_fusion), channel_id=1, replica_groups=mesh['dp'=4,'grp'=16,'pos'=4] {'grp'}, dimensions={0} | all-to-all | bytes 5701632 | tf_op jit(solution)/shard_map/all_to_all | solution.py:90
  105.0 1.4 copy-done.3
  106.5 3.7 fusion.4
  110.2 1.8 pad_maximum_fusion
  111.9 4.5 %all-to-all-start.1 = ((bf16[3,16,56,512]{3,2,0,1:T(8,128)(2,1)}), bf16[3,16,56,512]{3,2,0,1:T(8,128)(2,1)}, u32[]{:S(2)}, u32[]{:S(2)}) async-start(bf16[3,16,56,512]{3,2,0,1:T(8,128)(2,1)} %pad_maximum_fusion), calls=%async_computation.2 | async-start | bytes 5505024 | tf_op jit(solution)/shard_map/all_to_all | solution.py:34
  116.6 73.3 %all-to-all-done.1 = bf16[3,16,56,512]{3,2,0,1:T(8,128)(2,1)} async-done(((bf16[3,16,56,512]{3,2,0,1:T(8,128)(2,1)}), bf16[3,16,56,512]{3,2,0,1:T(8,128)(2,1)}, u32[]{:S(2)}, u32[]{:S(2)}) %all-to-all-start.1) | async-done | bytes 2752544 | tf_op jit(solution)/shard_map/all_to_all | solution.py:34
  189.8 4.0 %gather_fusion.2 = bf16[16,3,56,512]{3,2,1,0:T(8,128)(2,1)} fusion(bf16[3,16,56,512]{3,2,0,1:T(8,128)(2,1)} %all-to-all-done.1, s32[1024]{0:T(1024)S(1)} %pad_clamp_fusion), kind=kCustom, calls=%fused_computation.2 | custom fusion | bytes 5505088 | tf_op jit(solution)/shard_map/jit(_take)/gather | solution.py:35
  193.8 2.1 select_bitcast_fusion
  196.0 75.3 %all_to_all.16 = bf16[3,16,56,512]{3,2,0,1:T(8,128)(2,1)S(1)} all-to-all(bf16[3,16,56,512]{3,2,0,1:T(8,128)(2,1)S(1)} %select_bitcast_fusion), channel_id=1, replica_groups=mesh['dp'=4,'grp'=16,'pos'=4] {'grp'}, dimensions={1} | all-to-all | bytes 5505024 | tf_op jit(solution)/shard_map/all_to_all | solution.py:36
  271.3 1.1 fusion.23
  272.5 1.5 convert.5
  274.0 1.5 convert.6
  275.4 47.7 %all-gather.6.cloned.1.call-done = bf16[64,24,3712]{2,1,0:T(8,128)(2,1)} async-done(((bf16[16,24,3712]{2,1,0:T(8,128)(2,1)}), bf16[64,24,3712]{2,1,0:T(8,128)(2,1)}) %all-gather.6.cloned.1.call-update) | async-done | bytes 11403280 | tf_op jit(solution)/shard_map/all_gather | solution.py:91
  323.2 1.0 slice.63
  324.2 9.6 %slice.59 = bf16[4,16,24,3584]{3,2,1,0:T(8,128)(2,1)} slice(bf16[4,16,24,3712]{3,2,1,0:T(8,128)(2,1)} %bitcast.89), slice={[0:4], [0:16], [0:24], [0:3584]} | slice | bytes 22020096 | tf_op jit(solution)/shard_map/slice | solution.py:108
  333.8 0.5 copy.48
  334.2 0.1 reshape.177
  334.3 43.7 %all-gather.4.cloned.1.call-done = bf16[3584,512]{1,0:T(8,128)(2,1)} async-done(((bf16[896,512]{1,0:T(8,128)(2,1)}), bf16[3584,512]{1,0:T(8,128)(2,1)}) %all-gather.4.cloned.1.call-update) | async-done | bytes 3670032 | tf_op jit(solution)/shard_map/all_gather | solution.py:112
  378.1 9.7 %fusion.24 = f32[1536,512]{1,0:T(8,128)S(1)} fusion(bf16[1536,3584]{1,0:T(8,128)(2,1)} %bitcast.90, bf16[3584,512]{1,0:T(8,128)(2,1)} %all-gather.4.cloned.1.call-done), kind=kOutput, calls=%fused_computation.55 | convolution fusion | flops 5637144576 | bytes 17825792 | tf_op jit(solution)/shard_map/dot_general | solution.py:110
  387.8 0.4 fusion.6
  388.3 1.0 copy.45
  (35 shorter events, 0.5 us)
Async XLA Ops:
  8.0 1.2 copy-start
  8.0 97.0 %reduce-scatter.2.cloned.1.call-start = ((), (), s32[]{:S(2)}) async-start(), calls=%async_computation.4 | async-start | bytes 4587520 | tf_op jit(solution)/shard_map/reduce_scatter | solution.py:93
  13.1 0.9 copy-start.5
  13.1 1.0 copy-start.6
  13.1 1.1 copy-start.7
  13.1 1.8 copy-start.2
  13.1 2.5 copy-start.4
  13.2 310.0 %all-gather.6.cloned.1.call-start = ((), (), s32[]{:S(2)}) async-start(), calls=%async_computation.6 | async-start | bytes 14254080 | tf_op jit(solution)/shard_map/all_gather | solution.py:91
  105.0 1.5 copy-start.3
  111.9 77.9 %all-to-all-start.1 = ((bf16[3,16,56,512]{3,2,0,1:T(8,128)(2,1)}), bf16[3,16,56,512]{3,2,0,1:T(8,128)(2,1)}, u32[]{:S(2)}, u32[]{:S(2)}) async-start(bf16[3,16,56,512]{3,2,0,1:T(8,128)(2,1)} %pad_maximum_fusion), calls=%async_computation.2 | async-start | bytes 5505024 | tf_op jit(solution)/shard_map/all_to_all | solution.py:34
  116.5 261.6 %all-gather.4.cloned.1.call-start = ((), (), s32[]{:S(2)}) async-start(), calls=%async_computation.5 | async-start | bytes 4587520 | tf_op jit(solution)/shard_map/all_gather | solution.py:112
  378.1 11.2 %copy-start.1 = (bf16[1,1,128,3584]{3,2,1,0:T(8,128)(2,1)S(1)}, bf16[1,1,128,3584]{3,2,1,0:T(8,128)(2,1)}, u32[]{:S(2)}) copy-start(bf16[1,1,128,3584]{3,2,1,0:T(8,128)(2,1)} %param.13) | copy-start | bytes 2752516
Sparse Core Ops, SparseCore 0:
  13.3 46.2 reduce-scatter.1
Sparse Core Ops, SparseCore 1:
  105.1 218.0 all-gather.5
  325.4 52.6 all-gather.3

commit v2 on v1

--- a/solution.py
+++ b/solution.py
@@ -67,8 +67,7 @@
     new_owner,
 ):
     groups = lax.axis_size("grp")
-    per_group = lax.axis_size("pos")
-    experts = groups * per_group
+    experts = groups * GRP
     token_slots = tokens.shape[2]
     capacity = min(token_slots, 3 * token_slots // groups)
     width = weights.shape[2]
@@ -88,7 +87,8 @@
     payload = jnp.concatenate([packed, scale_cols], axis=2)
     to_group = jnp.take(payload, holder, axis=0)
     by_group = lax.all_to_all(to_group, "grp", split_axis=0, concat_axis=0, tiled=True)
-    received = lax.all_gather(by_group, "pos", axis=0, tiled=False)
+    from_ylo = lax.ppermute(by_group, "ylo", perm=[(0, 1), (1, 0)])
+    near = jnp.stack([by_group, from_ylo]).reshape(2 * groups * capacity, D + SCALE_PAD)
 
     grads = lax.psum_scatter(
         lax.dot_general(
@@ -105,18 +105,24 @@
     moved = migrate(state, group_source, groups)
     new_weight = moved[0]
 
-    token_rows = received[:, :, :, :D].reshape(experts * capacity, D)
-    scaling = received[:, :, :, D].reshape(experts * capacity).astype(jnp.float32)
-    projected = jnp.dot(
-        token_rows,
-        lax.all_gather(new_weight, "dp", axis=0, tiled=True),
-        preferred_element_type=jnp.float32,
-    )
+    partner_weight = lax.ppermute(new_weight, "xhi", perm=[(0, 1), (1, 0)])
+    both = lax.all_gather(jnp.stack([new_weight, partner_weight]), "dp", axis=1, tiled=True)
+    both = jnp.pad(both, ((0, 0), (0, SCALE_PAD), (0, 0)))
+    projected = jnp.einsum("rd,kdn->krn", near, both, preferred_element_type=jnp.float32)
+    scaling = near[:, D].astype(jnp.float32)
     result = (
-        jax.nn.silu(projected[:, :hidden_units]) * projected[:, hidden_units:] * scaling[:, None]
-    )
-    hidden = result.astype(jnp.bfloat16).reshape(per_group, groups, capacity, hidden_units)
-    hidden = jnp.transpose(hidden, (1, 0, 2, 3)).reshape(1, 1, experts * capacity, hidden_units)
+        jax.nn.silu(projected[:, :, :hidden_units])
+        * projected[:, :, hidden_units:]
+        * scaling[None, :, None]
+    ).astype(jnp.bfloat16)
+    for_partner = lax.ppermute(result[1], "xhi", perm=[(0, 1), (1, 0)])
+    mine = jnp.stack([result[0], for_partner]).reshape(2, 2, groups, capacity, hidden_units)
+    ylo = lax.axis_index("ylo")
+    xhi = lax.axis_index("xhi")
+    flip = jnp.arange(2, dtype=jnp.int32)
+    mine = jnp.take(mine, flip ^ xhi, axis=0)
+    mine = jnp.take(mine, flip ^ ylo, axis=1)
+    hidden = jnp.transpose(mine, (2, 1, 0, 3, 4)).reshape(1, 1, experts * capacity, hidden_units)
     return (
         hidden,
         new_weight[None],
@@ -128,10 +134,10 @@
 def solution(mesh):
     n_dp = mesh.shape["dp"]
     n_expert = mesh.shape["expert"]
-    mesh3 = Mesh(
-        mesh.devices.reshape(n_dp, n_expert // GRP, GRP), ("dp", "grp", "pos")
+    mesh4 = Mesh(
+        mesh.devices.reshape(n_dp, n_expert // GRP, 2, 2), ("dp", "grp", "ylo", "xhi")
     )
-    ex = ("grp", "pos")
+    ex = ("grp", "ylo", "xhi")
     in_specs = (
         P("dp", ex, None, None),
         P("dp", ex, None, None),
@@ -151,4 +157,4 @@
         P(ex, "dp", None),
         P(ex, "dp", None),
     )
-    return jax.shard_map(local, mesh=mesh3, in_specs=in_specs, out_specs=out_specs, check_vma=False)
+    return jax.shard_map(local, mesh=mesh4, in_specs=in_specs, out_specs=out_specs, check_vma=False)

time: 399 us -> 419 us (1.050)
  waiting for transfers between devices: 165 us -> 263 us
  blocking collectives: 156 us -> 74 us
  starting transfers between devices: 4.64 us -> 16.1 us
  local copies, waits for them, and re-layouts: 25.2 us -> 18.7 us
    all_gather x2 -> x1, waiting for transfers between devices: 91.5 us -> 0.02 us  [local(): lax.all_gather(jnp.stack([new_weight, partner_weight]), 'dp', axis=1, til...]
    ppermute x0 -> x3, waiting for transfers between devices: none -> 86.1 us  [the longest x1 60.5 us: local(): from_ylo = lax.ppermute(by_group, 'ylo', perm=[(0, 1), (1, 0)])]
    all_to_all x1 -> x0, blocking collectives: 75.3 us -> none  [migrate(): lax.all_to_all(chosen, 'grp', split_axis=1, concat_axis=1, tiled=True)]
    all_to_all x0 -> x1, waiting for transfers between devices: none -> 64.4 us  [migrate(): lax.all_to_all(chosen, 'grp', split_axis=1, concat_axis=1, tiled=True)]
    reduce_scatter x1, waiting for transfers between devices: 0.02 us -> 46.4 us  [local(): lax.psum_scatter(lax.dot_general(activations, cotangent, (((0,), (0,)), (...]
    slice x2 -> x3, local copies, waits for them, and re-layouts: 10.6 us -> 0.83 us  [the longest x1 0.6 us: local(): new_weight = moved[0]]
    all_to_all x1, waiting for transfers between devices: 73.3 us -> 65.7 us  [migrate(): lax.all_to_all(split, 'grp', split_axis=1, concat_axis=1, tiled=True)]
    all_to_all x1, blocking collectives: 80.3 us -> 74 us  [local(): lax.all_to_all(to_group, 'grp', split_axis=0, concat_axis=0, tiled=True)]
  transfers between devices with their start and end apart: 4 -> 7, of which waited for: 3 -> 6; matrix products, arithmetic and copies ran while one was open for 9% -> 3% of each run, Pallas kernels for 0% -> 0%
where the time goes in v2:
time: 419 us
  waiting for transfers between devices  263 us (63%)
  blocking collectives  74 us (18%)
  local copies, waits for them, and re-layouts  18.7 us (4%)
  other arithmetic  17.4 us (4%)
  starting transfers between devices  16.1 us (4%)
  matrix products  15.1 us (4%)
  between operations  15 us (4%)
    all_to_all x1, blocking collectives, local(): lax.all_to_all(to_group, 'grp', split_axis=0, concat_axis=0, tiled=True)  74 us
    all_to_all x1, waiting for transfers between devices, migrate(): lax.all_to_all(split, 'grp', split_axis=1, concat_axis=1, tiled=True)  65.7 us
    all_to_all x1, waiting for transfers between devices, migrate(): lax.all_to_all(chosen, 'grp', split_axis=1, concat_axis=1, tiled=True)  64.4 us
    ppermute x1, waiting for transfers between devices, local(): from_ylo = lax.ppermute(by_group, 'ylo', perm=[(0, 1), (1, 0)])  60.5 us
    reduce_scatter x1, waiting for transfers between devices, local(): lax.psum_scatter(lax.dot_general(activations, cotangent, (((0,), (0,)), (...  46.4 us
    ppermute x1, waiting for transfers between devices, local(): partner_weight = lax.ppermute(new_weight, 'xhi', perm=[(0, 1), (1, 0)])  20.4 us
    dot_general x1, matrix products, local(): jnp.einsum('rd,kdn->krn', near, both, preferred_element_type=jnp.float32)  10.3 us
    all_to_all x1, starting transfers between devices, migrate(): lax.all_to_all(split, 'grp', split_axis=1, concat_axis=1, tiled=True)  9.71 us
  transfers between devices with their start and end apart: 7, of which 6 were waited for; matrix products, arithmetic and copies ran while one was open for 3% of the time, Pallas kernels for 0%

profile of v2, /device:TPU:4, one launch (start us, length us, event | category | flops | bytes accessed | tf_op | source)
XLA Modules:
  0.0 418.9 jit_solution(3127450031065847990)
XLA Ops:
  7.2 1.1 copy-done
  8.4 3.8 convolution_convert_fusion
  12.2 46.4 %reduce-scatter.2.cloned.1.call-done = bf16[896,512]{1,0:T(8,128)(2,1)} async-done(((bf16[3584,512]{1,0:T(8,128)(2,1)}), bf16[896,512]{1,0:T(8,128)(2,1)}) %reduce-scatter.2.cloned.1.call-update) | async-done | bytes 917520 | tf_op jit(solution)/shard_map/reduce_scatter | solution.py:93
  58.6 3.4 fusion.9
  62.0 1.8 pad_maximum_fusion.1
  63.8 9.7 %all-to-all-start = ((bf16[3,16,56,512]{3,2,0,1:T(8,128)(2,1)}), bf16[3,16,56,512]{3,2,0,1:T(8,128)(2,1)S(1)}, u32[]{:S(2)}, u32[]{:S(2)}) async-start(bf16[3,16,56,512]{3,2,0,1:T(8,128)(2,1)} %pad_maximum_fusion.1), calls=%async_computation.1 | async-start | bytes 5505024 | tf_op jit(solution)/shard_map/all_to_all | solution.py:34
  73.7 0.7 gather_fusion
  74.4 65.7 %all-to-all-done = bf16[3,16,56,512]{3,2,0,1:T(8,128)(2,1)S(1)} async-done(((bf16[3,16,56,512]{3,2,0,1:T(8,128)(2,1)}), bf16[3,16,56,512]{3,2,0,1:T(8,128)(2,1)S(1)}, u32[]{:S(2)}, u32[]{:S(2)}) %all-to-all-start) | async-done | bytes 2752544 | tf_op jit(solution)/shard_map/all_to_all | solution.py:34
  140.1 1.8 copy.60
  141.8 2.5 gather_fusion.1
  144.3 1.9 select_bitcast_fusion
  146.2 3.9 all-to-all-start.1
  151.2 64.4 %all-to-all-done.1 = bf16[3,16,56,512]{3,2,0,1:T(8,128)(2,1)S(1)} async-done(((bf16[3,16,56,512]{3,2,0,1:T(8,128)(2,1)}), bf16[3,16,56,512]{3,2,0,1:T(8,128)(2,1)S(1)}, u32[]{:S(2)}, u32[]{:S(2)}) %all-to-all-start.1) | async-done | bytes 2752544 | tf_op jit(solution)/shard_map/all_to_all | solution.py:36
  215.6 1.6 fusion.31
  217.1 2.3 copy.61
  219.4 0.8 collective-permute-start
  220.5 0.6 copy.62
  221.2 20.4 %collective-permute-done = bf16[896,512]{0,1:T(8,128)(2,1)S(1)} collective-permute-done((bf16[896,512]{0,1:T(8,128)(2,1)}, bf16[896,512]{0,1:T(8,128)(2,1)S(1)}, u32[]{:S(2)}, u32[]{:S(2)}) %collective-permute-start) | collective-permute-done | bytes 917536 | tf_op jit(solution)/shard_map/ppermute | solution.py:108
  241.5 1.4 pad_maximum_fusion.2
  243.2 0.9 convolution_convert_fusion.1
  244.0 1.8 fusion.3
  245.9 2.8 gather_fusion.2
  249.0 74.0 %all_to_all.15 = bf16[16,24,3712]{2,1,0:T(8,128)(2,1)S(1)} all-to-all(bf16[16,24,3712]{2,1,0:T(8,128)(2,1)S(1)} %broadcast_select_fusion), channel_id=1, replica_groups=mesh['dp'=4,'grp'=16,'ylo'=2,'xhi'=2] {'grp'}, dimensions={0} | all-to-all | bytes 5701632 | tf_op jit(solution)/shard_map/all_to_all | solution.py:89
  323.6 60.5 %collective-permute-done.1 = bf16[16,24,3712]{2,1,0:T(8,128)(2,1)} collective-permute-done((bf16[16,24,3712]{2,1,0:T(8,128)(2,1)S(1)}, bf16[16,24,3712]{2,1,0:T(8,128)(2,1)}, u32[]{:S(2)}, u32[]{:S(2)}) %collective-permute-start.1) | collective-permute-done | bytes 2850848 | tf_op jit(solution)/shard_map/ppermute | solution.py:90
  384.1 2.4 pad_maximum_fusion
  386.5 2.5 copy-done.4
  389.1 10.3 %fusion.4 = f32[2,768,512]{1,2,0:T(8,128)S(1)} fusion(bf16[768,3712,1]{1,0,2:T(8,128)(2,1)} %bitcast.101, bf16[2,3584,512]{1,2,0:T(8,128)(2,1)} %all-gather.2.cloned.1.call-done), kind=kOutput, calls=%fused_computation.18 | convolution fusion | flops 5838471168 | bytes 16187392 | tf_op jit(solution)/shard_map/rd,kdn->krn/dot_general | solution.py:111
  399.9 0.9 collective-permute-start.2
  400.9 1.5 convert.5
  402.4 1.5 convert.6
  404.1 5.2 %collective-permute-done.2 = bf16[768,256]{0,1:T(8,128)(2,1)S(1)} collective-permute-done((bf16[768,256]{0,1:T(8,128)(2,1)S(1)}, bf16[768,256]{0,1:T(8,128)(2,1)S(1)}, u32[]{:S(2)}, u32[]{:S(2)}) %collective-permute-start.2) | collective-permute-done | bytes 393248 | tf_op jit(solution)/shard_map/ppermute | solution.py:118
  411.1 1.0 copy.69
  (65 shorter events, 4.6 us)
Async XLA Ops:
  7.2 1.2 copy-start
  7.2 51.4 %reduce-scatter.2.cloned.1.call-start = ((), (), s32[]{:S(2)}) async-start(), calls=%async_computation.4 | async-start | bytes 4587520 | tf_op jit(solution)/shard_map/reduce_scatter | solution.py:93
  12.2 46.4 %copy-start.7 = (f32[1,896,512]{2,1,0:T(8,128)S(1)}, f32[1,896,512]{2,1,0:T(8,128)}, u32[]{:S(2)}) copy-start(f32[1,896,512]{2,1,0:T(8,128)} %param.16) | copy-start | bytes 5505028
  12.2 46.4 %copy-start.9 = (bf16[1,896,512]{2,1,0:T(8,128)(2,1)S(1)}, bf16[1,896,512]{2,1,0:T(8,128)(2,1)}, u32[]{:S(2)}) copy-start(bf16[1,896,512]{2,1,0:T(8,128)(2,1)} %param.15) | copy-start | bytes 2752516
  63.8 9.7 %copy-start.11 = (s32[16]{0:T(128)S(1)}, s32[16]{0:T(128)}, u32[]{:S(2)}) copy-start(s32[16]{0:T(128)} %param.23) | copy-start | bytes 196
  63.8 9.9 %copy-start.2 = (s32[16]{0:T(128)S(1)}, s32[16]{0:T(128)}, u32[]{:S(2)}) copy-start(s32[16]{0:T(128)} %param.22) | copy-start | bytes 196
  63.8 76.3 %all-to-all-start = ((bf16[3,16,56,512]{3,2,0,1:T(8,128)(2,1)}), bf16[3,16,56,512]{3,2,0,1:T(8,128)(2,1)S(1)}, u32[]{:S(2)}, u32[]{:S(2)}) async-start(bf16[3,16,56,512]{3,2,0,1:T(8,128)(2,1)} %pad_maximum_fusion.1), calls=%async_computation.1 | async-start | bytes 5505024 | tf_op jit(solution)/shard_map/all_to_all | solution.py:34
  146.2 4.7 %copy-start.10 = (s32[1,1,128,2]{2,3,1,0:T(2,128)S(1)}, s32[1,1,128,2]{2,3,1,0:T(2,128)}, u32[]{:S(2)}) copy-start(s32[1,1,128,2]{2,3,1,0:T(2,128)} %param.19) | copy-start | bytes 3076
  146.2 69.3 %all-to-all-start.1 = ((bf16[3,16,56,512]{3,2,0,1:T(8,128)(2,1)}), bf16[3,16,56,512]{3,2,0,1:T(8,128)(2,1)S(1)}, u32[]{:S(2)}, u32[]{:S(2)}) async-start(bf16[3,16,56,512]{3,2,0,1:T(8,128)(2,1)} %select_bitcast_fusion), calls=%async_computation.2 | async-start | bytes 5505024 | tf_op jit(solution)/shard_map/all_to_all | solution.py:36
  150.2 238.9 %all-gather.2.cloned.1.call-start = ((), (), s32[]{:S(2)}) async-start(), calls=%async_computation.5 | async-start | bytes 9175040 | tf_op jit(solution)/shard_map/all_gather | solution.py:109
  151.2 69.2 %copy-start.12 = (bf16[1,1,128,2]{2,3,1,0:T(2,128)(2,1)S(1)}, bf16[1,1,128,2]{2,3,1,0:T(2,128)(2,1)}, u32[]{:S(2)}) copy-start(bf16[1,1,128,2]{2,3,1,0:T(2,128)(2,1)} %param.20) | copy-start | bytes 1540
  217.1 3.4 copy-start.3
  219.4 22.1 %collective-permute-start = (bf16[896,512]{0,1:T(8,128)(2,1)}, bf16[896,512]{0,1:T(8,128)(2,1)S(1)}, u32[]{:S(2)}, u32[]{:S(2)}) collective-permute-start(bf16[896,512]{0,1:T(8,128)(2,1)} %copy.61), channel_id=1, source_target_pairs={{0,1},{1,0},{2,3},{3,2},{4,5},{5,4},{6,7},{7,6},{8,9},{9,8},{10,11... | collective-permute-start | bytes 2752520 | tf_op jit(solution)/shard_map/ppermute | solution.py:108
  241.5 1.6 copy-start.8
  323.0 61.1 %collective-permute-start.1 = (bf16[16,24,3712]{2,1,0:T(8,128)(2,1)S(1)}, bf16[16,24,3712]{2,1,0:T(8,128)(2,1)}, u32[]{:S(2)}, u32[]{:S(2)}) collective-permute-start(bf16[16,24,3712]{2,1,0:T(8,128)(2,1)S(1)} %all_to_all.15), channel_id=1, source_target_pairs={{0,2},{2,0},{1,3},{3,1},{4,6},{6,4},{5,7},{7,5},{8,10},{10,8},{9,1... | collective-permute-start | bytes 8552456 | tf_op jit(solution)/shard_map/ppermute | solution.py:90
  386.5 2.5 copy-start.4
  399.4 1.6 copy-start.6
  399.9 2.5 copy-start.5
  399.9 9.4 %collective-permute-start.2 = (bf16[768,256]{0,1:T(8,128)(2,1)S(1)}, bf16[768,256]{0,1:T(8,128)(2,1)S(1)}, u32[]{:S(2)}, u32[]{:S(2)}) collective-permute-start(bf16[768,256]{0,1:T(8,128)(2,1)S(1)} %get-tuple-element.29), channel_id=1, source_target_pairs={{0,1},{1,0},{2,3},{3,2},{4,5},{5,4},{6,7},{7,6},{8,9},{9,8},{10,11... | collective-permute-start | bytes 1179656 | tf_op jit(solution)/shard_map/ppermute | solution.py:118
  410.2 1.9 copy-start.1
Sparse Core Ops, SparseCore 0:
  12.3 46.2 reduce-scatter.1
  243.1 71.2 all-gather.1

commit v3 on v2

--- a/solution.py
+++ b/solution.py
@@ -87,8 +87,6 @@
     payload = jnp.concatenate([packed, scale_cols], axis=2)
     to_group = jnp.take(payload, holder, axis=0)
     by_group = lax.all_to_all(to_group, "grp", split_axis=0, concat_axis=0, tiled=True)
-    from_ylo = lax.ppermute(by_group, "ylo", perm=[(0, 1), (1, 0)])
-    near = jnp.stack([by_group, from_ylo]).reshape(2 * groups * capacity, D + SCALE_PAD)
 
     grads = lax.psum_scatter(
         lax.dot_general(
@@ -97,7 +95,11 @@
         "dp",
         scatter_dimension=0,
         tiled=True,
-    ).astype(jnp.float32)
+    )
+    by_group, grads = lax.optimization_barrier((by_group, grads))
+    grads = grads.astype(jnp.float32)
+    near = lax.all_gather(by_group, "ylo", axis=0, tiled=False)
+    near = near.reshape(2 * groups * capacity, D + SCALE_PAD)
     stepped, first_next, second_next = adamw(weights[0], first_moment[0], second_moment[0], grads)
     state = jnp.stack(
         [stepped, first_next.astype(jnp.bfloat16), second_next.astype(jnp.bfloat16)]
@@ -117,11 +119,9 @@
     ).astype(jnp.bfloat16)
     for_partner = lax.ppermute(result[1], "xhi", perm=[(0, 1), (1, 0)])
     mine = jnp.stack([result[0], for_partner]).reshape(2, 2, groups, capacity, hidden_units)
-    ylo = lax.axis_index("ylo")
     xhi = lax.axis_index("xhi")
     flip = jnp.arange(2, dtype=jnp.int32)
     mine = jnp.take(mine, flip ^ xhi, axis=0)
-    mine = jnp.take(mine, flip ^ ylo, axis=1)
     hidden = jnp.transpose(mine, (2, 1, 0, 3, 4)).reshape(1, 1, experts * capacity, hidden_units)
     return (
         hidden,

time: 419 us -> 406 us (0.969)
  waiting for transfers between devices: 263 us -> 252 us
  starting transfers between devices: 16.1 us -> 9.39 us
  blocking collectives: 74 us -> 80.6 us
    all_gather x1, waiting for transfers between devices: 0.02 us -> 76.7 us  [local(): lax.all_gather(jnp.stack([new_weight, partner_weight]), 'dp', axis=1, til...]
    ppermute x1 -> x0, waiting for transfers between devices: 60.5 us -> none  [local(): from_ylo = lax.ppermute(by_group, 'ylo', perm=[(0, 1), (1, 0)])]
    reduce_scatter x1, waiting for transfers between devices: 46.4 us -> 0.01 us  [local(): lax.psum_scatter(lax.dot_general(activations, cotangent, (((0,), (0,)), (...]
    all_gather x0 -> x1, waiting for transfers between devices: none -> 15.3 us  [local(): near = lax.all_gather(by_group, 'ylo', axis=0, tiled=False)]
    all_to_all x1, blocking collectives: 74 us -> 80.6 us  [local(): lax.all_to_all(to_group, 'grp', split_axis=0, concat_axis=0, tiled=True)]
    all_to_all x1, starting transfers between devices: 9.71 us -> 3.73 us  [migrate(): lax.all_to_all(split, 'grp', split_axis=1, concat_axis=1, tiled=True)]
  transfers between devices with their start and end apart: 7 -> 7, of which waited for: 6 -> 6; matrix products, arithmetic and copies ran while one was open for 3% -> 5% of each run, Pallas kernels for 0% -> 0%
where the time goes in v3:
time: 406 us; the launch traced here: 404 us
  waiting for transfers between devices  252 us (62%)
  blocking collectives  80.6 us (20%)
  matrix products  16.3 us (4%)
  local copies, waits for them, and re-layouts  15.9 us (4%)
  other arithmetic  15.8 us (4%)
  between operations  14.7 us (4%)
  starting transfers between devices  9.39 us (2%)
    all_to_all x1, blocking collectives, local(): lax.all_to_all(to_group, 'grp', split_axis=0, concat_axis=0, tiled=True)  80.6 us
    all_gather x1, waiting for transfers between devices, local(): lax.all_gather(jnp.stack([new_weight, partner_weight]), 'dp', axis=1, til...  76.7 us
    all_to_all x1, waiting for transfers between devices, migrate(): lax.all_to_all(chosen, 'grp', split_axis=1, concat_axis=1, tiled=True)  65.2 us
    all_to_all x1, waiting for transfers between devices, migrate(): lax.all_to_all(split, 'grp', split_axis=1, concat_axis=1, tiled=True)  64.5 us
    ppermute x1, waiting for transfers between devices, local(): partner_weight = lax.ppermute(new_weight, 'xhi', perm=[(0, 1), (1, 0)])  20.1 us
    all_gather x1, waiting for transfers between devices, local(): near = lax.all_gather(by_group, 'ylo', axis=0, tiled=False)  15.3 us
    dot_general x1, matrix products, local(): jnp.einsum('rd,kdn->krn', near, both, preferred_element_type=jnp.float32)  10.3 us
    ppermute x1, waiting for transfers between devices, local(): for_partner = lax.ppermute(result[1], 'xhi', perm=[(0, 1), (1, 0)])  9.13 us
  transfers between devices with their start and end apart: 7, of which 6 were waited for; matrix products, arithmetic and copies ran while one was open for 5% of the time, Pallas kernels for 0%

profile of v3, /device:TPU:4, one launch (start us, length us, event | category | flops | bytes accessed | tf_op | source)
XLA Modules:
  0.0 404.3 jit_solution(6695283364746242156)
XLA Ops:
  7.2 1.1 copy-done
  8.4 3.8 convolution_convert_fusion
  13.5 2.0 convolution_convert_fusion.1
  15.9 1.8 fusion.3
  17.6 2.8 gather_fusion.1
  20.4 0.7 gather_fusion
  21.5 80.6 %all_to_all.15 = bf16[16,24,3712]{2,1,0:T(8,128)(2,1)} all-to-all(bf16[16,24,3712]{2,1,0:T(8,128)(2,1)S(1)} %broadcast_select_fusion), channel_id=1, replica_groups=mesh['dp'=4,'grp'=16,'ylo'=2,'xhi'=2] {'grp'}, dimensions={0} | all-to-all | bytes 5701632 | tf_op jit(solution)/shard_map/all_to_all | solution.py:89
  102.1 3.4 fusion.9
  105.5 1.8 pad_maximum_fusion
  107.3 3.7 all-to-all-start.1
  111.1 64.5 %all-to-all-done.1 = bf16[3,16,56,512]{3,2,0,1:T(8,128)(2,1)S(1)} async-done(((bf16[3,16,56,512]{3,2,0,1:T(8,128)(2,1)}), bf16[3,16,56,512]{3,2,0,1:T(8,128)(2,1)S(1)}, u32[]{:S(2)}, u32[]{:S(2)}) %all-to-all-start.1) | async-done | bytes 2752544 | tf_op jit(solution)/shard_map/all_to_all | solution.py:34
  175.6 1.8 copy.63
  177.4 2.5 gather_fusion.2
  179.9 1.9 select_bitcast_fusion
  181.8 4.0 all-to-all-start.2
  185.8 0.7 all-gather.6.cloned.1.call-update
  186.6 65.2 %all-to-all-done.2 = bf16[3,16,56,512]{3,2,0,1:T(8,128)(2,1)S(1)} async-done(((bf16[3,16,56,512]{3,2,0,1:T(8,128)(2,1)}), bf16[3,16,56,512]{3,2,0,1:T(8,128)(2,1)S(1)}, u32[]{:S(2)}, u32[]{:S(2)}) %all-to-all-start.2) | async-done | bytes 2752544 | tf_op jit(solution)/shard_map/all_to_all | solution.py:36
  251.8 1.6 fusion.30
  253.4 1.5 copy.64
  255.5 1.5 copy.65
  257.1 20.1 %collective-permute-done = bf16[896,512]{0,1:T(8,128)(2,1)S(1)} collective-permute-done((bf16[896,512]{0,1:T(8,128)(2,1)S(1)}, bf16[896,512]{0,1:T(8,128)(2,1)S(1)}, u32[]{:S(2)}, u32[]{:S(2)}) %collective-permute-start) | collective-permute-done | bytes 917536 | tf_op jit(solution)/shard_map/ppermute | solution.py:110
  277.2 1.4 pad_maximum_fusion.1
  278.6 15.3 %all-gather.6.cloned.1.call-done = bf16[32,24,3712]{2,1,0:T(8,128)(2,1)} async-done(((bf16[16,24,3712]{2,1,0:T(8,128)(2,1)}), bf16[32,24,3712]{2,1,0:T(8,128)(2,1)}) %all-gather.6.cloned.1.call-update) | async-done | bytes 5701648 | tf_op jit(solution)/shard_map/all_gather | solution.py:101
  293.9 1.1 convert_reduce_fusion
  295.0 76.7 %all-gather.4.cloned.1.call-done = bf16[2,3584,512]{1,2,0:T(8,128)(2,1)} async-done(((bf16[2,896,512]{1,2,0:T(8,128)(2,1)}), bf16[2,3584,512]{1,2,0:T(8,128)(2,1)}) %all-gather.4.cloned.1.call-update) | async-done | bytes 7340048 | tf_op jit(solution)/shard_map/all_gather | solution.py:111
  371.7 10.3 %fusion.4 = f32[2,768,512]{1,2,0:T(8,128)S(1)} fusion(bf16[768,3712,1]{1,0,2:T(8,128)(2,1)} %bitcast.107, bf16[2,3584,512]{1,2,0:T(8,128)(2,1)} %all-gather.4.cloned.1.call-done), kind=kOutput, calls=%fused_computation.16 | convolution fusion | flops 5838471168 | bytes 16187392 | tf_op jit(solution)/shard_map/rd,kdn->krn/dot_general | solution.py:113
  382.6 0.9 collective-permute-start.1
  383.5 1.5 convert.5
  385.0 1.5 convert.6
  386.7 9.1 %collective-permute-done.1 = bf16[768,256]{0,1:T(8,128)(2,1)S(1)} collective-permute-done((bf16[768,256]{0,1:T(8,128)(2,1)S(1)}, bf16[768,256]{0,1:T(8,128)(2,1)S(1)}, u32[]{:S(2)}, u32[]{:S(2)}) %collective-permute-start.1) | collective-permute-done | bytes 393248 | tf_op jit(solution)/shard_map/ppermute | solution.py:120
  396.1 0.6 gather_fusion.3
  396.8 1.0 copy.68
  (54 shorter events, 3.2 us)
Async XLA Ops:
  7.2 1.2 copy-start
  7.2 94.9 %reduce-scatter.2.cloned.1.call-start = ((), (), s32[]{:S(2)}) async-start(), calls=%async_computation.4 | async-start | bytes 4587520 | tf_op jit(solution)/shard_map/reduce_scatter | solution.py:91
  12.2 0.7 copy-start.7
  12.2 1.1 copy-start.8
  12.2 3.3 copy-start.9
  17.6 2.8 copy-start.2
  21.5 80.6 %copy-start.5 = (f32[1,896,512]{2,1,0:T(8,128)S(1)}, f32[1,896,512]{2,1,0:T(8,128)}, u32[]{:S(2)}) copy-start(f32[1,896,512]{2,1,0:T(8,128)} %param.16) | copy-start | bytes 5505028
  21.5 80.6 %copy-start.6 = (bf16[1,896,512]{2,1,0:T(8,128)(2,1)S(1)}, bf16[1,896,512]{2,1,0:T(8,128)(2,1)}, u32[]{:S(2)}) copy-start(bf16[1,896,512]{2,1,0:T(8,128)(2,1)} %param.15) | copy-start | bytes 2752516
  107.3 68.3 %all-to-all-start.1 = ((bf16[3,16,56,512]{3,2,0,1:T(8,128)(2,1)}), bf16[3,16,56,512]{3,2,0,1:T(8,128)(2,1)S(1)}, u32[]{:S(2)}, u32[]{:S(2)}) async-start(bf16[3,16,56,512]{3,2,0,1:T(8,128)(2,1)} %pad_maximum_fusion), calls=%async_computation.2 | async-start | bytes 5505024 | tf_op jit(solution)/shard_map/all_to_all | solution.py:34
  181.8 70.1 %all-to-all-start.2 = ((bf16[3,16,56,512]{3,2,0,1:T(8,128)(2,1)}), bf16[3,16,56,512]{3,2,0,1:T(8,128)(2,1)S(1)}, u32[]{:S(2)}, u32[]{:S(2)}) async-start(bf16[3,16,56,512]{3,2,0,1:T(8,128)(2,1)} %select_bitcast_fusion), calls=%async_computation.3 | async-start | bytes 5505024 | tf_op jit(solution)/shard_map/all_to_all | solution.py:36
  185.8 108.1 %all-gather.6.cloned.1.call-start = ((), (), s32[]{:S(2)}) async-start(), calls=%async_computation.6 | async-start | bytes 8552448 | tf_op jit(solution)/shard_map/all_gather | solution.py:101
  186.5 185.2 %all-gather.4.cloned.1.call-start = ((), (), s32[]{:S(2)}) async-start(), calls=%async_computation.5 | async-start | bytes 9175040 | tf_op jit(solution)/shard_map/all_gather | solution.py:111
  254.9 22.3 %collective-permute-start = (bf16[896,512]{0,1:T(8,128)(2,1)S(1)}, bf16[896,512]{0,1:T(8,128)(2,1)S(1)}, u32[]{:S(2)}, u32[]{:S(2)}) collective-permute-start(bf16[896,512]{0,1:T(8,128)(2,1)S(1)} %copy.64), channel_id=1, source_target_pairs={{0,1},{1,0},{2,3},{3,2},{4,5},{5,4},{6,7},{7,6},{8,9},{9,8},{10,11... | collective-permute-start | bytes 2752520 | tf_op jit(solution)/shard_map/ppermute | solution.py:110
  382.0 1.5 copy-start.4
  382.5 2.5 copy-start.3
  382.6 13.2 %collective-permute-start.1 = (bf16[768,256]{0,1:T(8,128)(2,1)S(1)}, bf16[768,256]{0,1:T(8,128)(2,1)S(1)}, u32[]{:S(2)}, u32[]{:S(2)}) collective-permute-start(bf16[768,256]{0,1:T(8,128)(2,1)S(1)} %get-tuple-element.33), channel_id=1, source_target_pairs={{0,1},{1,0},{2,3},{3,2},{4,5},{5,4},{6,7},{7,6},{8,9},{9,8},{10,11... | collective-permute-start | bytes 1179656 | tf_op jit(solution)/shard_map/ppermute | solution.py:120
  396.0 1.8 copy-start.1
Sparse Core Ops, SparseCore 0:
  12.3 46.2 reduce-scatter.1
  188.4 105.4 all-gather.5
  296.3 75.3 all-gather.3

commit v4 on v3

--- a/solution.py
+++ b/solution.py
@@ -27,12 +27,13 @@
     return stepped.astype(jnp.bfloat16), first_next, second_next
 
 
-def migrate(state, group_source, groups):
+def migrate(state, group_source, groups, held):
     layers, rows_dev, width = state.shape
     piece_rows = rows_dev // groups
     split = state.reshape(layers, groups, piece_rows, width)
     spread = lax.all_to_all(split, "grp", split_axis=1, concat_axis=1, tiled=True)
     chosen = jnp.take(spread, group_source, axis=1)
+    chosen, _ = lax.optimization_barrier((chosen, held))
     home = lax.all_to_all(chosen, "grp", split_axis=1, concat_axis=1, tiled=True)
     return home.reshape(layers, rows_dev, width)
 
@@ -92,7 +93,7 @@
         lax.dot_general(
             activations, cotangent, (((0,), (0,)), ((), ())), preferred_element_type=jnp.float32
         ).astype(jnp.bfloat16),
-        "dp",
+        ("xlo", "core"),
         scatter_dimension=0,
         tiled=True,
     )
@@ -104,11 +105,13 @@
     state = jnp.stack(
         [stepped, first_next.astype(jnp.bfloat16), second_next.astype(jnp.bfloat16)]
     )
-    moved = migrate(state, group_source, groups)
+    moved = migrate(state, group_source, groups, near)
     new_weight = moved[0]
 
     partner_weight = lax.ppermute(new_weight, "xhi", perm=[(0, 1), (1, 0)])
-    both = lax.all_gather(jnp.stack([new_weight, partner_weight]), "dp", axis=1, tiled=True)
+    shards = lax.all_gather(jnp.stack([new_weight, partner_weight]), "xlo", axis=0, tiled=False)
+    shards = lax.all_gather(shards, "core", axis=0, tiled=False)
+    both = jnp.transpose(shards, (2, 1, 0, 3, 4)).reshape(2, -1, width)
     both = jnp.pad(both, ((0, 0), (0, SCALE_PAD), (0, 0)))
     projected = jnp.einsum("rd,kdn->krn", near, both, preferred_element_type=jnp.float32)
     scaling = near[:, D].astype(jnp.float32)
@@ -135,26 +138,28 @@
     n_dp = mesh.shape["dp"]
     n_expert = mesh.shape["expert"]
     mesh4 = Mesh(
-        mesh.devices.reshape(n_dp, n_expert // GRP, 2, 2), ("dp", "grp", "ylo", "xhi")
+        mesh.devices.reshape(2, n_dp // 2, n_expert // GRP, 2, 2),
+        ("xlo", "core", "grp", "ylo", "xhi"),
     )
+    dp = ("xlo", "core")
     ex = ("grp", "ylo", "xhi")
     in_specs = (
-        P("dp", ex, None, None),
-        P("dp", ex, None, None),
-        P(ex, "dp", None),
-        P(ex, "dp", None),
-        P(ex, "dp", None),
-        P("dp", ex, None, None),
-        P("dp", ex, None, None),
-        P("dp", ex, None, None),
-        P("dp", ex),
+        P(dp, ex, None, None),
+        P(dp, ex, None, None),
+        P(ex, dp, None),
+        P(ex, dp, None),
+        P(ex, dp, None),
+        P(dp, ex, None, None),
+        P(dp, ex, None, None),
+        P(dp, ex, None, None),
+        P(dp, ex),
         P(),
         P(),
     )
     out_specs = (
-        P("dp", ex, None, None),
-        P(ex, "dp", None),
-        P(ex, "dp", None),
-        P(ex, "dp", None),
+        P(dp, ex, None, None),
+        P(ex, dp, None),
+        P(ex, dp, None),
+        P(ex, dp, None),
     )
     return jax.shard_map(local, mesh=mesh4, in_specs=in_specs, out_specs=out_specs, check_vma=False)

time: 406 us -> 459 us (1.13)
  blocking collectives: 80.6 us -> 158 us
  waiting for transfers between devices: 252 us -> 190 us
  local copies, waits for them, and re-layouts: 15.9 us -> 49.4 us
  other arithmetic: 15.8 us -> 21.5 us
    all_to_all x0 -> x1, blocking collectives: none -> 77.4 us  [migrate(): lax.all_to_all(chosen, 'grp', split_axis=1, concat_axis=1, tiled=True)]
    all_to_all x1 -> x0, waiting for transfers between devices: 65.2 us -> none  [migrate(): lax.all_to_all(chosen, 'grp', split_axis=1, concat_axis=1, tiled=True)]
    transpose x0 -> x1, local copies, waits for them, and re-layouts: none -> 18.9 us  [local(): both = jnp.transpose(shards, (2, 1, 0, 3, 4)).reshape(2, -1, width)]
    reshape x0 -> x1, local copies, waits for them, and re-layouts: none -> 16.3 us  [local(): both = jnp.transpose(shards, (2, 1, 0, 3, 4)).reshape(2, -1, width)]
    all_gather x1 -> x2, waiting for transfers between devices: 76.7 us -> 76.6 us  [the longest x1 51.1 us: local(): lax.all_gather(jnp.stack([new_weight, partner_weight]), 'xlo', axis=0, ti...]
  transfers between devices with their start and end apart: 7 -> 7, of which waited for: 6 -> 6; matrix products, arithmetic and copies ran while one was open for 5% -> 7% of each run, Pallas kernels for 0% -> 0%
where the time goes in v4:
time: 459 us; the launch traced here: 456 us
  waiting for transfers between devices  190 us (41%)
  blocking collectives  158 us (34%)
  local copies, waits for them, and re-layouts  49.4 us (11%)
  other arithmetic  21.5 us (5%)
  matrix products  16.7 us (4%)
  between operations  14.7 us (3%)
  starting transfers between devices  6.39 us (1%)
    all_to_all x1, blocking collectives, local(): lax.all_to_all(to_group, 'grp', split_axis=0, concat_axis=0, tiled=True)  80.6 us
    all_to_all x1, blocking collectives, migrate(): lax.all_to_all(chosen, 'grp', split_axis=1, concat_axis=1, tiled=True)  77.4 us
    all_to_all x1, waiting for transfers between devices, migrate(): lax.all_to_all(split, 'grp', split_axis=1, concat_axis=1, tiled=True)  64.2 us
    all_gather x1, waiting for transfers between devices, local(): lax.all_gather(jnp.stack([new_weight, partner_weight]), 'xlo', axis=0, ti...  51.1 us
    all_gather x1, waiting for transfers between devices, local(): shards = lax.all_gather(shards, 'core', axis=0, tiled=False)  25.5 us
    ppermute x1, waiting for transfers between devices, local(): partner_weight = lax.ppermute(new_weight, 'xhi', perm=[(0, 1), (1, 0)])  21.6 us
    transpose x1, local copies, waits for them, and re-layouts, local(): both = jnp.transpose(shards, (2, 1, 0, 3, 4)).reshape(2, -1, width)  18.9 us
    all_gather x1, waiting for transfers between devices, local(): near = lax.all_gather(by_group, 'ylo', axis=0, tiled=False)  18.5 us
  transfers between devices with their start and end apart: 7, of which 6 were waited for; matrix products, arithmetic and copies ran while one was open for 7% of the time, Pallas kernels for 0%

profile of v4, /device:TPU:4, one launch (start us, length us, event | category | flops | bytes accessed | tf_op | source)
XLA Modules:
  0.0 456.4 jit_solution(17772084890998923934)
XLA Ops:
  7.2 1.1 copy-done
  8.4 3.8 convolution_convert_fusion
  13.6 2.4 convolution_convert_fusion.1
  16.4 3.5 fusion.3
  19.9 4.3 gather_fusion.1
  24.2 0.7 gather_fusion
  24.9 2.2 broadcast_select_fusion
  27.1 80.6 %all_to_all.15 = bf16[16,24,3712]{2,1,0:T(8,128)(2,1)} all-to-all(bf16[16,24,3712]{2,1,0:T(8,128)(2,1)S(1)} %broadcast_select_fusion), channel_id=1, replica_groups=mesh['xlo'=2,'core'=2,'grp'=16,'ylo'=2,'xhi'=2] {'grp'}, dimensions={0} | all-to-all | bytes 5701632 | tf_op jit(solution)/shard_map/all_to_all | solution.py:90
  107.7 1.5 copy-done.4
  109.2 3.7 fusion.9
  112.9 1.9 pad_maximum_fusion
  114.8 4.5 all-to-all-start.1
  119.4 64.2 %all-to-all-done.1 = bf16[3,16,56,512]{3,2,0,1:T(8,128)(2,1)} async-done(((bf16[3,16,56,512]{3,2,0,1:T(8,128)(2,1)}), bf16[3,16,56,512]{3,2,0,1:T(8,128)(2,1)}, u32[]{:S(2)}, u32[]{:S(2)}) %all-to-all-start.1) | async-done | bytes 2752544 | tf_op jit(solution)/shard_map/all_to_all | solution.py:34
  183.5 4.1 gather_fusion.2
  187.6 3.7 select_bitcast_fusion
  191.3 18.5 %all-gather.7.cloned.1.call-done = bf16[32,24,3712]{2,1,0:T(8,128)(2,1)} async-done(((bf16[16,24,3712]{2,1,0:T(8,128)(2,1)}), bf16[32,24,3712]{2,1,0:T(8,128)(2,1)}) %all-gather.7.cloned.1.call-update) | async-done | bytes 5701648 | tf_op jit(solution)/shard_map/all_gather | solution.py:102
  209.8 77.4 %all_to_all.16 = bf16[3,16,56,512]{3,2,0,1:T(8,128)(2,1)S(1)} all-to-all(bf16[3,16,56,512]{3,2,0,1:T(8,128)(2,1)} %select_bitcast_fusion), channel_id=1, replica_groups=mesh['xlo'=2,'core'=2,'grp'=16,'ylo'=2,'xhi'=2] {'grp'}, dimensions={1} | all-to-all | bytes 5505024 | tf_op jit(solution)/shard_map/all_to_all | solution.py:37
  287.4 0.6 collective-permute-start
  288.0 21.6 %collective-permute-done = bf16[896,512]{1,0:T(8,128)(2,1)S(1)} collective-permute-done((bf16[896,512]{1,0:T(8,128)(2,1)S(1)}, bf16[896,512]{1,0:T(8,128)(2,1)S(1)}, u32[]{:S(2)}, u32[]{:S(2)}) %collective-permute-start) | collective-permute-done | bytes 917536 | tf_op jit(solution)/shard_map/ppermute | solution.py:111
  309.6 1.4 pad_maximum_fusion.1
  311.3 51.1 %all-gather.9.cloned.1.call-done = bf16[4,896,512]{2,1,0:T(8,128)(2,1)} async-done(((bf16[2,896,512]{2,1,0:T(8,128)(2,1)}), bf16[4,896,512]{2,1,0:T(8,128)(2,1)}) %all-gather.9.cloned.1.call-update) | async-done | bytes 3670032 | tf_op jit(solution)/shard_map/all_gather | solution.py:112
  362.3 1.1 convert_reduce_fusion
  363.4 25.5 %all-gather.11.cloned.1.call-done = bf16[4,2,896,512]{3,2,1,0:T(8,128)(2,1)} async-done(((bf16[2,2,896,512]{3,2,1,0:T(8,128)(2,1)}), bf16[4,2,896,512]{3,2,1,0:T(8,128)(2,1)}) %all-gather.11.cloned.1.call-update) | async-done | bytes 7340048 | tf_op jit(solution)/shard_map/all_gather | solution.py:113
  388.9 18.9 %copy.56 = bf16[2,2,2,896,512]{3,2,1,4,0:T(2,128)(2,1)} copy(bf16[2,2,2,896,512]{4,3,0,1,2:T(8,128)(2,1)} %bitcast.98) | data formatting | bytes 14680064 | tf_op jit(solution)/shard_map/transpose | solution.py:114
  407.8 16.3 %reshape.199 = bf16[2,3584,512]{1,2,0:T(8,128)(2,1)} reshape(bf16[2,2,2,896,512]{3,2,1,4,0:T(2,128)(2,1)} %copy.56) | data formatting | bytes 14680064 | tf_op jit(solution)/shard_map/reshape | solution.py:114
  424.1 10.2 %fusion.4 = f32[2,768,512]{1,2,0:T(8,128)S(1)} fusion(bf16[768,3712,1]{1,0,2:T(8,128)(2,1)} %bitcast.115, bf16[2,3584,512]{1,2,0:T(8,128)(2,1)} %reshape.199), kind=kOutput, calls=%fused_computation.16 | convolution fusion | flops 5838471168 | bytes 16187392 | tf_op jit(solution)/shard_map/rd,kdn->krn/dot_general | solution.py:116
  434.9 0.9 collective-permute-start.1
  435.9 1.5 convert.5
  437.4 1.5 convert.6
  439.0 8.8 %collective-permute-done.1 = bf16[768,256]{0,1:T(8,128)(2,1)S(1)} collective-permute-done((bf16[768,256]{0,1:T(8,128)(2,1)S(1)}, bf16[768,256]{0,1:T(8,128)(2,1)S(1)}, u32[]{:S(2)}, u32[]{:S(2)}) %collective-permute-start.1) | collective-permute-done | bytes 393248 | tf_op jit(solution)/shard_map/ppermute | solution.py:123
  448.1 0.6 gather_fusion.3
  448.9 1.0 copy.59
  (53 shorter events, 2.7 us)
Async XLA Ops:
  7.2 1.2 copy-start
  7.2 100.5 %reduce-scatter.2.cloned.1.call-start = ((), (), s32[]{:S(2)}) async-start(), calls=%async_computation.4 | async-start | bytes 4587520 | tf_op jit(solution)/shard_map/reduce_scatter | solution.py:92
  12.2 0.8 copy-start.6
  12.2 1.2 copy-start.7
  12.2 1.4 copy-start.5
  12.2 3.8 copy-start.8
  12.2 197.5 %all-gather.7.cloned.1.call-start = ((), (), s32[]{:S(2)}) async-start(), calls=%async_computation.5 | async-start | bytes 8552448 | tf_op jit(solution)/shard_map/all_gather | solution.py:102
  19.9 4.3 copy-start.2
  107.7 1.5 copy-start.4
  114.8 68.8 %all-to-all-start.1 = ((bf16[3,16,56,512]{3,2,0,1:T(8,128)(2,1)}), bf16[3,16,56,512]{3,2,0,1:T(8,128)(2,1)}, u32[]{:S(2)}, u32[]{:S(2)}) async-start(bf16[3,16,56,512]{3,2,0,1:T(8,128)(2,1)} %pad_maximum_fusion), calls=%async_computation.2 | async-start | bytes 5505024 | tf_op jit(solution)/shard_map/all_to_all | solution.py:34
  119.3 243.0 %all-gather.9.cloned.1.call-start = ((), (), s32[]{:S(2)}) async-start(), calls=%async_computation.6 | async-start | bytes 5505024 | tf_op jit(solution)/shard_map/all_gather | solution.py:112
  287.4 23.6 %copy-start.3 = (bf16[1,16,56,512]{3,2,0,1:T(8,128)(2,1)}, bf16[1,16,56,512]{3,2,0,1:T(8,128)(2,1)S(1)}, u32[]{:S(2)}) copy-start(bf16[1,16,56,512]{3,2,0,1:T(8,128)(2,1)S(1)} %get-tuple-element.26) | copy-start | bytes 2752516
  287.4 22.2 %collective-permute-start = (bf16[896,512]{1,0:T(8,128)(2,1)S(1)}, bf16[896,512]{1,0:T(8,128)(2,1)S(1)}, u32[]{:S(2)}, u32[]{:S(2)}) collective-permute-start(bf16[896,512]{1,0:T(8,128)(2,1)S(1)} %bitcast.100), channel_id=1, source_target_pairs={{0,1},{1,0},{2,3},{3,2},{4,5},{5,4},{6,7},{7,6},{8,9},{9,8},{10,11... | collective-permute-start | bytes 2752520 | tf_op jit(solution)/shard_map/ppermute | solution.py:111
  311.0 77.9 %all-gather.11.cloned.1.call-start = ((), (), s32[]{:S(2)}) async-start(), calls=%async_computation.7 | async-start | bytes 11010048 | tf_op jit(solution)/shard_map/all_gather | solution.py:113
  434.9 12.9 %collective-permute-start.1 = (bf16[768,256]{0,1:T(8,128)(2,1)S(1)}, bf16[768,256]{0,1:T(8,128)(2,1)S(1)}, u32[]{:S(2)}, u32[]{:S(2)}) collective-permute-start(bf16[768,256]{0,1:T(8,128)(2,1)S(1)} %get-tuple-element.31), channel_id=1, source_target_pairs={{0,1},{1,0},{2,3},{3,2},{4,5},{5,4},{6,7},{7,6},{8,9},{9,8},{10,11... | collective-permute-start | bytes 1179656 | tf_op jit(solution)/shard_map/ppermute | solution.py:123
  448.0 1.8 copy-start.1
Sparse Core Ops, SparseCore 0:
  12.3 46.2 reduce-scatter.1
  107.9 101.8 all-gather.6
  311.1 51.1 all-gather.8
  364.0 24.9 all-gather.10

commit v5 on v3

--- a/solution.py
+++ b/solution.py
@@ -101,11 +101,10 @@
     near = lax.all_gather(by_group, "ylo", axis=0, tiled=False)
     near = near.reshape(2 * groups * capacity, D + SCALE_PAD)
     stepped, first_next, second_next = adamw(weights[0], first_moment[0], second_moment[0], grads)
-    state = jnp.stack(
-        [stepped, first_next.astype(jnp.bfloat16), second_next.astype(jnp.bfloat16)]
-    )
-    moved = migrate(state, group_source, groups)
-    new_weight = moved[0]
+    new_weight = migrate(stepped[None], group_source, groups)[0]
+    moments = jnp.stack([first_next.astype(jnp.bfloat16), second_next.astype(jnp.bfloat16)])
+    moments, new_weight = lax.optimization_barrier((moments, new_weight))
+    moved = migrate(moments, group_source, groups)
 
     partner_weight = lax.ppermute(new_weight, "xhi", perm=[(0, 1), (1, 0)])
     both = lax.all_gather(jnp.stack([new_weight, partner_weight]), "dp", axis=1, tiled=True)
@@ -126,8 +125,8 @@
     return (
         hidden,
         new_weight[None],
+        moved[0].astype(jnp.float32)[None],
         moved[1].astype(jnp.float32)[None],
-        moved[2].astype(jnp.float32)[None],
     )
 
 

time: 406 us -> 311 us (0.77)
  waiting for transfers between devices: 252 us -> 99.3 us
  blocking collectives: 80.6 us -> 133 us
    all_gather x1, waiting for transfers between devices: 76.7 us -> 15.1 us  [local(): lax.all_gather(jnp.stack([new_weight, partner_weight]), 'dp', axis=1, til...]
    all_to_all x0 -> x1, blocking collectives: none -> 52.9 us  [migrate(): lax.all_to_all(split, 'grp', split_axis=1, concat_axis=1, tiled=True)]
    all_to_all x1, waiting for transfers between devices: 64.5 us -> 25.3 us  [migrate(): lax.all_to_all(split, 'grp', split_axis=1, concat_axis=1, tiled=True)]
    all_to_all x1 -> x2, waiting for transfers between devices: 65.2 us -> 38.9 us  [migrate(): lax.all_to_all(chosen, 'grp', split_axis=1, concat_axis=1, tiled=True)]
    all_gather x1, waiting for transfers between devices: 15.3 us -> 0.02 us  [local(): near = lax.all_gather(by_group, 'ylo', axis=0, tiled=False)]
    ppermute x1, waiting for transfers between devices: 9.13 us -> 0.01 us  [local(): for_partner = lax.ppermute(result[1], 'xhi', perm=[(0, 1), (1, 0)])]
  transfers between devices with their start and end apart: 7 -> 8, of which waited for: 6 -> 5; matrix products, arithmetic and copies ran while one was open for 5% -> 13% of each run, Pallas kernels for 0% -> 0%
where the time goes in v5:
time: 311 us
  blocking collectives  133 us (43%)
  waiting for transfers between devices  99.3 us (32%)
  other arithmetic  18.8 us (6%)
  matrix products  16.4 us (5%)
  local copies, waits for them, and re-layouts  15 us (5%)
  between operations  14.7 us (5%)
  starting transfers between devices  13.2 us (4%)
    all_to_all x1, blocking collectives, local(): lax.all_to_all(to_group, 'grp', split_axis=0, concat_axis=0, tiled=True)  80.3 us
    all_to_all x1, blocking collectives, migrate(): lax.all_to_all(split, 'grp', split_axis=1, concat_axis=1, tiled=True)  52.9 us
    all_to_all x2, waiting for transfers between devices, migrate(): lax.all_to_all(chosen, 'grp', split_axis=1, concat_axis=1, tiled=True)  38.9 us
    all_to_all x1, waiting for transfers between devices, migrate(): lax.all_to_all(split, 'grp', split_axis=1, concat_axis=1, tiled=True)  25.3 us
    ppermute x1, waiting for transfers between devices, local(): partner_weight = lax.ppermute(new_weight, 'xhi', perm=[(0, 1), (1, 0)])  19.9 us
    all_gather x1, waiting for transfers between devices, local(): lax.all_gather(jnp.stack([new_weight, partner_weight]), 'dp', axis=1, til...  15.1 us
    dot_general x1, matrix products, local(): jnp.einsum('rd,kdn->krn', near, both, preferred_element_type=jnp.float32)  10.3 us
    all_to_all x2, starting transfers between devices, migrate(): lax.all_to_all(chosen, 'grp', split_axis=1, concat_axis=1, tiled=True)  8.03 us
  transfers between devices with their start and end apart: 8, of which 5 were waited for; matrix products, arithmetic and copies ran while one was open for 13% of the time, Pallas kernels for 0%

profile of v5, /device:TPU:4, one launch (start us, length us, event | category | flops | bytes accessed | tf_op | source)
XLA Modules:
  0.0 310.5 jit_solution(9463162961277146493)
XLA Ops:
  7.2 1.1 copy-done
  8.4 3.9 %convolution_convert_fusion = bf16[3584,512]{1,0:T(8,128)(2,1)} fusion(bf16[1,1,128,3584]{3,2,1,0:T(8,128)(2,1)S(1)} %copy-done, bf16[1,1,128,512]{3,2,1,0:T(8,128)(2,1)} %param.14), kind=kOutput, calls=%fused_computation.7 | convolution fusion | flops 471597056 | bytes 4718592 | tf_op jit(solution)/shard_map/dot_general | solution.py:92
  13.6 2.1 convolution_convert_fusion.1
  16.0 1.8 fusion.3
  17.7 2.8 gather_fusion
  20.5 0.7 gather_fusion.1
  21.6 80.3 %all_to_all.25 = bf16[16,24,3712]{2,1,0:T(8,128)(2,1)} all-to-all(bf16[16,24,3712]{2,1,0:T(8,128)(2,1)S(1)} %broadcast_select_fusion), channel_id=1, replica_groups=mesh['dp'=4,'grp'=16,'ylo'=2,'xhi'=2] {'grp'}, dimensions={0} | all-to-all | bytes 5701632 | tf_op jit(solution)/shard_map/all_to_all | solution.py:89
  101.9 1.5 copy-done.4
  103.6 4.7 %fusion.9 = (bf16[896,512]{1,0:T(8,128)(2,1)}, bf16[1,896,512]{2,1,0:T(8,128)(2,1)}, bf16[1,896,512]{2,1,0:T(8,128)(2,1)}) fusion(bf16[1,896,512]{2,1,0:T(8,128)(2,1)S(1)} %copy-done.5, bf16[896,512]{1,0:T(8,128)(2,1)} %reduce-scatter.2.cloned.1.call-done, f32[1,896,512]{2,1,0:T(8,128)S(1)} %copy-done.4, f32[1,896,512]{2,1,0:T(8,128)} %param.17), kind=kLoop, calls=%fused_computation.21 | loop fusion | flops 8257536 | bytes 8257536 | tf_op jit(solution)/shard_map/convert_element_type | solution.py:27
  108.3 3.7 %all-to-all-start.1 = ((bf16[1,16,56,512]{3,2,0,1:T(8,128)(2,1)}), bf16[1,16,56,512]{3,2,0,1:T(8,128)(2,1)S(1)}, u32[]{:S(2)}, u32[]{:S(2)}) async-start(bf16[1,16,56,512]{3,2,0,1:T(8,128)(2,1)} %bitcast.22), calls=%async_computation.2 | async-start | bytes 1835008 | tf_op jit(solution)/shard_map/all_to_all | solution.py:34
  112.0 25.3 %all-to-all-done.1 = bf16[1,16,56,512]{3,2,0,1:T(8,128)(2,1)S(1)} async-done(((bf16[1,16,56,512]{3,2,0,1:T(8,128)(2,1)}), bf16[1,16,56,512]{3,2,0,1:T(8,128)(2,1)S(1)}, u32[]{:S(2)}, u32[]{:S(2)}) %all-to-all-start.1) | async-done | bytes 917536 | tf_op jit(solution)/shard_map/all_to_all | solution.py:34
  137.9 1.1 fusion.17
  139.0 4.3 %all-to-all-start.2 = ((bf16[1,16,56,512]{3,2,0,1:T(8,128)(2,1)}), bf16[1,16,56,512]{3,2,0,1:T(8,128)(2,1)}, u32[]{:S(2)}, u32[]{:S(2)}) async-start(bf16[1,16,56,512]{3,2,0,1:T(8,128)(2,1)} %fusion.17), calls=%async_computation.3 | async-start | bytes 1835008 | tf_op jit(solution)/shard_map/all_to_all | solution.py:36
  143.4 1.4 pad_maximum_fusion
  144.7 25.4 %all-to-all-done.2 = bf16[1,16,56,512]{3,2,0,1:T(8,128)(2,1)} async-done(((bf16[1,16,56,512]{3,2,0,1:T(8,128)(2,1)}), bf16[1,16,56,512]{3,2,0,1:T(8,128)(2,1)}, u32[]{:S(2)}, u32[]{:S(2)}) %all-to-all-start.2) | async-done | bytes 917536 | tf_op jit(solution)/shard_map/all_to_all | solution.py:36
  170.1 1.5 copy.63
  172.2 19.9 %collective-permute-done = bf16[896,512]{0,1:T(8,128)(2,1)S(1)} collective-permute-done((bf16[896,512]{0,1:T(8,128)(2,1)S(1)}, bf16[896,512]{0,1:T(8,128)(2,1)S(1)}, u32[]{:S(2)}, u32[]{:S(2)}) %collective-permute-start) | collective-permute-done | bytes 917536 | tf_op jit(solution)/shard_map/ppermute | solution.py:109
  192.1 1.4 pad_maximum_fusion.1
  193.8 52.9 %all_to_all.26 = bf16[2,16,56,512]{3,2,0,1:T(8,128)(2,1)S(1)} all-to-all(bf16[2,16,56,512]{3,2,0,1:T(8,128)(2,1)S(1)} %copy.68), channel_id=1, replica_groups=mesh['dp'=4,'grp'=16,'ylo'=2,'xhi'=2] {'grp'}, dimensions={1} | all-to-all | bytes 3670016 | tf_op jit(solution)/shard_map/all_to_all | solution.py:34
  246.7 1.9 gather_fusion.4
  248.6 3.0 select_bitcast_fusion
  251.5 3.7 %all-to-all-start.4 = ((bf16[2,16,56,512]{3,2,0,1:T(8,128)(2,1)}), bf16[2,16,56,512]{3,2,0,1:T(8,128)(2,1)S(1)}, u32[]{:S(2)}, u32[]{:S(2)}) async-start(bf16[2,16,56,512]{3,2,0,1:T(8,128)(2,1)} %select_bitcast_fusion), calls=%async_computation.5 | async-start | bytes 3670016 | tf_op jit(solution)/shard_map/all_to_all | solution.py:36
  255.3 1.1 convert_reduce_fusion
  256.4 15.1 %all-gather.4.cloned.1.call-done = bf16[2,3584,512]{1,2,0:T(8,128)(2,1)} async-done(((bf16[2,896,512]{1,2,0:T(8,128)(2,1)}), bf16[2,3584,512]{1,2,0:T(8,128)(2,1)}) %all-gather.4.cloned.1.call-update) | async-done | bytes 7340048 | tf_op jit(solution)/shard_map/all_gather | solution.py:110
  271.5 10.3 %fusion.4 = f32[2,768,512]{1,2,0:T(8,128)S(1)} fusion(bf16[768,3712,1]{1,0,2:T(8,128)(2,1)} %bitcast.115, bf16[2,3584,512]{1,2,0:T(8,128)(2,1)} %all-gather.4.cloned.1.call-done), kind=kOutput, calls=%fused_computation.15 | convolution fusion | flops 5838471168 | bytes 16187392 | tf_op jit(solution)/shard_map/rd,kdn->krn/dot_general | solution.py:112
  282.3 0.8 fusion.34
  283.1 0.8 collective-permute-start.1
  283.9 1.3 copy.69
  285.2 13.5 %all-to-all-done.4 = bf16[2,16,56,512]{3,2,0,1:T(8,128)(2,1)S(1)} async-done(((bf16[2,16,56,512]{3,2,0,1:T(8,128)(2,1)}), bf16[2,16,56,512]{3,2,0,1:T(8,128)(2,1)S(1)}, u32[]{:S(2)}, u32[]{:S(2)}) %all-to-all-start.4) | async-done | bytes 1835040 | tf_op jit(solution)/shard_map/all_to_all | solution.py:36
  298.9 1.5 convert.5
  300.3 1.5 convert.6
  303.0 1.0 copy.67
  (57 shorter events, 4.9 us)
Async XLA Ops:
  7.2 1.2 copy-start
  7.2 94.7 %reduce-scatter.2.cloned.1.call-start = ((), (), s32[]{:S(2)}) async-start(), calls=%async_computation.6 | async-start | bytes 4587520 | tf_op jit(solution)/shard_map/reduce_scatter | solution.py:91
  12.3 0.7 copy-start.6
  12.3 1.1 copy-start.7
  12.3 243.0 %all-gather.6.cloned.1.call-start = ((), (), s32[]{:S(2)}) async-start(), calls=%async_computation.8 | async-start | bytes 8552448 | tf_op jit(solution)/shard_map/all_gather | solution.py:101
  13.6 2.1 copy-start.8
  17.7 2.8 copy-start.2
  101.9 1.5 copy-start.4
  101.9 1.7 copy-start.5
  108.3 29.0 %all-to-all-start.1 = ((bf16[1,16,56,512]{3,2,0,1:T(8,128)(2,1)}), bf16[1,16,56,512]{3,2,0,1:T(8,128)(2,1)S(1)}, u32[]{:S(2)}, u32[]{:S(2)}) async-start(bf16[1,16,56,512]{3,2,0,1:T(8,128)(2,1)} %bitcast.22), calls=%async_computation.2 | async-start | bytes 1835008 | tf_op jit(solution)/shard_map/all_to_all | solution.py:34
  137.9 5.5 %copy-start.3 = (bf16[1,896,512]{2,1,0:T(8,128)(2,1)S(1)}, bf16[1,896,512]{2,1,0:T(8,128)(2,1)}, u32[]{:S(2)}) copy-start(bf16[1,896,512]{2,1,0:T(8,128)(2,1)} %get-tuple-element.47) | copy-start | bytes 2752516
  139.0 31.1 %all-to-all-start.2 = ((bf16[1,16,56,512]{3,2,0,1:T(8,128)(2,1)}), bf16[1,16,56,512]{3,2,0,1:T(8,128)(2,1)}, u32[]{:S(2)}, u32[]{:S(2)}) async-start(bf16[1,16,56,512]{3,2,0,1:T(8,128)(2,1)} %fusion.17), calls=%async_computation.3 | async-start | bytes 1835008 | tf_op jit(solution)/shard_map/all_to_all | solution.py:36
  143.3 128.2 %all-gather.4.cloned.1.call-start = ((), (), s32[]{:S(2)}) async-start(), calls=%async_computation.7 | async-start | bytes 9175040 | tf_op jit(solution)/shard_map/all_gather | solution.py:110
  171.7 20.5 %collective-permute-start = (bf16[896,512]{0,1:T(8,128)(2,1)S(1)}, bf16[896,512]{0,1:T(8,128)(2,1)S(1)}, u32[]{:S(2)}, u32[]{:S(2)}) collective-permute-start(bf16[896,512]{0,1:T(8,128)(2,1)S(1)} %copy.63), channel_id=1, source_target_pairs={{0,1},{1,0},{2,3},{3,2},{4,5},{5,4},{6,7},{7,6},{8,9},{9,8},{10,11... | collective-permute-start | bytes 2752520 | tf_op jit(solution)/shard_map/ppermute | solution.py:109
  251.5 47.2 %all-to-all-start.4 = ((bf16[2,16,56,512]{3,2,0,1:T(8,128)(2,1)}), bf16[2,16,56,512]{3,2,0,1:T(8,128)(2,1)S(1)}, u32[]{:S(2)}, u32[]{:S(2)}) async-start(bf16[2,16,56,512]{3,2,0,1:T(8,128)(2,1)} %select_bitcast_fusion), calls=%async_computation.5 | async-start | bytes 3670016 | tf_op jit(solution)/shard_map/all_to_all | solution.py:36
  283.1 18.9 %collective-permute-start.1 = (bf16[768,256]{0,1:T(8,128)(2,1)}, bf16[768,256]{0,1:T(8,128)(2,1)S(1)}, u32[]{:S(2)}, u32[]{:S(2)}) collective-permute-start(bf16[768,256]{0,1:T(8,128)(2,1)} %get-tuple-element.52), channel_id=1, source_target_pairs={{0,1},{1,0},{2,3},{3,2},{4,5},{5,4},{6,7},{7,6},{8,9},{9,8},{10,11... | collective-permute-start | bytes 1179656 | tf_op jit(solution)/shard_map/ppermute | solution.py:119
  302.3 1.7 copy-start.1
Sparse Core Ops, SparseCore 0:
  12.4 46.2 reduce-scatter.1
  102.0 92.1 all-gather.5
  196.6 74.8 all-gather.3

commit v6 on v5

--- a/solution.py
+++ b/solution.py
@@ -37,8 +37,7 @@
     return home.reshape(layers, rows_dev, width)
 
 
-def pack_tokens(token_block, route_block, gate_block, limit, hot_count, capacity):
-    hot_index = jnp.arange(hot_count, dtype=jnp.int32)
+def pack_tokens(token_block, route_block, gate_block, limit, hot_index, capacity):
     valid = jnp.arange(token_block.shape[0], dtype=jnp.int32) < limit
     hits = (route_block[:, :, None] == hot_index[None, None, :]) & valid[:, None, None]
     named = jnp.sum(hits.astype(jnp.int32), axis=1)
@@ -81,12 +80,11 @@
     group_source = jnp.take(old_owner, holder)
 
     packed, gate_scale = pack_tokens(
-        tokens[0, 0], routing[0, 0], gates[0, 0], token_counts[0, 0], groups, capacity
+        tokens[0, 0], routing[0, 0], gates[0, 0], token_counts[0, 0], holder, capacity
     )
     scale_cols = jnp.zeros((groups, capacity, SCALE_PAD), jnp.bfloat16).at[:, :, 0].set(gate_scale)
     payload = jnp.concatenate([packed, scale_cols], axis=2)
-    to_group = jnp.take(payload, holder, axis=0)
-    by_group = lax.all_to_all(to_group, "grp", split_axis=0, concat_axis=0, tiled=True)
+    by_group = lax.all_to_all(payload, "grp", split_axis=0, concat_axis=0, tiled=True)
 
     grads = lax.psum_scatter(
         lax.dot_general(
@@ -106,8 +104,8 @@
     moments, new_weight = lax.optimization_barrier((moments, new_weight))
     moved = migrate(moments, group_source, groups)
 
-    partner_weight = lax.ppermute(new_weight, "xhi", perm=[(0, 1), (1, 0)])
-    both = lax.all_gather(jnp.stack([new_weight, partner_weight]), "dp", axis=1, tiled=True)
+    both = lax.all_gather(new_weight, ("xhi", "dp"), axis=0, tiled=True)
+    both = both.reshape(2, -1, width)
     both = jnp.pad(both, ((0, 0), (0, SCALE_PAD), (0, 0)))
     projected = jnp.einsum("rd,kdn->krn", near, both, preferred_element_type=jnp.float32)
     scaling = near[:, D].astype(jnp.float32)
@@ -116,9 +114,11 @@
         * projected[:, :, hidden_units:]
         * scaling[None, :, None]
     ).astype(jnp.bfloat16)
-    for_partner = lax.ppermute(result[1], "xhi", perm=[(0, 1), (1, 0)])
-    mine = jnp.stack([result[0], for_partner]).reshape(2, 2, groups, capacity, hidden_units)
     xhi = lax.axis_index("xhi")
+    own = lax.dynamic_index_in_dim(result, xhi, axis=0, keepdims=False)
+    other = lax.dynamic_index_in_dim(result, 1 - xhi, axis=0, keepdims=False)
+    for_partner = lax.ppermute(other, "xhi", perm=[(0, 1), (1, 0)])
+    mine = jnp.stack([own, for_partner]).reshape(2, 2, groups, capacity, hidden_units)
     flip = jnp.arange(2, dtype=jnp.int32)
     mine = jnp.take(mine, flip ^ xhi, axis=0)
     hidden = jnp.transpose(mine, (2, 1, 0, 3, 4)).reshape(1, 1, experts * capacity, hidden_units)

time: 311 us -> 303 us (0.974)
  waiting for transfers between devices: 99.3 us -> 88.9 us
  local copies, waits for them, and re-layouts: 15 us -> 22 us
    all_gather x1, waiting for transfers between devices: 15.1 us -> 30.5 us  [local(): both = lax.all_gather(new_weight, ('xhi', 'dp'), axis=0, tiled=True)]
    all_to_all x2, waiting for transfers between devices: 38.9 us -> 25.7 us  [migrate(): lax.all_to_all(chosen, 'grp', split_axis=1, concat_axis=1, tiled=True)]
    ppermute x2 -> x1, waiting for transfers between devices: 19.9 us -> 8.02 us  [local(): for_partner = lax.ppermute(other, 'xhi', perm=[(0, 1), (1, 0)])]
    reshape x0 -> x1, local copies, waits for them, and re-layouts: none -> 10.1 us  [local(): both = both.reshape(2, -1, width)]
  transfers between devices with their start and end apart: 8 -> 7, of which waited for: 5 -> 4; matrix products, arithmetic and copies ran while one was open for 13% -> 14% of each run, Pallas kernels for 0% -> 0%
where the time goes in v6:
time: 303 us; the launch traced here: 300 us
  blocking collectives  130 us (43%)
  waiting for transfers between devices  88.9 us (29%)
  local copies, waits for them, and re-layouts  22 us (7%)
  other arithmetic  15.8 us (5%)
  matrix products  15.1 us (5%)
  between operations  14.7 us (5%)
  starting transfers between devices  13.1 us (4%)
    all_to_all x1, blocking collectives, local(): lax.all_to_all(payload, 'grp', split_axis=0, concat_axis=0, tiled=True)  80.3 us
    all_to_all x1, blocking collectives, migrate(): lax.all_to_all(split, 'grp', split_axis=1, concat_axis=1, tiled=True)  50.2 us
    all_gather x1, waiting for transfers between devices, local(): both = lax.all_gather(new_weight, ('xhi', 'dp'), axis=0, tiled=True)  30.5 us
    all_to_all x2, waiting for transfers between devices, migrate(): lax.all_to_all(chosen, 'grp', split_axis=1, concat_axis=1, tiled=True)  25.7 us
    all_to_all x1, waiting for transfers between devices, migrate(): lax.all_to_all(split, 'grp', split_axis=1, concat_axis=1, tiled=True)  24.6 us
    dot_general x1, matrix products, local(): jnp.einsum('rd,kdn->krn', near, both, preferred_element_type=jnp.float32)  10.2 us
    reshape x1, local copies, waits for them, and re-layouts, local(): both = both.reshape(2, -1, width)  10.1 us
    ppermute x1, waiting for transfers between devices, local(): for_partner = lax.ppermute(other, 'xhi', perm=[(0, 1), (1, 0)])  8.02 us
  transfers between devices with their start and end apart: 7, of which 4 were waited for; matrix products, arithmetic and copies ran while one was open for 14% of the time, Pallas kernels for 0%

profile of v6, /device:TPU:4, one launch (start us, length us, event | category | flops | bytes accessed | tf_op | source)
XLA Modules:
  0.0 300.1 jit_solution(1389748277967422917)
XLA Ops:
  7.2 1.1 copy-done
  8.4 3.8 %convolution_convert_fusion = bf16[3584,512]{1,0:T(8,128)(2,1)} fusion(bf16[1,1,128,3584]{3,2,1,0:T(8,128)(2,1)S(1)} %copy-done, bf16[1,1,128,512]{3,2,1,0:T(8,128)(2,1)} %param.14), kind=kOutput, calls=%fused_computation.6 | convolution fusion | flops 471597056 | bytes 4718592 | tf_op jit(solution)/shard_map/dot_general | solution.py:90
  12.3 0.6 copy-done.9
  14.5 0.9 convolution_convert_fusion.1
  15.6 80.3 %all_to_all.25 = bf16[16,24,3712]{2,1,0:T(8,128)(2,1)} all-to-all(bf16[16,24,3712]{2,1,0:T(8,128)(2,1)S(1)} %fusion.3), channel_id=1, replica_groups=mesh['dp'=4,'grp'=16,'ylo'=2,'xhi'=2] {'grp'}, dimensions={0} | all-to-all | bytes 5701632 | tf_op jit(solution)/shard_map/all_to_all | solution.py:87
  96.0 1.5 copy-done.5
  97.7 4.7 %fusion.9 = (bf16[896,512]{1,0:T(8,128)(2,1)}, bf16[1,896,512]{2,1,0:T(8,128)(2,1)}, bf16[1,896,512]{2,1,0:T(8,128)(2,1)}) fusion(bf16[1,896,512]{2,1,0:T(8,128)(2,1)S(1)} %copy-done.7, bf16[896,512]{1,0:T(8,128)(2,1)} %reduce-scatter.2.cloned.1.call-done, f32[1,896,512]{2,1,0:T(8,128)S(1)} %copy-done.5, f32[1,896,512]{2,1,0:T(8,128)} %param.17), kind=kLoop, calls=%fused_computation.18 | loop fusion | flops 8257536 | bytes 8257536 | tf_op jit(solution)/shard_map/convert_element_type | solution.py:27
  102.3 3.8 %all-to-all-start.1 = ((bf16[1,16,56,512]{3,2,0,1:T(8,128)(2,1)}), bf16[1,16,56,512]{3,2,0,1:T(8,128)(2,1)S(1)}, u32[]{:S(2)}, u32[]{:S(2)}) async-start(bf16[1,16,56,512]{3,2,0,1:T(8,128)(2,1)} %bitcast.22), calls=%async_computation.2 | async-start | bytes 1835008 | tf_op jit(solution)/shard_map/all_to_all | solution.py:34
  106.2 0.7 gather_fusion
  106.9 24.6 %all-to-all-done.1 = bf16[1,16,56,512]{3,2,0,1:T(8,128)(2,1)S(1)} async-done(((bf16[1,16,56,512]{3,2,0,1:T(8,128)(2,1)}), bf16[1,16,56,512]{3,2,0,1:T(8,128)(2,1)S(1)}, u32[]{:S(2)}, u32[]{:S(2)}) %all-to-all-start.1) | async-done | bytes 917536 | tf_op jit(solution)/shard_map/all_to_all | solution.py:34
  131.5 0.6 gather_fusion.1
  132.1 1.1 fusion.17
  133.2 3.8 %all-to-all-start.2 = ((bf16[1,16,56,512]{3,2,0,1:T(8,128)(2,1)}), bf16[1,16,56,512]{3,2,0,1:T(8,128)(2,1)S(1)}, u32[]{:S(2)}, u32[]{:S(2)}) async-start(bf16[1,16,56,512]{3,2,0,1:T(8,128)(2,1)} %fusion.17), calls=%async_computation.3 | async-start | bytes 1835008 | tf_op jit(solution)/shard_map/all_to_all | solution.py:36
  137.0 1.6 pad_maximum_fusion
  138.7 25.7 %all-to-all-done.2 = bf16[1,16,56,512]{3,2,0,1:T(8,128)(2,1)S(1)} async-done(((bf16[1,16,56,512]{3,2,0,1:T(8,128)(2,1)}), bf16[1,16,56,512]{3,2,0,1:T(8,128)(2,1)S(1)}, u32[]{:S(2)}, u32[]{:S(2)}) %all-to-all-start.2) | async-done | bytes 917536 | tf_op jit(solution)/shard_map/all_to_all | solution.py:36
  164.3 0.9 copy-done.3
  165.5 50.2 %all_to_all.26 = bf16[2,16,56,512]{3,2,0,1:T(8,128)(2,1)S(1)} all-to-all(bf16[2,16,56,512]{3,2,0,1:T(8,128)(2,1)S(1)} %copy.57), channel_id=1, replica_groups=mesh['dp'=4,'grp'=16,'ylo'=2,'xhi'=2] {'grp'}, dimensions={1} | all-to-all | bytes 3670016 | tf_op jit(solution)/shard_map/all_to_all | solution.py:34
  215.7 1.9 gather_fusion.3
  217.6 3.0 select_bitcast_fusion
  220.6 3.7 %all-to-all-start.4 = ((bf16[2,16,56,512]{3,2,0,1:T(8,128)(2,1)}), bf16[2,16,56,512]{3,2,0,1:T(8,128)(2,1)S(1)}, u32[]{:S(2)}, u32[]{:S(2)}) async-start(bf16[2,16,56,512]{3,2,0,1:T(8,128)(2,1)} %select_bitcast_fusion), calls=%async_computation.5 | async-start | bytes 3670016 | tf_op jit(solution)/shard_map/all_to_all | solution.py:36
  224.3 1.1 convert_reduce_fusion
  225.4 30.5 %all-gather.4.cloned.1.call-done = bf16[7168,512]{1,0:T(8,128)(2,1)} async-done(((bf16[896,512]{1,0:T(8,128)(2,1)}), bf16[7168,512]{1,0:T(8,128)(2,1)}) %all-gather.4.cloned.1.call-update) | async-done | bytes 7340048 | tf_op jit(solution)/shard_map/all_gather | solution.py:107
  255.9 10.1 %copy.53 = bf16[2,3584,512]{1,2,0:T(8,128)(2,1)} copy(bf16[2,3584,512]{2,1,0:T(8,128)(2,1)} %bitcast.103) | data formatting | bytes 14680064 | tf_op jit(solution)/shard_map/reshape | solution.py:108
  266.0 10.2 %fusion.4 = f32[2,768,512]{1,2,0:T(8,128)S(1)} fusion(bf16[768,3712,1]{1,0,2:T(8,128)(2,1)} %bitcast.114, bf16[2,3584,512]{1,2,0:T(8,128)(2,1)} %copy.53), kind=kOutput, calls=%fused_computation.13 | convolution fusion | flops 5838471168 | bytes 16187392 | tf_op jit(solution)/shard_map/rd,kdn->krn/dot_general | solution.py:110
  276.8 0.9 copy.55
  277.7 1.7 collective-permute-start
  279.6 1.5 convert.5
  281.0 1.5 convert.6
  282.7 8.0 %collective-permute-done = bf16[768,256]{1,0:T(8,128)(2,1)S(1)} collective-permute-done((bf16[768,256]{1,0:T(8,128)(2,1)}, bf16[768,256]{1,0:T(8,128)(2,1)S(1)}, u32[]{:S(2)}, u32[]{:S(2)}) %collective-permute-start) | collective-permute-done | bytes 393248 | tf_op jit(solution)/shard_map/ppermute | solution.py:120
  290.8 0.6 gather_fusion.2
  291.6 1.0 copy.56
  292.6 0.9 copy.62
  (56 shorter events, 3.1 us)
Async XLA Ops:
  7.2 1.2 copy-start
  7.2 88.7 %reduce-scatter.2.cloned.1.call-start = ((), (), s32[]{:S(2)}) async-start(), calls=%async_computation.6 | async-start | bytes 4587520 | tf_op jit(solution)/shard_map/reduce_scatter | solution.py:89
  12.2 0.7 copy-start.9
  12.2 1.4 copy-start.8
  12.2 1.9 copy-start.10
  12.2 2.3 copy-start.6
  12.2 212.1 %all-gather.6.cloned.1.call-start = ((), (), s32[]{:S(2)}) async-start(), calls=%async_computation.8 | async-start | bytes 8552448 | tf_op jit(solution)/shard_map/all_gather | solution.py:99
  95.9 1.5 copy-start.5
  95.9 1.7 copy-start.7
  102.3 3.8 %copy-start.2 = (s32[16]{0:T(128)S(1)}, s32[16]{0:T(128)}, u32[]{:S(2)}) copy-start(s32[16]{0:T(128)} %param.22) | copy-start | bytes 196
  102.3 29.1 %all-to-all-start.1 = ((bf16[1,16,56,512]{3,2,0,1:T(8,128)(2,1)}), bf16[1,16,56,512]{3,2,0,1:T(8,128)(2,1)S(1)}, u32[]{:S(2)}, u32[]{:S(2)}) async-start(bf16[1,16,56,512]{3,2,0,1:T(8,128)(2,1)} %bitcast.22), calls=%async_computation.2 | async-start | bytes 1835008 | tf_op jit(solution)/shard_map/all_to_all | solution.py:34
  133.2 31.2 %all-to-all-start.2 = ((bf16[1,16,56,512]{3,2,0,1:T(8,128)(2,1)}), bf16[1,16,56,512]{3,2,0,1:T(8,128)(2,1)S(1)}, u32[]{:S(2)}, u32[]{:S(2)}) async-start(bf16[1,16,56,512]{3,2,0,1:T(8,128)(2,1)} %fusion.17), calls=%async_computation.3 | async-start | bytes 1835008 | tf_op jit(solution)/shard_map/all_to_all | solution.py:36
  137.0 118.9 %all-gather.4.cloned.1.call-start = ((), (), s32[]{:S(2)}) async-start(), calls=%async_computation.7 | async-start | bytes 8257536 | tf_op jit(solution)/shard_map/all_gather | solution.py:107
  164.3 0.9 copy-start.3
  220.6 58.9 %all-to-all-start.4 = ((bf16[2,16,56,512]{3,2,0,1:T(8,128)(2,1)}), bf16[2,16,56,512]{3,2,0,1:T(8,128)(2,1)S(1)}, u32[]{:S(2)}, u32[]{:S(2)}) async-start(bf16[2,16,56,512]{3,2,0,1:T(8,128)(2,1)} %select_bitcast_fusion), calls=%async_computation.5 | async-start | bytes 3670016 | tf_op jit(solution)/shard_map/all_to_all | solution.py:36
  277.7 13.0 %collective-permute-start = (bf16[768,256]{1,0:T(8,128)(2,1)}, bf16[768,256]{1,0:T(8,128)(2,1)S(1)}, u32[]{:S(2)}, u32[]{:S(2)}) collective-permute-start(bf16[768,256]{1,0:T(8,128)(2,1)} %bitcast.34), channel_id=1, source_target_pairs={{0,1},{1,0},{2,3},{3,2},{4,5},{5,4},{6,7},{7,6},{8,9},{9,8},{10,11... | collective-permute-start | bytes 1179656 | tf_op jit(solution)/shard_map/ppermute | solution.py:120
  291.4 1.2 copy-start.4
  291.4 2.1 copy-start.1
Sparse Core Ops, SparseCore 0:
  12.3 46.2 reduce-scatter.1
  96.1 106.9 all-gather.5
  205.5 50.3 all-gather.3

commit v7 on v6

--- a/solution.py
+++ b/solution.py
@@ -107,7 +107,9 @@
     both = lax.all_gather(new_weight, ("xhi", "dp"), axis=0, tiled=True)
     both = both.reshape(2, -1, width)
     both = jnp.pad(both, ((0, 0), (0, SCALE_PAD), (0, 0)))
-    projected = jnp.einsum("rd,kdn->krn", near, both, preferred_element_type=jnp.float32)
+    projected = jnp.stack(
+        [jnp.dot(near, both[k], preferred_element_type=jnp.float32) for k in range(2)]
+    )
     scaling = near[:, D].astype(jnp.float32)
     result = (
         jax.nn.silu(projected[:, :, :hidden_units])

time: 303 us -> 288 us (0.950)
  waiting for transfers between devices: 88.9 us -> 81.1 us
  local copies, waits for them, and re-layouts: 22 us -> 14.9 us
    reshape x1 -> x0, local copies, waits for them, and re-layouts: 10.1 us -> none  [local(): both = both.reshape(2, -1, width)]
    all_to_all x2, waiting for transfers between devices: 25.7 us -> 34.3 us  [migrate(): lax.all_to_all(chosen, 'grp', split_axis=1, concat_axis=1, tiled=True)]
    all_gather x1, waiting for transfers between devices: 30.5 us -> 22.1 us  [local(): both = lax.all_gather(new_weight, ('xhi', 'dp'), axis=0, tiled=True)]
    ppermute x1, waiting for transfers between devices: 8.02 us -> 0.01 us  [local(): for_partner = lax.ppermute(other, 'xhi', perm=[(0, 1), (1, 0)])]
    dot_general x1 -> x2, matrix products: 10.2 us -> 9.38 us  [local(): jnp.dot(near, both[k], preferred_element_type=jnp.float32)]
    unnamed x23 -> x24, local copies, waits for them, and re-layouts: 5.35 us -> 6.1 us
  transfers between devices with their start and end apart: 7 -> 7, of which waited for: 4 -> 4; matrix products, arithmetic and copies ran while one was open for 14% -> 12% of each run, Pallas kernels for 0% -> 0%
where the time goes in v7:
time: 288 us; the launch traced here: 287 us
  blocking collectives  130 us (45%)
  waiting for transfers between devices  81.1 us (28%)
  other arithmetic  18.3 us (6%)
  local copies, waits for them, and re-layouts  14.9 us (5%)
  between operations  14.7 us (5%)
  matrix products  14.2 us (5%)
  starting transfers between devices  13.2 us (5%)
    all_to_all x1, blocking collectives, local(): lax.all_to_all(payload, 'grp', split_axis=0, concat_axis=0, tiled=True)  80.3 us
    all_to_all x1, blocking collectives, migrate(): lax.all_to_all(split, 'grp', split_axis=1, concat_axis=1, tiled=True)  50.2 us
    all_to_all x2, waiting for transfers between devices, migrate(): lax.all_to_all(chosen, 'grp', split_axis=1, concat_axis=1, tiled=True)  34.3 us
    all_to_all x1, waiting for transfers between devices, migrate(): lax.all_to_all(split, 'grp', split_axis=1, concat_axis=1, tiled=True)  24.6 us
    all_gather x1, waiting for transfers between devices, local(): both = lax.all_gather(new_weight, ('xhi', 'dp'), axis=0, tiled=True)  22.1 us
    dot_general x2, matrix products, local(): jnp.dot(near, both[k], preferred_element_type=jnp.float32)  9.38 us
    all_to_all x2, starting transfers between devices, migrate(): lax.all_to_all(chosen, 'grp', split_axis=1, concat_axis=1, tiled=True)  7.55 us
    unnamed x24, local copies, waits for them, and re-layouts  6.1 us
  transfers between devices with their start and end apart: 7, of which 4 were waited for; matrix products, arithmetic and copies ran while one was open for 12% of the time, Pallas kernels for 0%

profile of v7, /device:TPU:4, one launch (start us, length us, event | category | flops | bytes accessed | tf_op | source)
XLA Modules:
  0.0 286.9 jit_solution(13511312873063780638)
XLA Ops:
  7.2 1.1 copy-done
  8.3 3.8 %convolution_convert_fusion = bf16[3584,512]{1,0:T(8,128)(2,1)} fusion(bf16[1,1,128,3584]{3,2,1,0:T(8,128)(2,1)S(1)} %copy-done, bf16[1,1,128,512]{3,2,1,0:T(8,128)(2,1)} %param.14), kind=kOutput, calls=%fused_computation.6 | convolution fusion | flops 471597056 | bytes 4718592 | tf_op jit(solution)/shard_map/dot_general | solution.py:90
  14.5 0.9 convolution_convert_fusion.1
  15.6 80.3 %all_to_all.25 = bf16[16,24,3712]{2,1,0:T(8,128)(2,1)} all-to-all(bf16[16,24,3712]{2,1,0:T(8,128)(2,1)S(1)} %fusion.7), channel_id=1, replica_groups=mesh['dp'=4,'grp'=16,'ylo'=2,'xhi'=2] {'grp'}, dimensions={0} | all-to-all | bytes 5701632 | tf_op jit(solution)/shard_map/all_to_all | solution.py:87
  95.9 1.1 copy-done.5
  97.1 5.1 %fusion.10 = (bf16[896,512]{1,0:T(8,128)(2,1)}, bf16[1,896,512]{2,1,0:T(8,128)(2,1)S(1)}, bf16[1,896,512]{2,1,0:T(8,128)(2,1)}) fusion(bf16[1,896,512]{2,1,0:T(8,128)(2,1)S(1)} %copy-done.5, bf16[896,512]{1,0:T(8,128)(2,1)} %reduce-scatter.2.cloned.1.call-done, f32[1,896,512]{2,1,0:T(8,128)} %param.16, f32[1,896,512]{2,1,0:T(8,128)} %param.17), kind=kLoop, calls=%fused_computation.23 | loop fusion | flops 8257536 | bytes 8257536 | tf_op jit(solution)/shard_map/convert_element_type | solution.py:27
  102.2 3.8 %all-to-all-start.1 = ((bf16[1,16,56,512]{3,2,0,1:T(8,128)(2,1)}), bf16[1,16,56,512]{3,2,0,1:T(8,128)(2,1)S(1)}, u32[]{:S(2)}, u32[]{:S(2)}) async-start(bf16[1,16,56,512]{3,2,0,1:T(8,128)(2,1)} %bitcast.119), calls=%async_computation.2 | async-start | bytes 1835008 | tf_op jit(solution)/shard_map/all_to_all | solution.py:34
  106.1 0.7 gather_fusion
  106.8 24.6 %all-to-all-done.1 = bf16[1,16,56,512]{3,2,0,1:T(8,128)(2,1)S(1)} async-done(((bf16[1,16,56,512]{3,2,0,1:T(8,128)(2,1)}), bf16[1,16,56,512]{3,2,0,1:T(8,128)(2,1)S(1)}, u32[]{:S(2)}, u32[]{:S(2)}) %all-to-all-start.1) | async-done | bytes 917536 | tf_op jit(solution)/shard_map/all_to_all | solution.py:34
  131.4 1.5 gather_fusion.1
  132.9 2.2 fusion.26
  135.1 3.8 %all-to-all-start.2 = ((bf16[1,16,56,512]{3,2,0,1:T(8,128)(2,1)}), bf16[1,16,56,512]{3,2,0,1:T(8,128)(2,1)S(1)}, u32[]{:S(2)}, u32[]{:S(2)}) async-start(bf16[1,16,56,512]{3,2,0,1:T(8,128)(2,1)} %fusion.26), calls=%async_computation.3 | async-start | bytes 1835008 | tf_op jit(solution)/shard_map/all_to_all | solution.py:36
  139.0 2.6 pad_maximum_fusion
  141.6 24.7 %all-to-all-done.2 = bf16[1,16,56,512]{3,2,0,1:T(8,128)(2,1)S(1)} async-done(((bf16[1,16,56,512]{3,2,0,1:T(8,128)(2,1)}), bf16[1,16,56,512]{3,2,0,1:T(8,128)(2,1)S(1)}, u32[]{:S(2)}, u32[]{:S(2)}) %all-to-all-start.2) | async-done | bytes 917536 | tf_op jit(solution)/shard_map/all_to_all | solution.py:36
  166.4 0.9 copy-done.2
  167.3 1.7 copy.50
  169.0 50.2 %all_to_all.26 = bf16[2,16,56,512]{3,2,0,1:T(8,128)(2,1)S(1)} all-to-all(bf16[2,16,56,512]{3,2,0,1:T(8,128)(2,1)S(1)} %copy.50), channel_id=1, replica_groups=mesh['dp'=4,'grp'=16,'ylo'=2,'xhi'=2] {'grp'}, dimensions={1} | all-to-all | bytes 3670016 | tf_op jit(solution)/shard_map/all_to_all | solution.py:34
  219.2 1.9 gather_fusion.3
  221.1 3.0 %select_bitcast_fusion = bf16[2,16,56,512]{3,2,0,1:T(8,128)(2,1)} fusion(bf16[16,2,56,512]{3,2,1,0:T(8,128)(2,1)} %gather_fusion.3, pred[16]{0:T(512)(128)(4,1)S(1)} %compare_and_fusion.1), kind=kLoop, calls=%fused_computation.24 | loop fusion | flops 917504 | bytes 3670032 | tf_op jit(solution)/shard_map/jit(_take)/select_n | solution.py:35
  224.1 3.7 %all-to-all-start.4 = ((bf16[2,16,56,512]{3,2,0,1:T(8,128)(2,1)}), bf16[2,16,56,512]{3,2,0,1:T(8,128)(2,1)S(1)}, u32[]{:S(2)}, u32[]{:S(2)}) async-start(bf16[2,16,56,512]{3,2,0,1:T(8,128)(2,1)} %select_bitcast_fusion), calls=%async_computation.5 | async-start | bytes 3670016 | tf_op jit(solution)/shard_map/all_to_all | solution.py:36
  227.8 0.9 slice.59
  228.9 22.1 %all-gather.4.cloned.1.call-done = bf16[7168,512]{1,0:T(8,128)(2,1)} async-done(((bf16[896,512]{1,0:T(8,128)(2,1)}), bf16[7168,512]{1,0:T(8,128)(2,1)}) %all-gather.4.cloned.1.call-update) | async-done | bytes 7340048 | tf_op jit(solution)/shard_map/all_gather | solution.py:107
  251.1 6.3 %fusion.15 = f32[1,768,512]{2,1,0:T(8,128)S(1)} fusion(bf16[768,3712]{1,0:T(8,128)(2,1)} %bitcast.125, bf16[2,3584,512]{2,1,0:T(8,128)(2,1)} %bitcast.129), kind=kOutput, calls=%fused_computation.30 | convolution fusion | flops 2919235584 | bytes 14614528 | tf_op jit(solution)/shard_map/dot_general | solution.py:111
  257.4 1.2 copy-done.8
  258.6 3.1 %fusion.18 = f32[1,768,512]{2,1,0:T(8,128)S(1)} fusion(bf16[768,3712]{1,0:T(8,128)(2,1)S(1)} %bitcast.126, bf16[2,3584,512]{2,1,0:T(8,128)(2,1)S(1)} %bitcast.130), kind=kOutput, calls=%fused_computation.31 | convolution fusion | flops 2919235584 | bytes 14614528 | tf_op jit(solution)/shard_map/dot_general | solution.py:111
  262.2 1.8 collective-permute-start
  263.9 9.5 %all-to-all-done.4 = bf16[2,16,56,512]{3,2,0,1:T(8,128)(2,1)S(1)} async-done(((bf16[2,16,56,512]{3,2,0,1:T(8,128)(2,1)}), bf16[2,16,56,512]{3,2,0,1:T(8,128)(2,1)S(1)}, u32[]{:S(2)}, u32[]{:S(2)}) %all-to-all-start.4) | async-done | bytes 1835040 | tf_op jit(solution)/shard_map/all_to_all | solution.py:36
  273.6 1.5 convert.5
  275.1 1.5 convert.6
  276.6 1.1 pad_maximum_fusion.2
  278.4 1.0 copy.49
  279.5 0.9 copy.56
  (56 shorter events, 3.7 us)
Async XLA Ops:
  7.2 1.2 copy-start
  7.2 88.7 %reduce-scatter.2.cloned.1.call-start = ((), (), s32[]{:S(2)}) async-start(), calls=%async_computation.6 | async-start | bytes 4587520 | tf_op jit(solution)/shard_map/reduce_scatter | solution.py:89
  12.2 0.7 copy-start.9
  12.2 1.4 copy-start.7
  12.2 1.9 copy-start.10
  12.2 2.3 copy-start.4
  12.2 215.6 %all-gather.6.cloned.1.call-start = ((), (), s32[]{:S(2)}) async-start(), calls=%async_computation.8 | async-start | bytes 8552448 | tf_op jit(solution)/shard_map/all_gather | solution.py:99
  95.9 1.2 copy-start.5
  102.2 3.8 %copy-start.1 = (s32[16]{0:T(128)S(1)}, s32[16]{0:T(128)}, u32[]{:S(2)}) copy-start(s32[16]{0:T(128)} %param.22) | copy-start | bytes 196
  102.2 29.1 %all-to-all-start.1 = ((bf16[1,16,56,512]{3,2,0,1:T(8,128)(2,1)}), bf16[1,16,56,512]{3,2,0,1:T(8,128)(2,1)S(1)}, u32[]{:S(2)}, u32[]{:S(2)}) async-start(bf16[1,16,56,512]{3,2,0,1:T(8,128)(2,1)} %bitcast.119), calls=%async_computation.2 | async-start | bytes 1835008 | tf_op jit(solution)/shard_map/all_to_all | solution.py:34
  135.1 31.2 %all-to-all-start.2 = ((bf16[1,16,56,512]{3,2,0,1:T(8,128)(2,1)}), bf16[1,16,56,512]{3,2,0,1:T(8,128)(2,1)S(1)}, u32[]{:S(2)}, u32[]{:S(2)}) async-start(bf16[1,16,56,512]{3,2,0,1:T(8,128)(2,1)} %fusion.26), calls=%async_computation.3 | async-start | bytes 1835008 | tf_op jit(solution)/shard_map/all_to_all | solution.py:36
  139.0 112.1 %all-gather.4.cloned.1.call-start = ((), (), s32[]{:S(2)}) async-start(), calls=%async_computation.7 | async-start | bytes 8257536 | tf_op jit(solution)/shard_map/all_gather | solution.py:107
  166.3 0.9 copy-start.2
  224.1 49.4 %all-to-all-start.4 = ((bf16[2,16,56,512]{3,2,0,1:T(8,128)(2,1)}), bf16[2,16,56,512]{3,2,0,1:T(8,128)(2,1)S(1)}, u32[]{:S(2)}, u32[]{:S(2)}) async-start(bf16[2,16,56,512]{3,2,0,1:T(8,128)(2,1)} %select_bitcast_fusion), calls=%async_computation.5 | async-start | bytes 3670016 | tf_op jit(solution)/shard_map/all_to_all | solution.py:36
  251.1 6.3 %copy-start.6 = (bf16[32,24,3712]{2,1,0:T(8,128)(2,1)S(1)}, bf16[32,24,3712]{2,1,0:T(8,128)(2,1)}, u32[]{:S(2)}) copy-start(bf16[32,24,3712]{2,1,0:T(8,128)(2,1)} %all-gather.6.cloned.1.call-done) | copy-start | bytes 17104900
  251.1 7.5 %copy-start.8 = (bf16[7168,512]{1,0:T(8,128)(2,1)S(1)}, bf16[7168,512]{1,0:T(8,128)(2,1)}, u32[]{:S(2)}) copy-start(bf16[7168,512]{1,0:T(8,128)(2,1)} %all-gather.4.cloned.1.call-done) | copy-start | bytes 22020100
  262.2 14.4 %collective-permute-start = (bf16[768,256]{1,0:T(8,128)(2,1)S(1)}, bf16[768,256]{1,0:T(8,128)(2,1)}, u32[]{:S(2)}, u32[]{:S(2)}) collective-permute-start(bf16[768,256]{1,0:T(8,128)(2,1)S(1)} %get-tuple-element.30), channel_id=1, source_target_pairs={{0,1},{1,0},{2,3},{3,2},{4,5},{5,4},{6,7},{7,6},{8,9},{9,8},{10,11... | collective-permute-start | bytes 1179656 | tf_op jit(solution)/shard_map/ppermute | solution.py:122
  278.2 1.2 copy-start.3
Sparse Core Ops, SparseCore 0:
  12.3 46.2 reduce-scatter.1
  96.1 104.6 all-gather.5
  203.2 47.8 all-gather.3

commit v8 on v7

--- a/solution.py
+++ b/solution.py
@@ -84,7 +84,13 @@
     )
     scale_cols = jnp.zeros((groups, capacity, SCALE_PAD), jnp.bfloat16).at[:, :, 0].set(gate_scale)
     payload = jnp.concatenate([packed, scale_cols], axis=2)
-    by_group = lax.all_to_all(payload, "grp", split_axis=0, concat_axis=0, tiled=True)
+    g = lax.axis_index("grp")
+    by_shift = [lax.dynamic_index_in_dim(payload, g, axis=0, keepdims=False)]
+    for k in range(1, groups):
+        send = lax.dynamic_index_in_dim(payload, (g + k) % groups, axis=0, keepdims=False)
+        pairs = [(i, (i + k) % groups) for i in range(groups)]
+        by_shift.append(lax.ppermute(send, "grp", perm=pairs))
+    by_group = jnp.stack(by_shift)
 
     grads = lax.psum_scatter(
         lax.dot_general(
@@ -123,6 +129,7 @@
     mine = jnp.stack([own, for_partner]).reshape(2, 2, groups, capacity, hidden_units)
     flip = jnp.arange(2, dtype=jnp.int32)
     mine = jnp.take(mine, flip ^ xhi, axis=0)
+    mine = jnp.take(mine, (g - jnp.arange(groups, dtype=jnp.int32)) % groups, axis=2)
     hidden = jnp.transpose(mine, (2, 1, 0, 3, 4)).reshape(1, 1, experts * capacity, hidden_units)
     return (
         hidden,

time: 288 us -> 323 us (1.12)
  blocking collectives: 130 us -> 50.2 us
  starting transfers between devices: 13.2 us -> 78.4 us
  waiting for transfers between devices: 81.1 us -> 119 us
  local copies, waits for them, and re-layouts: 14.9 us -> 21.6 us
    all_to_all x1 -> x0, blocking collectives: 80.3 us -> none  [local(): lax.all_to_all(payload, 'grp', split_axis=0, concat_axis=0, tiled=True)]
    ppermute x0 -> x15, starting transfers between devices: none -> 61.6 us  [local(): by_shift.append(lax.ppermute(send, 'grp', perm=pairs))]
    ppermute x0 -> x15, waiting for transfers between devices: none -> 26 us  [local(): by_shift.append(lax.ppermute(send, 'grp', perm=pairs))]
    all_gather x1, waiting for transfers between devices: 22.1 us -> 35 us  [local(): both = lax.all_gather(new_weight, ('xhi', 'dp'), axis=0, tiled=True)]
    all_to_all x2, waiting for transfers between devices: 34.3 us -> 25.7 us  [migrate(): lax.all_to_all(chosen, 'grp', split_axis=1, concat_axis=1, tiled=True)]
    ppermute x1, waiting for transfers between devices: 0.01 us -> 8.09 us  [local(): for_partner = lax.ppermute(other, 'xhi', perm=[(0, 1), (1, 0)])]
    unnamed x24 -> x34, local copies, waits for them, and re-layouts: 6.1 us -> 12.7 us
    all_to_all x1, starting transfers between devices: 3.78 us -> 7.48 us  [migrate(): lax.all_to_all(split, 'grp', split_axis=1, concat_axis=1, tiled=True)]
  transfers between devices with their start and end apart: 7 -> 22, of which waited for: 4 -> 10; matrix products, arithmetic and copies ran while one was open for 12% -> 13% of each run, Pallas kernels for 0% -> 0%
where the time goes in v8:
time: 323 us; the launch traced here: 321 us
  waiting for transfers between devices  119 us (37%)
  starting transfers between devices  78.4 us (24%)
  blocking collectives  50.2 us (16%)
  local copies, waits for them, and re-layouts  21.6 us (7%)
  other arithmetic  20.7 us (6%)
  matrix products  16 us (5%)
  between operations  14.9 us (5%)
    ppermute x15, starting transfers between devices, local(): by_shift.append(lax.ppermute(send, 'grp', perm=pairs))  61.6 us
    all_to_all x1, blocking collectives, migrate(): lax.all_to_all(split, 'grp', split_axis=1, concat_axis=1, tiled=True)  50.2 us
    all_gather x1, waiting for transfers between devices, local(): both = lax.all_gather(new_weight, ('xhi', 'dp'), axis=0, tiled=True)  35 us
    ppermute x15, waiting for transfers between devices, local(): by_shift.append(lax.ppermute(send, 'grp', perm=pairs))  26 us
    all_to_all x2, waiting for transfers between devices, migrate(): lax.all_to_all(chosen, 'grp', split_axis=1, concat_axis=1, tiled=True)  25.7 us
    all_to_all x1, waiting for transfers between devices, migrate(): lax.all_to_all(split, 'grp', split_axis=1, concat_axis=1, tiled=True)  24.5 us
    unnamed x34, local copies, waits for them, and re-layouts  12.7 us
    dot_general x2, matrix products, local(): jnp.dot(near, both[k], preferred_element_type=jnp.float32)  9.38 us
  transfers between devices with their start and end apart: 22, of which 10 were waited for; matrix products, arithmetic and copies ran while one was open for 13% of the time, Pallas kernels for 0%

profile of v8, /device:TPU:4, one launch (start us, length us, event | category | flops | bytes accessed | tf_op | source)
XLA Modules:
  0.0 321.0 jit_solution(1752367189216590840)
XLA Ops:
  11.8 3.6 %convolution_convert_fusion.1 = bf16[16,24,3584]{2,1,0:T(8,128)(2,1)} fusion(bf16[1,1,128,3584]{3,2,1,0:T(8,128)(2,1)} %param.18, s32[16,128]{1,0:T(8,128)S(1)} %copy.44, pred[16,128]{1,0:T(8,128)(4,1)S(1)} %compare_bitcast_fusion), kind=kOutput, calls=%fused_computation.10 | convolution fusion | flops 353796096 | bytes 3680256 | tf_op jit(solution)/shard_map/hct,td->hcd/dot_general | solution.py:48
  15.4 2.0 fusion.7
  18.5 3.2 collective-permute-start
  21.7 1.9 collective-permute-start.1
  23.6 3.0 collective-permute-start.2
  26.7 3.6 %collective-permute-start.3 = (bf16[24,3712]{1,0:T(8,128)(2,1)S(1)}, bf16[24,3712]{1,0:T(8,128)(2,1)S(1)}, u32[]{:S(2)}, u32[]{:S(2)}) collective-permute-start(bf16[24,3712]{1,0:T(8,128)(2,1)S(1)} %get-tuple-element.35), channel_id=1, source_target_pairs={{0,16},{4,20},{8,24},{12,28},{16,32},{20,36},{24,40},{28,44},{32,4... | collective-permute-start | bytes 534536 | tf_op jit(solution)/shard_map/ppermute | solution.py:92
  30.3 4.1 %collective-permute-start.4 = (bf16[24,3712]{1,0:T(8,128)(2,1)S(1)}, bf16[24,3712]{1,0:T(8,128)(2,1)S(1)}, u32[]{:S(2)}, u32[]{:S(2)}) collective-permute-start(bf16[24,3712]{1,0:T(8,128)(2,1)S(1)} %get-tuple-element.34), channel_id=1, source_target_pairs={{0,20},{4,24},{8,28},{12,32},{16,36},{20,40},{24,44},{28,48},{32,5... | collective-permute-start | bytes 534536 | tf_op jit(solution)/shard_map/ppermute | solution.py:92
  34.4 2.9 convolution_convert_fusion
  38.2 6.3 %collective-permute-start.6 = (bf16[24,3712]{1,0:T(8,128)(2,1)S(1)}, bf16[24,3712]{1,0:T(8,128)(2,1)S(1)}, u32[]{:S(2)}, u32[]{:S(2)}) collective-permute-start(bf16[24,3712]{1,0:T(8,128)(2,1)S(1)} %get-tuple-element.32), channel_id=1, source_target_pairs={{0,28},{4,32},{8,36},{12,40},{16,44},{20,48},{24,52},{28,56},{32,6... | collective-permute-start | bytes 534536 | tf_op jit(solution)/shard_map/ppermute | solution.py:92
  45.9 13.0 %collective-permute-start.8 = (bf16[24,3712]{1,0:T(8,128)(2,1)}, bf16[24,3712]{1,0:T(8,128)(2,1)S(1)}, u32[]{:S(2)}, u32[]{:S(2)}) collective-permute-start(bf16[24,3712]{1,0:T(8,128)(2,1)} %get-tuple-element.30), channel_id=1, source_target_pairs={{0,36},{4,40},{8,44},{12,48},{16,52},{20,56},{24,60},{28,0},{32,4}... | collective-permute-start | bytes 534536 | tf_op jit(solution)/shard_map/ppermute | solution.py:92
  59.5 8.5 %collective-permute-done.4 = bf16[24,3712]{1,0:T(8,128)(2,1)S(1)} collective-permute-done((bf16[24,3712]{1,0:T(8,128)(2,1)S(1)}, bf16[24,3712]{1,0:T(8,128)(2,1)S(1)}, u32[]{:S(2)}, u32[]{:S(2)}) %collective-permute-start.4) | collective-permute-done | bytes 178208 | tf_op jit(solution)/shard_map/ppermute | solution.py:92
  70.6 14.1 %collective-permute-start.10 = (bf16[24,3712]{1,0:T(8,128)(2,1)}, bf16[24,3712]{1,0:T(8,128)(2,1)S(1)}, u32[]{:S(2)}, u32[]{:S(2)}) collective-permute-start(bf16[24,3712]{1,0:T(8,128)(2,1)} %get-tuple-element.28), channel_id=1, source_target_pairs={{0,44},{4,48},{8,52},{12,56},{16,60},{20,0},{24,4},{28,8},{32,12},... | collective-permute-start | bytes 534536 | tf_op jit(solution)/shard_map/ppermute | solution.py:92
  85.4 7.9 %collective-permute-start.11 = (bf16[24,3712]{1,0:T(8,128)(2,1)S(1)}, bf16[24,3712]{1,0:T(8,128)(2,1)S(1)}, u32[]{:S(2)}, u32[]{:S(2)}) collective-permute-start(bf16[24,3712]{1,0:T(8,128)(2,1)S(1)} %get-tuple-element.27), channel_id=1, source_target_pairs={{0,48},{4,52},{8,56},{12,60},{16,0},{20,4},{24,8},{28,12},{32,16},... | collective-permute-start | bytes 534536 | tf_op jit(solution)/shard_map/ppermute | solution.py:92
  94.0 2.7 collective-permute-start.12
  100.1 5.5 %collective-permute-done.11 = bf16[24,3712]{1,0:T(8,128)(2,1)S(1)} collective-permute-done((bf16[24,3712]{1,0:T(8,128)(2,1)S(1)}, bf16[24,3712]{1,0:T(8,128)(2,1)S(1)}, u32[]{:S(2)}, u32[]{:S(2)}) %collective-permute-start.11) | collective-permute-done | bytes 178208 | tf_op jit(solution)/shard_map/ppermute | solution.py:92
  106.3 6.3 %collective-permute-done.12 = bf16[24,3712]{1,0:T(8,128)(2,1)S(1)} collective-permute-done((bf16[24,3712]{1,0:T(8,128)(2,1)S(1)}, bf16[24,3712]{1,0:T(8,128)(2,1)S(1)}, u32[]{:S(2)}, u32[]{:S(2)}) %collective-permute-start.12) | collective-permute-done | bytes 178208 | tf_op jit(solution)/shard_map/ppermute | solution.py:92
  113.3 3.1 collective-permute-done.13
  119.4 5.0 %fusion.10 = (bf16[896,512]{1,0:T(8,128)(2,1)}, bf16[1,896,512]{2,1,0:T(8,128)(2,1)}, bf16[1,896,512]{2,1,0:T(8,128)(2,1)}) fusion(bf16[1,896,512]{2,1,0:T(8,128)(2,1)} %param.15, bf16[896,512]{1,0:T(8,128)(2,1)} %reduce-scatter.2.cloned.1.call-done, f32[1,896,512]{2,1,0:T(8,128)S(1)} %copy-done.5, f32[1,896,512]{2,1,0:T(8,128)} %param.17), kind=kLoop, calls=%fused_computation.24 | loop fusion | flops 8257536 | bytes 8257536 | tf_op jit(solution)/shard_map/convert_element_type | solution.py:27
  124.4 7.5 %all-to-all-start = ((bf16[1,16,56,512]{3,2,0,1:T(8,128)(2,1)}), bf16[1,16,56,512]{3,2,0,1:T(8,128)(2,1)S(1)}, u32[]{:S(2)}, u32[]{:S(2)}) async-start(bf16[1,16,56,512]{3,2,0,1:T(8,128)(2,1)} %bitcast.53), calls=%async_computation.1 | async-start | bytes 1835008 | tf_op jit(solution)/shard_map/all_to_all | solution.py:34
  132.6 24.5 %all-to-all-done = bf16[1,16,56,512]{3,2,0,1:T(8,128)(2,1)S(1)} async-done(((bf16[1,16,56,512]{3,2,0,1:T(8,128)(2,1)}), bf16[1,16,56,512]{3,2,0,1:T(8,128)(2,1)S(1)}, u32[]{:S(2)}, u32[]{:S(2)}) %all-to-all-start) | async-done | bytes 917536 | tf_op jit(solution)/shard_map/all_to_all | solution.py:34
  158.8 3.7 %all-to-all-start.1 = ((bf16[1,16,56,512]{3,2,0,1:T(8,128)(2,1)}), bf16[1,16,56,512]{3,2,0,1:T(8,128)(2,1)S(1)}, u32[]{:S(2)}, u32[]{:S(2)}) async-start(bf16[1,16,56,512]{3,2,0,1:T(8,128)(2,1)} %fusion.26), calls=%async_computation.2 | async-start | bytes 1835008 | tf_op jit(solution)/shard_map/all_to_all | solution.py:36
  162.6 1.6 pad_maximum_fusion
  164.2 25.7 %all-to-all-done.1 = bf16[1,16,56,512]{3,2,0,1:T(8,128)(2,1)S(1)} async-done(((bf16[1,16,56,512]{3,2,0,1:T(8,128)(2,1)}), bf16[1,16,56,512]{3,2,0,1:T(8,128)(2,1)S(1)}, u32[]{:S(2)}, u32[]{:S(2)}) %all-to-all-start.1) | async-done | bytes 917536 | tf_op jit(solution)/shard_map/all_to_all | solution.py:36
  191.0 50.2 %all_to_all.20 = bf16[2,16,56,512]{3,2,0,1:T(8,128)(2,1)S(1)} all-to-all(bf16[2,16,56,512]{3,2,0,1:T(8,128)(2,1)S(1)} %copy.50), channel_id=1, replica_groups=mesh['dp'=4,'grp'=16,'ylo'=2,'xhi'=2] {'grp'}, dimensions={1} | all-to-all | bytes 3670016 | tf_op jit(solution)/shard_map/all_to_all | solution.py:34
  241.2 1.9 gather_fusion.4
  243.1 3.0 select_bitcast_fusion
  246.1 3.7 %all-to-all-start.3 = ((bf16[2,16,56,512]{3,2,0,1:T(8,128)(2,1)}), bf16[2,16,56,512]{3,2,0,1:T(8,128)(2,1)S(1)}, u32[]{:S(2)}, u32[]{:S(2)}) async-start(bf16[2,16,56,512]{3,2,0,1:T(8,128)(2,1)} %select_bitcast_fusion), calls=%async_computation.4 | async-start | bytes 3670016 | tf_op jit(solution)/shard_map/all_to_all | solution.py:36
  251.0 35.0 %all-gather.4.cloned.1.call-done = bf16[7168,512]{1,0:T(8,128)(2,1)} async-done(((bf16[896,512]{1,0:T(8,128)(2,1)}), bf16[7168,512]{1,0:T(8,128)(2,1)}) %all-gather.4.cloned.1.call-update) | async-done | bytes 7340048 | tf_op jit(solution)/shard_map/all_gather | solution.py:113
  286.0 6.3 %fusion.18 = f32[1,768,512]{2,1,0:T(8,128)S(1)} fusion(bf16[768,3712]{1,0:T(8,128)(2,1)} %bitcast.186, bf16[2,3584,512]{2,1,0:T(8,128)(2,1)} %bitcast.190), kind=kOutput, calls=%fused_computation.32 | convolution fusion | flops 2919235584 | bytes 14614528 | tf_op jit(solution)/shard_map/dot_general | solution.py:117
  293.5 3.1 fusion.15
  297.1 1.8 collective-permute-start.15
  301.9 8.1 %collective-permute-done.15 = bf16[768,256]{1,0:T(8,128)(2,1)} collective-permute-done((bf16[768,256]{1,0:T(8,128)(2,1)S(1)}, bf16[768,256]{1,0:T(8,128)(2,1)}, u32[]{:S(2)}, u32[]{:S(2)}) %collective-permute-start.15) | collective-permute-done | bytes 393248 | tf_op jit(solution)/shard_map/ppermute | solution.py:128
  (101 shorter events, 33.5 us)
Async XLA Ops:
  7.2 27.2 %copy-start = (bf16[1,1,128,3584]{3,2,1,0:T(8,128)(2,1)S(1)}, bf16[1,1,128,3584]{3,2,1,0:T(8,128)(2,1)}, u32[]{:S(2)}) copy-start(bf16[1,1,128,3584]{3,2,1,0:T(8,128)(2,1)} %param.13) | copy-start | bytes 2752516
  7.2 112.2 %reduce-scatter.2.cloned.1.call-start = ((), (), s32[]{:S(2)}) async-start(), calls=%async_computation.5 | async-start | bytes 4587520 | tf_op jit(solution)/shard_map/reduce_scatter | solution.py:95
  17.3 17.0 %copy-start.6 = (bf16[1,1,128,512]{3,2,1,0:T(8,128)(2,1)S(1)}, bf16[1,1,128,512]{3,2,1,0:T(8,128)(2,1)}, u32[]{:S(2)}) copy-start(bf16[1,1,128,512]{3,2,1,0:T(8,128)(2,1)} %param.14) | copy-start | bytes 393220
  18.5 18.8 %collective-permute-start = (bf16[24,3712]{1,0:T(8,128)(2,1)}, bf16[24,3712]{1,0:T(8,128)(2,1)S(1)}, u32[]{:S(2)}, u32[]{:S(2)}) collective-permute-start(bf16[24,3712]{1,0:T(8,128)(2,1)} %get-tuple-element.38), channel_id=1, source_target_pairs={{0,4},{4,8},{8,12},{12,16},{16,20},{20,24},{24,28},{28,32},{32,36}... | collective-permute-start | bytes 534536 | tf_op jit(solution)/shard_map/ppermute | solution.py:92
  21.7 16.5 %collective-permute-start.1 = (bf16[24,3712]{1,0:T(8,128)(2,1)}, bf16[24,3712]{1,0:T(8,128)(2,1)S(1)}, u32[]{:S(2)}, u32[]{:S(2)}) collective-permute-start(bf16[24,3712]{1,0:T(8,128)(2,1)} %get-tuple-element.37), channel_id=1, source_target_pairs={{0,8},{4,12},{8,16},{12,20},{16,24},{20,28},{24,32},{28,36},{32,40... | collective-permute-start | bytes 534536 | tf_op jit(solution)/shard_map/ppermute | solution.py:92
  23.6 21.6 %collective-permute-start.2 = (bf16[24,3712]{1,0:T(8,128)(2,1)}, bf16[24,3712]{1,0:T(8,128)(2,1)S(1)}, u32[]{:S(2)}, u32[]{:S(2)}) collective-permute-start(bf16[24,3712]{1,0:T(8,128)(2,1)} %get-tuple-element.36), channel_id=1, source_target_pairs={{0,12},{4,16},{8,20},{12,24},{16,28},{20,32},{24,36},{28,40},{32,4... | collective-permute-start | bytes 534536 | tf_op jit(solution)/shard_map/ppermute | solution.py:92
  26.7 19.2 %collective-permute-start.3 = (bf16[24,3712]{1,0:T(8,128)(2,1)S(1)}, bf16[24,3712]{1,0:T(8,128)(2,1)S(1)}, u32[]{:S(2)}, u32[]{:S(2)}) collective-permute-start(bf16[24,3712]{1,0:T(8,128)(2,1)S(1)} %get-tuple-element.35), channel_id=1, source_target_pairs={{0,16},{4,20},{8,24},{12,28},{16,32},{20,36},{24,40},{28,44},{32,4... | collective-permute-start | bytes 534536 | tf_op jit(solution)/shard_map/ppermute | solution.py:92
  30.3 37.7 %collective-permute-start.4 = (bf16[24,3712]{1,0:T(8,128)(2,1)S(1)}, bf16[24,3712]{1,0:T(8,128)(2,1)S(1)}, u32[]{:S(2)}, u32[]{:S(2)}) collective-permute-start(bf16[24,3712]{1,0:T(8,128)(2,1)S(1)} %get-tuple-element.34), channel_id=1, source_target_pairs={{0,20},{4,24},{8,28},{12,32},{16,36},{20,40},{24,44},{28,48},{32,5... | collective-permute-start | bytes 534536 | tf_op jit(solution)/shard_map/ppermute | solution.py:92
  37.3 212.6 %all-gather.6.cloned.1.call-start = ((), (), s32[]{:S(2)}) async-start(), calls=%async_computation.7 | async-start | bytes 8552448 | tf_op jit(solution)/shard_map/all_gather | solution.py:105
  37.4 33.2 %collective-permute-start.5 = (bf16[24,3712]{1,0:T(8,128)(2,1)S(1)}, bf16[24,3712]{1,0:T(8,128)(2,1)S(1)}, u32[]{:S(2)}, u32[]{:S(2)}) collective-permute-start(bf16[24,3712]{1,0:T(8,128)(2,1)S(1)} %get-tuple-element.33), channel_id=1, source_target_pairs={{0,24},{4,28},{8,32},{12,36},{16,40},{20,44},{24,48},{28,52},{32,5... | collective-permute-start | bytes 534536 | tf_op jit(solution)/shard_map/ppermute | solution.py:92
  38.2 47.1 %collective-permute-start.6 = (bf16[24,3712]{1,0:T(8,128)(2,1)S(1)}, bf16[24,3712]{1,0:T(8,128)(2,1)S(1)}, u32[]{:S(2)}, u32[]{:S(2)}) collective-permute-start(bf16[24,3712]{1,0:T(8,128)(2,1)S(1)} %get-tuple-element.32), channel_id=1, source_target_pairs={{0,28},{4,32},{8,36},{12,40},{16,44},{20,48},{24,52},{28,56},{32,6... | collective-permute-start | bytes 534536 | tf_op jit(solution)/shard_map/ppermute | solution.py:92
  45.2 48.7 %collective-permute-start.7 = (bf16[24,3712]{1,0:T(8,128)(2,1)S(1)}, bf16[24,3712]{1,0:T(8,128)(2,1)S(1)}, u32[]{:S(2)}, u32[]{:S(2)}) collective-permute-start(bf16[24,3712]{1,0:T(8,128)(2,1)S(1)} %get-tuple-element.31), channel_id=1, source_target_pairs={{0,32},{4,36},{8,40},{12,44},{16,48},{20,52},{24,56},{28,60},{32,0... | collective-permute-start | bytes 534536 | tf_op jit(solution)/shard_map/ppermute | solution.py:92
  45.9 51.5 %collective-permute-start.8 = (bf16[24,3712]{1,0:T(8,128)(2,1)}, bf16[24,3712]{1,0:T(8,128)(2,1)S(1)}, u32[]{:S(2)}, u32[]{:S(2)}) collective-permute-start(bf16[24,3712]{1,0:T(8,128)(2,1)} %get-tuple-element.30), channel_id=1, source_target_pairs={{0,36},{4,40},{8,44},{12,48},{16,52},{20,56},{24,60},{28,0},{32,4}... | collective-permute-start | bytes 534536 | tf_op jit(solution)/shard_map/ppermute | solution.py:92
  68.0 30.0 %collective-permute-start.9 = (bf16[24,3712]{1,0:T(8,128)(2,1)}, bf16[24,3712]{1,0:T(8,128)(2,1)S(1)}, u32[]{:S(2)}, u32[]{:S(2)}) collective-permute-start(bf16[24,3712]{1,0:T(8,128)(2,1)} %get-tuple-element.29), channel_id=1, source_target_pairs={{0,40},{4,44},{8,48},{12,52},{16,56},{20,60},{24,0},{28,4},{32,8},... | collective-permute-start | bytes 534536 | tf_op jit(solution)/shard_map/ppermute | solution.py:92
  70.6 28.8 %collective-permute-start.10 = (bf16[24,3712]{1,0:T(8,128)(2,1)}, bf16[24,3712]{1,0:T(8,128)(2,1)S(1)}, u32[]{:S(2)}, u32[]{:S(2)}) collective-permute-start(bf16[24,3712]{1,0:T(8,128)(2,1)} %get-tuple-element.28), channel_id=1, source_target_pairs={{0,44},{4,48},{8,52},{12,56},{16,60},{20,0},{24,4},{28,8},{32,12},... | collective-permute-start | bytes 534536 | tf_op jit(solution)/shard_map/ppermute | solution.py:92
  85.4 20.3 %collective-permute-start.11 = (bf16[24,3712]{1,0:T(8,128)(2,1)S(1)}, bf16[24,3712]{1,0:T(8,128)(2,1)S(1)}, u32[]{:S(2)}, u32[]{:S(2)}) collective-permute-start(bf16[24,3712]{1,0:T(8,128)(2,1)S(1)} %get-tuple-element.27), channel_id=1, source_target_pairs={{0,48},{4,52},{8,56},{12,60},{16,0},{20,4},{24,8},{28,12},{32,16},... | collective-permute-start | bytes 534536 | tf_op jit(solution)/shard_map/ppermute | solution.py:92
  94.0 25.4 %copy-start.5 = (f32[1,896,512]{2,1,0:T(8,128)S(1)}, f32[1,896,512]{2,1,0:T(8,128)}, u32[]{:S(2)}) copy-start(f32[1,896,512]{2,1,0:T(8,128)} %param.16) | copy-start | bytes 5505028
  94.0 18.7 %collective-permute-start.12 = (bf16[24,3712]{1,0:T(8,128)(2,1)S(1)}, bf16[24,3712]{1,0:T(8,128)(2,1)S(1)}, u32[]{:S(2)}, u32[]{:S(2)}) collective-permute-start(bf16[24,3712]{1,0:T(8,128)(2,1)S(1)} %get-tuple-element.26), channel_id=1, source_target_pairs={{0,52},{4,56},{8,60},{12,0},{16,4},{20,8},{24,12},{28,16},{32,20},... | collective-permute-start | bytes 534536 | tf_op jit(solution)/shard_map/ppermute | solution.py:92
  97.4 19.1 %collective-permute-start.13 = (bf16[24,3712]{1,0:T(8,128)(2,1)S(1)}, bf16[24,3712]{1,0:T(8,128)(2,1)S(1)}, u32[]{:S(2)}, u32[]{:S(2)}) collective-permute-start(bf16[24,3712]{1,0:T(8,128)(2,1)S(1)} %get-tuple-element.25), channel_id=1, source_target_pairs={{0,56},{4,60},{8,0},{12,4},{16,8},{20,12},{24,16},{28,20},{32,24},... | collective-permute-start | bytes 534536 | tf_op jit(solution)/shard_map/ppermute | solution.py:92
  98.0 20.7 %collective-permute-start.14 = (bf16[24,3712]{1,0:T(8,128)(2,1)S(1)}, bf16[24,3712]{1,0:T(8,128)(2,1)S(1)}, u32[]{:S(2)}, u32[]{:S(2)}) collective-permute-start(bf16[24,3712]{1,0:T(8,128)(2,1)S(1)} %get-tuple-element.24), channel_id=1, source_target_pairs={{0,60},{4,0},{8,4},{12,8},{16,12},{20,16},{24,20},{28,24},{32,28},... | collective-permute-start | bytes 534536 | tf_op jit(solution)/shard_map/ppermute | solution.py:92
  119.4 12.5 %copy-start.2 = (s32[16]{0:T(128)S(1)}, s32[16]{0:T(128)}, u32[]{:S(2)}) copy-start(s32[16]{0:T(128)} %param.22) | copy-start | bytes 196
  124.4 32.7 %all-to-all-start = ((bf16[1,16,56,512]{3,2,0,1:T(8,128)(2,1)}), bf16[1,16,56,512]{3,2,0,1:T(8,128)(2,1)S(1)}, u32[]{:S(2)}, u32[]{:S(2)}) async-start(bf16[1,16,56,512]{3,2,0,1:T(8,128)(2,1)} %bitcast.53), calls=%async_computation.1 | async-start | bytes 1835008 | tf_op jit(solution)/shard_map/all_to_all | solution.py:34
  158.8 31.1 %all-to-all-start.1 = ((bf16[1,16,56,512]{3,2,0,1:T(8,128)(2,1)}), bf16[1,16,56,512]{3,2,0,1:T(8,128)(2,1)S(1)}, u32[]{:S(2)}, u32[]{:S(2)}) async-start(bf16[1,16,56,512]{3,2,0,1:T(8,128)(2,1)} %fusion.26), calls=%async_computation.2 | async-start | bytes 1835008 | tf_op jit(solution)/shard_map/all_to_all | solution.py:36
  162.5 123.5 %all-gather.4.cloned.1.call-start = ((), (), s32[]{:S(2)}) async-start(), calls=%async_computation.6 | async-start | bytes 8257536 | tf_op jit(solution)/shard_map/all_gather | solution.py:113
  189.9 0.9 copy-start.3
  246.1 52.8 %all-to-all-start.3 = ((bf16[2,16,56,512]{3,2,0,1:T(8,128)(2,1)}), bf16[2,16,56,512]{3,2,0,1:T(8,128)(2,1)S(1)}, u32[]{:S(2)}, u32[]{:S(2)}) async-start(bf16[2,16,56,512]{3,2,0,1:T(8,128)(2,1)} %select_bitcast_fusion), calls=%async_computation.4 | async-start | bytes 3670016 | tf_op jit(solution)/shard_map/all_to_all | solution.py:36
  286.0 6.3 %copy-start.7 = (bf16[32,24,3712]{2,1,0:T(8,128)(2,1)S(1)}, bf16[32,24,3712]{2,1,0:T(8,128)(2,1)}, u32[]{:S(2)}) copy-start(bf16[32,24,3712]{2,1,0:T(8,128)(2,1)} %all-gather.6.cloned.1.call-done) | copy-start | bytes 17104900
  286.0 7.5 %copy-start.8 = (bf16[7168,512]{1,0:T(8,128)(2,1)S(1)}, bf16[7168,512]{1,0:T(8,128)(2,1)}, u32[]{:S(2)}) copy-start(bf16[7168,512]{1,0:T(8,128)(2,1)} %all-gather.4.cloned.1.call-done) | copy-start | bytes 22020100
  297.1 13.0 %collective-permute-start.15 = (bf16[768,256]{1,0:T(8,128)(2,1)S(1)}, bf16[768,256]{1,0:T(8,128)(2,1)}, u32[]{:S(2)}, u32[]{:S(2)}) collective-permute-start(bf16[768,256]{1,0:T(8,128)(2,1)S(1)} %get-tuple-element.46), channel_id=1, source_target_pairs={{0,1},{1,0},{2,3},{3,2},{4,5},{5,4},{6,7},{7,6},{8,9},{9,8},{10,11... | collective-permute-start | bytes 1179656 | tf_op jit(solution)/shard_map/ppermute | solution.py:128
  311.7 1.9 copy-start.4
  311.9 2.6 copy-start.1
Sparse Core Ops, SparseCore 0:
  37.4 40.9 reduce-scatter.1
  119.5 115.2 all-gather.5
  237.3 48.6 all-gather.3

commit v9 on v7

--- a/solution.py
+++ b/solution.py
@@ -6,7 +6,6 @@
 
 D = 3584
 GRP = 4
-SCALE_PAD = 128
 
 
 beta_first = 0.9
@@ -32,7 +31,7 @@
     piece_rows = rows_dev // groups
     split = state.reshape(layers, groups, piece_rows, width)
     spread = lax.all_to_all(split, "grp", split_axis=1, concat_axis=1, tiled=True)
-    chosen = jnp.take(spread, group_source, axis=1)
+    chosen = jnp.take(spread, group_source, axis=1, mode="clip", unique_indices=True)
     home = lax.all_to_all(chosen, "grp", split_axis=1, concat_axis=1, tiled=True)
     return home.reshape(layers, rows_dev, width)
 
@@ -82,9 +81,8 @@
     packed, gate_scale = pack_tokens(
         tokens[0, 0], routing[0, 0], gates[0, 0], token_counts[0, 0], holder, capacity
     )
-    scale_cols = jnp.zeros((groups, capacity, SCALE_PAD), jnp.bfloat16).at[:, :, 0].set(gate_scale)
-    payload = jnp.concatenate([packed, scale_cols], axis=2)
-    by_group = lax.all_to_all(payload, "grp", split_axis=0, concat_axis=0, tiled=True)
+    by_group = lax.all_to_all(packed, "grp", split_axis=0, concat_axis=0, tiled=True)
+    all_scales = lax.all_gather(gate_scale, ("grp", "ylo", "xhi"), axis=0, tiled=False)
 
     grads = lax.psum_scatter(
         lax.dot_general(
@@ -97,7 +95,7 @@
     by_group, grads = lax.optimization_barrier((by_group, grads))
     grads = grads.astype(jnp.float32)
     near = lax.all_gather(by_group, "ylo", axis=0, tiled=False)
-    near = near.reshape(2 * groups * capacity, D + SCALE_PAD)
+    near = near.reshape(2 * groups * capacity, D)
     stepped, first_next, second_next = adamw(weights[0], first_moment[0], second_moment[0], grads)
     new_weight = migrate(stepped[None], group_source, groups)[0]
     moments = jnp.stack([first_next.astype(jnp.bfloat16), second_next.astype(jnp.bfloat16)])
@@ -106,17 +104,20 @@
 
     both = lax.all_gather(new_weight, ("xhi", "dp"), axis=0, tiled=True)
     both = both.reshape(2, -1, width)
-    both = jnp.pad(both, ((0, 0), (0, SCALE_PAD), (0, 0)))
     projected = jnp.stack(
         [jnp.dot(near, both[k], preferred_element_type=jnp.float32) for k in range(2)]
     )
-    scaling = near[:, D].astype(jnp.float32)
+    g = lax.axis_index("grp")
+    xhi = lax.axis_index("xhi")
+    scales = all_scales.reshape(groups, 2, 2, groups, capacity)
+    scales = lax.dynamic_index_in_dim(scales, xhi, axis=2, keepdims=False)
+    scales = lax.dynamic_index_in_dim(scales, g, axis=2, keepdims=False)
+    scaling = jnp.transpose(scales, (1, 0, 2)).reshape(-1).astype(jnp.float32)
     result = (
         jax.nn.silu(projected[:, :, :hidden_units])
         * projected[:, :, hidden_units:]
         * scaling[None, :, None]
     ).astype(jnp.bfloat16)
-    xhi = lax.axis_index("xhi")
     own = lax.dynamic_index_in_dim(result, xhi, axis=0, keepdims=False)
     other = lax.dynamic_index_in_dim(result, 1 - xhi, axis=0, keepdims=False)
     for_partner = lax.ppermute(other, "xhi", perm=[(0, 1), (1, 0)])

time: 288 us -> 464 us (1.61)
  blocking collectives: 130 us -> 291 us
  waiting for transfers between devices: 81.1 us -> 100 us
  other arithmetic: 18.3 us -> 12.8 us
    all_gather x0 -> x1, blocking collectives: none -> 212 us  [local(): lax.all_gather(gate_scale, ('grp', 'ylo', 'xhi'), axis=0, tiled=False)]
    all_to_all x2 -> x1, blocking collectives: 130 us -> 78.4 us  [local(): lax.all_to_all(packed, 'grp', split_axis=0, concat_axis=0, tiled=True)]
    all_to_all x1 -> x2, waiting for transfers between devices: 24.6 us -> 70.3 us  [migrate(): lax.all_to_all(split, 'grp', split_axis=1, concat_axis=1, tiled=True)]
    all_gather x1, waiting for transfers between devices: 22.1 us -> 0.02 us  [local(): both = lax.all_gather(new_weight, ('xhi', 'dp'), axis=0, tiled=True)]
    all_to_all x2, waiting for transfers between devices: 34.3 us -> 24.7 us  [migrate(): lax.all_to_all(chosen, 'grp', split_axis=1, concat_axis=1, tiled=True)]
    ppermute x1, waiting for transfers between devices: 0.01 us -> 5.35 us  [local(): for_partner = lax.ppermute(other, 'xhi', perm=[(0, 1), (1, 0)])]
    select_n x3 -> x0, other arithmetic: 5.23 us -> none  [migrate(): chosen = jnp.take(spread, group_source, axis=1)]
  transfers between devices with their start and end apart: 7 -> 8, of which waited for: 4 -> 4; matrix products, arithmetic and copies ran while one was open for 12% -> 6% of each run, Pallas kernels for 0% -> 0%
where the time goes in v9:
time: 464 us; the launch traced here: 463 us
  blocking collectives  291 us (63%)
  waiting for transfers between devices  100 us (22%)
  starting transfers between devices  16.2 us (3%)
  between operations  14.7 us (3%)
  local copies, waits for them, and re-layouts  14.4 us (3%)
  matrix products  14.1 us (3%)
  other arithmetic  12.8 us (3%)
    all_gather x1, blocking collectives, local(): lax.all_gather(gate_scale, ('grp', 'ylo', 'xhi'), axis=0, tiled=False)  212 us
    all_to_all x1, blocking collectives, local(): lax.all_to_all(packed, 'grp', split_axis=0, concat_axis=0, tiled=True)  78.4 us
    all_to_all x2, waiting for transfers between devices, migrate(): lax.all_to_all(split, 'grp', split_axis=1, concat_axis=1, tiled=True)  70.3 us
    all_to_all x2, waiting for transfers between devices, migrate(): lax.all_to_all(chosen, 'grp', split_axis=1, concat_axis=1, tiled=True)  24.7 us
  transfers between devices with their start and end apart: 8, of which 4 were waited for; matrix products, arithmetic and copies ran while one was open for 6% of the time, Pallas kernels for 0%

profile of v9, /device:TPU:4, one launch (start us, length us, event | category | flops | bytes accessed | tf_op | source)
XLA Modules:
  0.0 463.3 jit_solution(14671783653669876661)
XLA Ops:
  7.2 1.1 copy-done
  8.3 3.8 convolution_convert_fusion
  13.6 0.9 convolution_convert_fusion.1
  14.4 78.4 %all_to_all.25 = bf16[16,24,3584]{2,1,0:T(8,128)(2,1)} all-to-all(bf16[16,24,3584]{2,1,0:T(8,128)(2,1)S(1)} %convolution_convert_fusion.1), channel_id=1, replica_groups=mesh['dp'=4,'grp'=16,'ylo'=2,'xhi'=2] {'grp'}, dimensions={0} | all-to-all | bytes 5505024 | tf_op jit(solution)/shard_map/all_to_all | solution.py:84
  92.9 1.1 copy-done.5
  94.0 5.1 %fusion.6 = (bf16[896,512]{1,0:T(8,128)(2,1)}, bf16[1,896,512]{2,1,0:T(8,128)(2,1)S(1)}, bf16[1,896,512]{2,1,0:T(8,128)(2,1)}) fusion(bf16[1,896,512]{2,1,0:T(8,128)(2,1)S(1)} %copy-done.5, bf16[896,512]{1,0:T(8,128)(2,1)} %reduce-scatter.2.cloned.1.call-done, f32[1,896,512]{2,1,0:T(8,128)} %param.14, f32[1,896,512]{2,1,0:T(8,128)} %param.15), kind=kLoop, calls=%fused_computation.18 | loop fusion | flops 8257536 | bytes 8257536 | tf_op jit(solution)/shard_map/convert_element_type | solution.py:26
  99.2 3.8 all-to-all-start.1
  103.0 0.7 gather_fusion
  103.7 24.4 %all-to-all-done.1 = bf16[1,16,56,512]{3,2,0,1:T(8,128)(2,1)S(1)} async-done(((bf16[1,16,56,512]{3,2,0,1:T(8,128)(2,1)}), bf16[1,16,56,512]{3,2,0,1:T(8,128)(2,1)S(1)}, u32[]{:S(2)}, u32[]{:S(2)}) %all-to-all-start.1) | async-done | bytes 917536 | tf_op jit(solution)/shard_map/all_to_all | solution.py:33
  128.1 1.5 gather_fusion.1
  129.6 3.8 all-to-all-start.2
  133.4 2.6 pad_maximum_fusion
  136.0 24.7 %all-to-all-done.2 = bf16[1,16,56,512]{3,2,0,1:T(8,128)(2,1)S(1)} async-done(((bf16[1,16,56,512]{3,2,0,1:T(8,128)(2,1)}), bf16[1,16,56,512]{3,2,0,1:T(8,128)(2,1)S(1)}, u32[]{:S(2)}, u32[]{:S(2)}) %all-to-all-start.2) | async-done | bytes 917536 | tf_op jit(solution)/shard_map/all_to_all | solution.py:35
  160.7 0.9 copy-done.2
  161.6 3.0 copy.62
  164.6 3.7 all-to-all-start.3
  168.3 45.9 %all-to-all-done.3 = bf16[2,16,56,512]{3,2,0,1:T(8,128)(2,1)S(1)} async-done(((bf16[2,16,56,512]{3,2,0,1:T(8,128)(2,1)}), bf16[2,16,56,512]{3,2,0,1:T(8,128)(2,1)S(1)}, u32[]{:S(2)}, u32[]{:S(2)}) %all-to-all-start.3) | async-done | bytes 1835040 | tf_op jit(solution)/shard_map/all_to_all | solution.py:33
  214.2 1.9 gather_fusion.3
  216.1 3.8 all-to-all-start.4
  220.2 212.2 %all-gather.1 = bf16[1024,24]{1,0:T(8,128)(2,1)S(1)} all-gather(bf16[16,24]{1,0:T(8,128)(2,1)S(1)} %convert_element_type.95), channel_id=3, replica_groups=mesh['dp'=4,'grp'=16,'ylo'=2,'xhi'=2] {'grp','ylo','xhi'}, dimensions={0}, use_global_device_ids=true | all-gather | bytes 49920 | tf_op jit(solution)/shard_map/all_gather | solution.py:85
  432.7 6.2 %fusion.11 = f32[1,768,512]{2,1,0:T(8,128)S(1)} fusion(bf16[768,3584]{1,0:T(8,128)(2,1)} %bitcast.119, bf16[7168,512]{1,0:T(8,128)(2,1)} %all-gather.5.cloned.1.call-done), kind=kOutput, calls=%fused_computation.24 | convolution fusion | flops 2818572288 | bytes 10747904 | tf_op jit(solution)/shard_map/dot_general | solution.py:108
  438.9 1.1 copy-done.8
  440.0 3.0 fusion.14
  443.0 0.4 fusion.10
  443.5 1.0 collective-permute-start
  444.6 1.5 convert.8
  446.1 1.5 convert.9
  447.6 5.3 %collective-permute-done = bf16[768,256]{1,0:T(8,128)(2,1)} collective-permute-done((bf16[768,256]{1,0:T(8,128)(2,1)S(1)}, bf16[768,256]{1,0:T(8,128)(2,1)}, u32[]{:S(2)}, u32[]{:S(2)}) %collective-permute-start) | collective-permute-done | bytes 393248 | tf_op jit(solution)/shard_map/ppermute | solution.py:123
  453.0 1.1 pad_maximum_fusion.2
  454.0 0.6 gather_fusion.2
  454.8 1.0 copy.61
  455.9 0.9 copy.73
  (53 shorter events, 1.6 us)
Async XLA Ops:
  7.2 1.2 copy-start
  7.2 85.7 %reduce-scatter.2.cloned.1.call-start = ((), (), s32[]{:S(2)}) async-start(), calls=%async_computation.6 | async-start | bytes 4587520 | tf_op jit(solution)/shard_map/reduce_scatter | solution.py:87
  12.2 0.8 copy-start.9
  12.2 0.9 copy-start.6
  12.2 1.4 copy-start.4
  12.2 420.4 %all-gather.7.cloned.1.call-start = ((), (), s32[]{:S(2)}) async-start(), calls=%async_computation.8 | async-start | bytes 8257536 | tf_op jit(solution)/shard_map/all_gather | solution.py:97
  92.8 1.2 copy-start.5
  99.2 3.8 copy-start.1
  99.2 28.9 %all-to-all-start.1 = ((bf16[1,16,56,512]{3,2,0,1:T(8,128)(2,1)}), bf16[1,16,56,512]{3,2,0,1:T(8,128)(2,1)S(1)}, u32[]{:S(2)}, u32[]{:S(2)}) async-start(bf16[1,16,56,512]{3,2,0,1:T(8,128)(2,1)} %bitcast.111), calls=%async_computation.2 | async-start | bytes 1835008 | tf_op jit(solution)/shard_map/all_to_all | solution.py:33
  129.6 31.1 %all-to-all-start.2 = ((bf16[1,16,56,512]{3,2,0,1:T(8,128)(2,1)}), bf16[1,16,56,512]{3,2,0,1:T(8,128)(2,1)S(1)}, u32[]{:S(2)}, u32[]{:S(2)}) async-start(bf16[1,16,56,512]{3,2,0,1:T(8,128)(2,1)} %bitcast.22), calls=%async_computation.3 | async-start | bytes 1835008 | tf_op jit(solution)/shard_map/all_to_all | solution.py:35
  133.4 299.3 %all-gather.5.cloned.1.call-start = ((), (), s32[]{:S(2)}) async-start(), calls=%async_computation.7 | async-start | bytes 8257536 | tf_op jit(solution)/shard_map/all_gather | solution.py:105
  160.7 0.9 copy-start.2
  164.6 49.6 %all-to-all-start.3 = ((bf16[2,16,56,512]{3,2,0,1:T(8,128)(2,1)}), bf16[2,16,56,512]{3,2,0,1:T(8,128)(2,1)S(1)}, u32[]{:S(2)}, u32[]{:S(2)}) async-start(bf16[2,16,56,512]{3,2,0,1:T(8,128)(2,1)} %copy.62), calls=%async_computation.4 | async-start | bytes 3670016 | tf_op jit(solution)/shard_map/all_to_all | solution.py:33
  216.1 3.9 copy-start.10
  216.1 228.4 %all-to-all-start.4 = ((bf16[2,16,56,512]{3,2,0,1:T(8,128)(2,1)}), bf16[2,16,56,512]{3,2,0,1:T(8,128)(2,1)S(1)}, u32[]{:S(2)}, u32[]{:S(2)}) async-start(bf16[2,16,56,512]{3,2,0,1:T(8,128)(2,1)} %bitcast.107), calls=%async_computation.5 | async-start | bytes 3670016 | tf_op jit(solution)/shard_map/all_to_all | solution.py:35
  432.7 6.2 %copy-start.7 = (bf16[7168,512]{1,0:T(8,128)(2,1)S(1)}, bf16[7168,512]{1,0:T(8,128)(2,1)}, u32[]{:S(2)}) copy-start(bf16[7168,512]{1,0:T(8,128)(2,1)} %all-gather.5.cloned.1.call-done) | copy-start | bytes 22020100
  432.7 7.3 %copy-start.8 = (bf16[32,24,3584]{2,1,0:T(8,128)(2,1)S(1)}, bf16[32,24,3584]{2,1,0:T(8,128)(2,1)}, u32[]{:S(2)}) copy-start(bf16[32,24,3584]{2,1,0:T(8,128)(2,1)} %all-gather.7.cloned.1.call-done) | copy-start | bytes 16515076
  443.5 9.5 %collective-permute-start = (bf16[768,256]{1,0:T(8,128)(2,1)S(1)}, bf16[768,256]{1,0:T(8,128)(2,1)}, u32[]{:S(2)}, u32[]{:S(2)}) collective-permute-start(bf16[768,256]{1,0:T(8,128)(2,1)S(1)} %get-tuple-element.18), channel_id=1, source_target_pairs={{0,1},{1,0},{2,3},{3,2},{4,5},{5,4},{6,7},{7,6},{8,9},{9,8},{10,11... | collective-permute-start | bytes 1179656 | tf_op jit(solution)/shard_map/ppermute | solution.py:123
  454.6 1.2 copy-start.3
Sparse Core Ops, SparseCore 0:
  12.3 46.2 reduce-scatter.1
  93.0 93.1 all-gather.6
  188.6 47.5 all-gather.4

commit v10 on v7

--- a/solution.py
+++ b/solution.py
@@ -32,7 +32,7 @@
     piece_rows = rows_dev // groups
     split = state.reshape(layers, groups, piece_rows, width)
     spread = lax.all_to_all(split, "grp", split_axis=1, concat_axis=1, tiled=True)
-    chosen = jnp.take(spread, group_source, axis=1)
+    chosen = jnp.take(spread, group_source, axis=1, mode="clip", unique_indices=True)
     home = lax.all_to_all(chosen, "grp", split_axis=1, concat_axis=1, tiled=True)
     return home.reshape(layers, rows_dev, width)
 

time: 288 us -> 290 us (level)
  waiting for transfers between devices: 81.1 us -> 87.2 us
  other arithmetic: 18.3 us -> 13.1 us
    all_to_all x2, waiting for transfers between devices: 34.3 us -> 26.5 us  [migrate(): lax.all_to_all(chosen, 'grp', split_axis=1, concat_axis=1, tiled=True)]
    all_gather x1, waiting for transfers between devices: 22.1 us -> 29.7 us  [local(): both = lax.all_gather(new_weight, ('xhi', 'dp'), axis=0, tiled=True)]
    ppermute x1, waiting for transfers between devices: 0.01 us -> 6.35 us  [local(): for_partner = lax.ppermute(other, 'xhi', perm=[(0, 1), (1, 0)])]
    select_n x3 -> x0, other arithmetic: 5.23 us -> none  [migrate(): chosen = jnp.take(spread, group_source, axis=1)]
  transfers between devices with their start and end apart: 7 -> 7, of which waited for: 4 -> 5; matrix products, arithmetic and copies ran while one was open for 12% -> 10% of each run, Pallas kernels for 0% -> 0%
where the time goes in v10:
time: 290 us; the launch traced here: 288 us
  blocking collectives  130 us (45%)
  waiting for transfers between devices  87.2 us (30%)
  local copies, waits for them, and re-layouts  14.9 us (5%)
  between operations  14.7 us (5%)
  matrix products  14.2 us (5%)
  starting transfers between devices  13.2 us (5%)
  other arithmetic  13.1 us (5%)
    all_to_all x1, blocking collectives, local(): lax.all_to_all(payload, 'grp', split_axis=0, concat_axis=0, tiled=True)  80.3 us
    all_to_all x1, blocking collectives, migrate(): lax.all_to_all(split, 'grp', split_axis=1, concat_axis=1, tiled=True)  50.2 us
    all_gather x1, waiting for transfers between devices, local(): both = lax.all_gather(new_weight, ('xhi', 'dp'), axis=0, tiled=True)  29.7 us
    all_to_all x2, waiting for transfers between devices, migrate(): lax.all_to_all(chosen, 'grp', split_axis=1, concat_axis=1, tiled=True)  26.5 us
    all_to_all x1, waiting for transfers between devices, migrate(): lax.all_to_all(split, 'grp', split_axis=1, concat_axis=1, tiled=True)  24.6 us
    dot_general x2, matrix products, local(): jnp.dot(near, both[k], preferred_element_type=jnp.float32)  9.38 us
    all_to_all x2, starting transfers between devices, migrate(): lax.all_to_all(chosen, 'grp', split_axis=1, concat_axis=1, tiled=True)  7.56 us
    ppermute x1, waiting for transfers between devices, local(): for_partner = lax.ppermute(other, 'xhi', perm=[(0, 1), (1, 0)])  6.35 us
  transfers between devices with their start and end apart: 7, of which 5 were waited for; matrix products, arithmetic and copies ran while one was open for 10% of the time, Pallas kernels for 0%

profile of v10, /device:TPU:4, one launch (start us, length us, event | category | flops | bytes accessed | tf_op | source)
XLA Modules:
  0.0 287.8 jit_solution(12718263698286540359)
XLA Ops:
  7.2 1.1 copy-done
  8.3 3.8 %convolution_convert_fusion = bf16[3584,512]{1,0:T(8,128)(2,1)} fusion(bf16[1,1,128,3584]{3,2,1,0:T(8,128)(2,1)S(1)} %copy-done, bf16[1,1,128,512]{3,2,1,0:T(8,128)(2,1)} %param.14), kind=kOutput, calls=%fused_computation.6 | convolution fusion | flops 471597056 | bytes 4718592 | tf_op jit(solution)/shard_map/dot_general | solution.py:90
  14.5 0.9 convolution_convert_fusion.1
  15.6 80.3 %all_to_all.25 = bf16[16,24,3712]{2,1,0:T(8,128)(2,1)} all-to-all(bf16[16,24,3712]{2,1,0:T(8,128)(2,1)S(1)} %fusion.7), channel_id=1, replica_groups=mesh['dp'=4,'grp'=16,'ylo'=2,'xhi'=2] {'grp'}, dimensions={0} | all-to-all | bytes 5701632 | tf_op jit(solution)/shard_map/all_to_all | solution.py:87
  95.9 1.1 copy-done.5
  97.1 5.1 %fusion.10 = (bf16[896,512]{1,0:T(8,128)(2,1)}, bf16[1,896,512]{2,1,0:T(8,128)(2,1)S(1)}, bf16[1,896,512]{2,1,0:T(8,128)(2,1)}) fusion(bf16[1,896,512]{2,1,0:T(8,128)(2,1)S(1)} %copy-done.5, bf16[896,512]{1,0:T(8,128)(2,1)} %reduce-scatter.2.cloned.1.call-done, f32[1,896,512]{2,1,0:T(8,128)} %param.16, f32[1,896,512]{2,1,0:T(8,128)} %param.17), kind=kLoop, calls=%fused_computation.23 | loop fusion | flops 8257536 | bytes 8257536 | tf_op jit(solution)/shard_map/convert_element_type | solution.py:27
  102.2 3.8 %all-to-all-start.1 = ((bf16[1,16,56,512]{3,2,0,1:T(8,128)(2,1)}), bf16[1,16,56,512]{3,2,0,1:T(8,128)(2,1)S(1)}, u32[]{:S(2)}, u32[]{:S(2)}) async-start(bf16[1,16,56,512]{3,2,0,1:T(8,128)(2,1)} %bitcast.116), calls=%async_computation.2 | async-start | bytes 1835008 | tf_op jit(solution)/shard_map/all_to_all | solution.py:34
  106.1 0.7 gather_fusion
  106.8 24.6 %all-to-all-done.1 = bf16[1,16,56,512]{3,2,0,1:T(8,128)(2,1)S(1)} async-done(((bf16[1,16,56,512]{3,2,0,1:T(8,128)(2,1)}), bf16[1,16,56,512]{3,2,0,1:T(8,128)(2,1)S(1)}, u32[]{:S(2)}, u32[]{:S(2)}) %all-to-all-start.1) | async-done | bytes 917536 | tf_op jit(solution)/shard_map/all_to_all | solution.py:34
  131.4 1.5 gather_fusion.1
  132.9 3.8 %all-to-all-start.2 = ((bf16[1,16,56,512]{3,2,0,1:T(8,128)(2,1)}), bf16[1,16,56,512]{3,2,0,1:T(8,128)(2,1)S(1)}, u32[]{:S(2)}, u32[]{:S(2)}) async-start(bf16[1,16,56,512]{3,2,0,1:T(8,128)(2,1)} %bitcast.28), calls=%async_computation.3 | async-start | bytes 1835008 | tf_op jit(solution)/shard_map/all_to_all | solution.py:36
  136.8 2.6 pad_maximum_fusion
  139.4 24.7 %all-to-all-done.2 = bf16[1,16,56,512]{3,2,0,1:T(8,128)(2,1)S(1)} async-done(((bf16[1,16,56,512]{3,2,0,1:T(8,128)(2,1)}), bf16[1,16,56,512]{3,2,0,1:T(8,128)(2,1)S(1)}, u32[]{:S(2)}, u32[]{:S(2)}) %all-to-all-start.2) | async-done | bytes 917536 | tf_op jit(solution)/shard_map/all_to_all | solution.py:36
  164.1 0.9 copy-done.2
  165.0 1.7 copy.50
  166.8 50.2 %all_to_all.26 = bf16[2,16,56,512]{3,2,0,1:T(8,128)(2,1)S(1)} all-to-all(bf16[2,16,56,512]{3,2,0,1:T(8,128)(2,1)S(1)} %copy.50), channel_id=1, replica_groups=mesh['dp'=4,'grp'=16,'ylo'=2,'xhi'=2] {'grp'}, dimensions={1} | all-to-all | bytes 3670016 | tf_op jit(solution)/shard_map/all_to_all | solution.py:34
  216.9 1.9 gather_fusion.3
  218.8 3.7 %all-to-all-start.4 = ((bf16[2,16,56,512]{3,2,0,1:T(8,128)(2,1)}), bf16[2,16,56,512]{3,2,0,1:T(8,128)(2,1)S(1)}, u32[]{:S(2)}, u32[]{:S(2)}) async-start(bf16[2,16,56,512]{3,2,0,1:T(8,128)(2,1)} %bitcast.112), calls=%async_computation.5 | async-start | bytes 3670016 | tf_op jit(solution)/shard_map/all_to_all | solution.py:36
  222.6 0.9 slice.59
  223.7 29.7 %all-gather.4.cloned.1.call-done = bf16[7168,512]{1,0:T(8,128)(2,1)} async-done(((bf16[896,512]{1,0:T(8,128)(2,1)}), bf16[7168,512]{1,0:T(8,128)(2,1)}) %all-gather.4.cloned.1.call-update) | async-done | bytes 7340048 | tf_op jit(solution)/shard_map/all_gather | solution.py:107
  253.4 6.3 %fusion.18 = f32[1,768,512]{2,1,0:T(8,128)S(1)} fusion(bf16[768,3712]{1,0:T(8,128)(2,1)} %bitcast.122, bf16[2,3584,512]{2,1,0:T(8,128)(2,1)} %bitcast.126), kind=kOutput, calls=%fused_computation.30 | convolution fusion | flops 2919235584 | bytes 14614528 | tf_op jit(solution)/shard_map/dot_general | solution.py:111
  259.7 1.2 copy-done.8
  260.9 3.1 %fusion.15 = f32[1,768,512]{2,1,0:T(8,128)S(1)} fusion(bf16[768,3712]{1,0:T(8,128)(2,1)S(1)} %bitcast.123, bf16[2,3584,512]{2,1,0:T(8,128)(2,1)S(1)} %bitcast.127), kind=kOutput, calls=%fused_computation.29 | convolution fusion | flops 2919235584 | bytes 14614528 | tf_op jit(solution)/shard_map/dot_general | solution.py:111
  264.5 1.8 collective-permute-start
  266.3 1.8 all-to-all-done.4
  268.2 1.5 convert.5
  269.6 1.5 convert.6
  271.1 6.3 %collective-permute-done = bf16[768,256]{1,0:T(8,128)(2,1)} collective-permute-done((bf16[768,256]{1,0:T(8,128)(2,1)S(1)}, bf16[768,256]{1,0:T(8,128)(2,1)}, u32[]{:S(2)}, u32[]{:S(2)}) %collective-permute-start) | collective-permute-done | bytes 393248 | tf_op jit(solution)/shard_map/ppermute | solution.py:122
  277.5 1.1 pad_maximum_fusion.2
  278.5 0.6 gather_fusion.2
  279.3 1.0 copy.49
  280.4 0.9 copy.56
  (53 shorter events, 3.0 us)
Async XLA Ops:
  7.2 1.2 copy-start
  7.2 88.7 %reduce-scatter.2.cloned.1.call-start = ((), (), s32[]{:S(2)}) async-start(), calls=%async_computation.6 | async-start | bytes 4587520 | tf_op jit(solution)/shard_map/reduce_scatter | solution.py:89
  12.2 0.7 copy-start.9
  12.2 1.4 copy-start.7
  12.2 1.9 copy-start.10
  12.2 2.3 copy-start.4
  12.2 210.4 %all-gather.6.cloned.1.call-start = ((), (), s32[]{:S(2)}) async-start(), calls=%async_computation.8 | async-start | bytes 8552448 | tf_op jit(solution)/shard_map/all_gather | solution.py:99
  95.9 1.2 copy-start.5
  102.2 3.8 %copy-start.1 = (s32[16]{0:T(128)S(1)}, s32[16]{0:T(128)}, u32[]{:S(2)}) copy-start(s32[16]{0:T(128)} %param.22) | copy-start | bytes 196
  102.2 29.1 %all-to-all-start.1 = ((bf16[1,16,56,512]{3,2,0,1:T(8,128)(2,1)}), bf16[1,16,56,512]{3,2,0,1:T(8,128)(2,1)S(1)}, u32[]{:S(2)}, u32[]{:S(2)}) async-start(bf16[1,16,56,512]{3,2,0,1:T(8,128)(2,1)} %bitcast.116), calls=%async_computation.2 | async-start | bytes 1835008 | tf_op jit(solution)/shard_map/all_to_all | solution.py:34
  132.9 31.2 %all-to-all-start.2 = ((bf16[1,16,56,512]{3,2,0,1:T(8,128)(2,1)}), bf16[1,16,56,512]{3,2,0,1:T(8,128)(2,1)S(1)}, u32[]{:S(2)}, u32[]{:S(2)}) async-start(bf16[1,16,56,512]{3,2,0,1:T(8,128)(2,1)} %bitcast.28), calls=%async_computation.3 | async-start | bytes 1835008 | tf_op jit(solution)/shard_map/all_to_all | solution.py:36
  136.7 116.7 %all-gather.4.cloned.1.call-start = ((), (), s32[]{:S(2)}) async-start(), calls=%async_computation.7 | async-start | bytes 8257536 | tf_op jit(solution)/shard_map/all_gather | solution.py:107
  164.1 0.9 copy-start.2
  218.8 49.2 %all-to-all-start.4 = ((bf16[2,16,56,512]{3,2,0,1:T(8,128)(2,1)}), bf16[2,16,56,512]{3,2,0,1:T(8,128)(2,1)S(1)}, u32[]{:S(2)}, u32[]{:S(2)}) async-start(bf16[2,16,56,512]{3,2,0,1:T(8,128)(2,1)} %bitcast.112), calls=%async_computation.5 | async-start | bytes 3670016 | tf_op jit(solution)/shard_map/all_to_all | solution.py:36
  253.4 6.3 %copy-start.6 = (bf16[32,24,3712]{2,1,0:T(8,128)(2,1)S(1)}, bf16[32,24,3712]{2,1,0:T(8,128)(2,1)}, u32[]{:S(2)}) copy-start(bf16[32,24,3712]{2,1,0:T(8,128)(2,1)} %all-gather.6.cloned.1.call-done) | copy-start | bytes 17104900
  253.4 7.5 %copy-start.8 = (bf16[7168,512]{1,0:T(8,128)(2,1)S(1)}, bf16[7168,512]{1,0:T(8,128)(2,1)}, u32[]{:S(2)}) copy-start(bf16[7168,512]{1,0:T(8,128)(2,1)} %all-gather.4.cloned.1.call-done) | copy-start | bytes 22020100
  264.5 13.0 %collective-permute-start = (bf16[768,256]{1,0:T(8,128)(2,1)S(1)}, bf16[768,256]{1,0:T(8,128)(2,1)}, u32[]{:S(2)}, u32[]{:S(2)}) collective-permute-start(bf16[768,256]{1,0:T(8,128)(2,1)S(1)} %get-tuple-element.30), channel_id=1, source_target_pairs={{0,1},{1,0},{2,3},{3,2},{4,5},{5,4},{6,7},{7,6},{8,9},{9,8},{10,11... | collective-permute-start | bytes 1179656 | tf_op jit(solution)/shard_map/ppermute | solution.py:122
  279.1 1.2 copy-start.3
Sparse Core Ops, SparseCore 0:
  12.3 46.2 reduce-scatter.1
  96.1 106.2 all-gather.5
  204.8 48.6 all-gather.3

commit v11 on v10

--- a/solution.py
+++ b/solution.py
@@ -84,7 +84,8 @@
     )
     scale_cols = jnp.zeros((groups, capacity, SCALE_PAD), jnp.bfloat16).at[:, :, 0].set(gate_scale)
     payload = jnp.concatenate([packed, scale_cols], axis=2)
-    by_group = lax.all_to_all(payload, "grp", split_axis=0, concat_axis=0, tiled=True)
+    half = capacity // 2
+    by_first = lax.all_to_all(payload[:, :half], "grp", split_axis=0, concat_axis=0, tiled=True)
 
     grads = lax.psum_scatter(
         lax.dot_general(
@@ -94,36 +95,47 @@
         scatter_dimension=0,
         tiled=True,
     )
-    by_group, grads = lax.optimization_barrier((by_group, grads))
+    by_first, grads = lax.optimization_barrier((by_first, grads))
     grads = grads.astype(jnp.float32)
-    near = lax.all_gather(by_group, "ylo", axis=0, tiled=False)
-    near = near.reshape(2 * groups * capacity, D + SCALE_PAD)
     stepped, first_next, second_next = adamw(weights[0], first_moment[0], second_moment[0], grads)
     new_weight = migrate(stepped[None], group_source, groups)[0]
+    second, new_weight = lax.optimization_barrier((payload[:, half:], new_weight))
+    by_second = lax.all_to_all(second, "grp", split_axis=0, concat_axis=0, tiled=True)
     moments = jnp.stack([first_next.astype(jnp.bfloat16), second_next.astype(jnp.bfloat16)])
-    moments, new_weight = lax.optimization_barrier((moments, new_weight))
+    moments, by_second = lax.optimization_barrier((moments, by_second))
     moved = migrate(moments, group_source, groups)
+    from_ylo = lax.ppermute(by_second, "ylo", perm=[(0, 1), (1, 0)])
+    near = [
+        lax.all_gather(by_first, "ylo", axis=0, tiled=False),
+        jnp.stack([by_second, from_ylo]),
+    ]
+    near = [n.reshape(2 * groups * half, D + SCALE_PAD) for n in near]
 
     both = lax.all_gather(new_weight, ("xhi", "dp"), axis=0, tiled=True)
     both = both.reshape(2, -1, width)
     both = jnp.pad(both, ((0, 0), (0, SCALE_PAD), (0, 0)))
     projected = jnp.stack(
-        [jnp.dot(near, both[k], preferred_element_type=jnp.float32) for k in range(2)]
+        [
+            jnp.stack([jnp.dot(n, both[k], preferred_element_type=jnp.float32) for n in near])
+            for k in range(2)
+        ]
     )
-    scaling = near[:, D].astype(jnp.float32)
+    scaling = jnp.stack([n[:, D] for n in near]).astype(jnp.float32)
     result = (
-        jax.nn.silu(projected[:, :, :hidden_units])
-        * projected[:, :, hidden_units:]
-        * scaling[None, :, None]
+        jax.nn.silu(projected[..., :hidden_units])
+        * projected[..., hidden_units:]
+        * scaling[None, :, :, None]
     ).astype(jnp.bfloat16)
     xhi = lax.axis_index("xhi")
     own = lax.dynamic_index_in_dim(result, xhi, axis=0, keepdims=False)
     other = lax.dynamic_index_in_dim(result, 1 - xhi, axis=0, keepdims=False)
     for_partner = lax.ppermute(other, "xhi", perm=[(0, 1), (1, 0)])
-    mine = jnp.stack([own, for_partner]).reshape(2, 2, groups, capacity, hidden_units)
+    mine = jnp.stack([own, for_partner]).reshape(2, 2, 2, groups, half, hidden_units)
     flip = jnp.arange(2, dtype=jnp.int32)
     mine = jnp.take(mine, flip ^ xhi, axis=0)
-    hidden = jnp.transpose(mine, (2, 1, 0, 3, 4)).reshape(1, 1, experts * capacity, hidden_units)
+    ylo = lax.axis_index("ylo")
+    mine = jnp.stack([mine[:, 0], jnp.take(mine[:, 1], flip ^ ylo, axis=1)], axis=1)
+    hidden = jnp.transpose(mine, (3, 2, 0, 1, 4, 5)).reshape(1, 1, experts * capacity, hidden_units)
     return (
         hidden,
         new_weight[None],

time: 290 us -> 319 us (1.10)
  blocking collectives: 130 us -> 90.4 us
  waiting for transfers between devices: 87.2 us -> 123 us
  local copies, waits for them, and re-layouts: 14.9 us -> 41.3 us
  starting transfers between devices: 13.2 us -> 18.6 us
    all_to_all x0 -> x1, waiting for transfers between devices: none -> 44.8 us  [local(): lax.all_to_all(second, 'grp', split_axis=0, concat_axis=0, tiled=True)]
    all_to_all x2, blocking collectives: 130 us -> 90.4 us  [the longest x1 59.6 us: local(): lax.all_to_all(payload[:, :half], 'grp', split_axis=0, concat_axis=0, til...]
    all_to_all x1 -> x2, waiting for transfers between devices: 24.6 us -> 56.9 us  [migrate(): lax.all_to_all(split, 'grp', split_axis=1, concat_axis=1, tiled=True)]
    all_gather x1, waiting for transfers between devices: 29.7 us -> 0.02 us  [local(): both = lax.all_gather(new_weight, ('xhi', 'dp'), axis=0, tiled=True)]
    reshape x0 -> x3, local copies, waits for them, and re-layouts: none -> 11.9 us  [the longest x2 10.8 us: local(): near = [n.reshape(2 * groups * half, D + SCALE_PAD) for n in near]]
    ppermute x1, waiting for transfers between devices: 6.35 us -> 0.01 us  [local(): for_partner = lax.ppermute(other, 'xhi', perm=[(0, 1), (1, 0)])]
    all_to_all x2 -> x1, waiting for transfers between devices: 26.5 us -> 21.5 us  [migrate(): lax.all_to_all(chosen, 'grp', split_axis=1, concat_axis=1, tiled=True)]
    all_to_all x1 -> x2, starting transfers between devices: 3.78 us -> 8.72 us  [migrate(): lax.all_to_all(split, 'grp', split_axis=1, concat_axis=1, tiled=True)]
  transfers between devices with their start and end apart: 7 -> 9, of which waited for: 5 -> 4; matrix products, arithmetic and copies ran while one was open for 10% -> 17% of each run, Pallas kernels for 0% -> 0%
where the time goes in v11:
time: 319 us; the launch traced here: 318 us
  waiting for transfers between devices  123 us (39%)
  blocking collectives  90.4 us (28%)
  local copies, waits for them, and re-layouts  41.3 us (13%)
  starting transfers between devices  18.6 us (6%)
  other arithmetic  15.2 us (5%)
  between operations  14.9 us (5%)
  matrix products  14.3 us (4%)
    all_to_all x1, blocking collectives, local(): lax.all_to_all(payload[:, :half], 'grp', split_axis=0, concat_axis=0, til...  59.6 us
    all_to_all x2, waiting for transfers between devices, migrate(): lax.all_to_all(split, 'grp', split_axis=1, concat_axis=1, tiled=True)  56.9 us
    all_to_all x1, waiting for transfers between devices, local(): lax.all_to_all(second, 'grp', split_axis=0, concat_axis=0, tiled=True)  44.8 us
    all_to_all x1, blocking collectives, migrate(): lax.all_to_all(chosen, 'grp', split_axis=1, concat_axis=1, tiled=True)  30.8 us
    all_to_all x1, waiting for transfers between devices, migrate(): lax.all_to_all(chosen, 'grp', split_axis=1, concat_axis=1, tiled=True)  21.5 us
    reshape x2, local copies, waits for them, and re-layouts, local(): near = [n.reshape(2 * groups * half, D + SCALE_PAD) for n in near]  10.8 us
    dot_general x4, matrix products, local(): jnp.dot(n, both[k], preferred_element_type=jnp.float32)  9.49 us
    all_to_all x2, starting transfers between devices, migrate(): lax.all_to_all(split, 'grp', split_axis=1, concat_axis=1, tiled=True)  8.72 us
  transfers between devices with their start and end apart: 9, of which 4 were waited for; matrix products, arithmetic and copies ran while one was open for 17% of the time, Pallas kernels for 0%

profile of v11, /device:TPU:4, one launch (start us, length us, event | category | flops | bytes accessed | tf_op | source)
XLA Modules:
  0.0 317.9 jit_solution(7171319454848312849)
XLA Ops:
  8.4 3.8 %convolution_convert_fusion = bf16[3584,512]{1,0:T(8,128)(2,1)} fusion(bf16[1,1,128,3584]{3,2,1,0:T(8,128)(2,1)S(1)} %copy-done, bf16[1,1,128,512]{3,2,1,0:T(8,128)(2,1)} %param.14), kind=kOutput, calls=%fused_computation.7 | convolution fusion | flops 471597056 | bytes 4718592 | tf_op jit(solution)/shard_map/dot_general | solution.py:91
  15.1 1.8 fusion.54
  16.9 59.6 %all_to_all.30 = bf16[16,12,3712]{2,1,0:T(8,128)(2,1)S(1)} all-to-all(bf16[16,12,3712]{2,1,0:T(8,128)(2,1)S(1)} %get-tuple-element.29), channel_id=1, replica_groups=mesh['dp'=4,'grp'=16,'ylo'=2,'xhi'=2] {'grp'}, dimensions={0} | all-to-all | bytes 2850816 | tf_op jit(solution)/shard_map/all_to_all | solution.py:88
  76.5 5.3 %fusion.14 = (bf16[896,512]{1,0:T(8,128)(2,1)}, bf16[1,896,512]{2,1,0:T(8,128)(2,1)}, bf16[1,896,512]{2,1,0:T(8,128)(2,1)}) fusion(bf16[1,896,512]{2,1,0:T(8,128)(2,1)S(1)} %copy-done.8, bf16[896,512]{1,0:T(8,128)(2,1)} %reduce-scatter.2.cloned.1.call-done, f32[1,896,512]{2,1,0:T(8,128)} %param.16, f32[1,896,512]{2,1,0:T(8,128)} %param.17), kind=kLoop, calls=%fused_computation.28 | loop fusion | flops 8257536 | bytes 8257536 | tf_op jit(solution)/shard_map/convert_element_type | solution.py:27
  81.7 4.3 %all-to-all-start.1 = ((bf16[1,16,56,512]{3,2,0,1:T(8,128)(2,1)}), bf16[1,16,56,512]{3,2,0,1:T(8,128)(2,1)}, u32[]{:S(2)}, u32[]{:S(2)}) async-start(bf16[1,16,56,512]{3,2,0,1:T(8,128)(2,1)} %bitcast.18), calls=%async_computation.2 | async-start | bytes 1835008 | tf_op jit(solution)/shard_map/all_to_all | solution.py:34
  86.1 1.3 copy.62
  88.2 23.1 %all-to-all-done.1 = bf16[1,16,56,512]{3,2,0,1:T(8,128)(2,1)} async-done(((bf16[1,16,56,512]{3,2,0,1:T(8,128)(2,1)}), bf16[1,16,56,512]{3,2,0,1:T(8,128)(2,1)}, u32[]{:S(2)}, u32[]{:S(2)}) %all-to-all-start.1) | async-done | bytes 917536 | tf_op jit(solution)/shard_map/all_to_all | solution.py:34
  111.3 1.8 gather_fusion.1
  113.1 30.8 %all_to_all.31 = bf16[1,16,56,512]{3,2,0,1:T(8,128)(2,1)} all-to-all(bf16[1,16,56,512]{3,2,0,1:T(8,128)(2,1)S(1)} %bitcast.141), channel_id=1, replica_groups=mesh['dp'=4,'grp'=16,'ylo'=2,'xhi'=2] {'grp'}, dimensions={1} | all-to-all | bytes 1835008 | tf_op jit(solution)/shard_map/all_to_all | solution.py:36
  144.0 3.9 %all-to-all-start.3 = ((bf16[16,12,3712]{2,1,0:T(8,128)(2,1)}), bf16[16,12,3712]{2,1,0:T(8,128)(2,1)S(1)}, u32[]{:S(2)}, u32[]{:S(2)}) async-start(bf16[16,12,3712]{2,1,0:T(8,128)(2,1)} %get-tuple-element.25), calls=%async_computation.4 | async-start | bytes 3801088 | tf_op jit(solution)/shard_map/all_to_all | solution.py:103
  147.8 2.6 pad_maximum_fusion.1
  150.4 44.8 %all-to-all-done.3 = bf16[16,12,3712]{2,1,0:T(8,128)(2,1)S(1)} async-done(((bf16[16,12,3712]{2,1,0:T(8,128)(2,1)}), bf16[16,12,3712]{2,1,0:T(8,128)(2,1)S(1)}, u32[]{:S(2)}, u32[]{:S(2)}) %all-to-all-start.3) | async-done | bytes 1425440 | tf_op jit(solution)/shard_map/all_to_all | solution.py:103
  195.2 3.0 copy.74
  198.2 4.4 %all-to-all-start.4 = ((bf16[2,16,56,512]{3,2,0,1:T(8,128)(2,1)}), bf16[2,16,56,512]{3,2,0,1:T(8,128)(2,1)}, u32[]{:S(2)}, u32[]{:S(2)}) async-start(bf16[2,16,56,512]{3,2,0,1:T(8,128)(2,1)} %copy.74), calls=%async_computation.5 | async-start | bytes 3670016 | tf_op jit(solution)/shard_map/all_to_all | solution.py:34
  202.6 1.3 copy.66
  204.6 4.5 %copy.63 = bf16[32,12,3712]{2,1,0:T(8,128)(2,1)} copy(bf16[32,12,3712]{2,0,1:T(8,128)(2,1)} %all-gather.6.cloned.1.call-done) | data formatting | bytes 5701632 | tf_op jit(solution)/shard_map/all_gather | solution.py:109
  209.2 5.4 %reshape.219 = bf16[384,3712]{1,0:T(8,128)(2,1)} reshape(bf16[32,12,3712]{2,1,0:T(8,128)(2,1)} %copy.63) | data formatting | bytes 5701632 | tf_op jit(solution)/shard_map/reshape | solution.py:112
  214.6 33.8 %all-to-all-done.4 = bf16[2,16,56,512]{3,2,0,1:T(8,128)(2,1)} async-done(((bf16[2,16,56,512]{3,2,0,1:T(8,128)(2,1)}), bf16[2,16,56,512]{3,2,0,1:T(8,128)(2,1)}, u32[]{:S(2)}, u32[]{:S(2)}) %all-to-all-start.4) | async-done | bytes 1835040 | tf_op jit(solution)/shard_map/all_to_all | solution.py:34
  248.4 3.4 %gather_fusion.4 = bf16[16,2,56,512]{3,2,1,0:T(8,128)(2,1)} fusion(bf16[2,16,56,512]{3,2,0,1:T(8,128)(2,1)} %all-to-all-done.4, s32[1024]{0:T(1024)S(1)} %pad_clamp_fusion.2), kind=kCustom, calls=%fused_computation.4 | custom fusion | bytes 3670080 | tf_op jit(solution)/shard_map/jit(_take)/gather | solution.py:35
  251.8 4.6 %all-to-all-start.5 = ((bf16[2,16,56,512]{3,2,0,1:T(8,128)(2,1)}), bf16[2,16,56,512]{3,2,0,1:T(8,128)(2,1)}, u32[]{:S(2)}, u32[]{:S(2)}) async-start(bf16[2,16,56,512]{3,2,0,1:T(8,128)(2,1)} %bitcast.140), calls=%async_computation.6 | async-start | bytes 3670016 | tf_op jit(solution)/shard_map/all_to_all | solution.py:36
  257.4 1.6 copy.79
  259.0 2.5 pad_maximum_fusion
  261.5 5.4 %reshape.221 = bf16[384,3712]{1,0:T(8,128)(2,1)} reshape(bf16[2,16,12,3712]{3,2,1,0:T(8,128)(2,1)} %pad_maximum_fusion) | data formatting | bytes 5701632 | tf_op jit(solution)/shard_map/reshape | solution.py:112
  268.0 4.7 %fusion.25 = f32[1,384,512]{2,1,0:T(8,128)S(1)} fusion(bf16[384,3712]{1,0:T(8,128)(2,1)} %reshape.219, bf16[2,3584,512]{2,1,0:T(8,128)(2,1)} %bitcast.150), kind=kOutput, calls=%fused_computation.38 | convolution fusion | flops 1459617792 | bytes 10977280 | tf_op jit(solution)/shard_map/dot_general | solution.py:119
  272.7 1.2 copy-done.10
  273.9 1.6 fusion.28
  275.7 1.6 fusion.19
  277.3 1.6 fusion.22
  280.4 21.5 %all-to-all-done.5 = bf16[2,16,56,512]{3,2,0,1:T(8,128)(2,1)} async-done(((bf16[2,16,56,512]{3,2,0,1:T(8,128)(2,1)}), bf16[2,16,56,512]{3,2,0,1:T(8,128)(2,1)}, u32[]{:S(2)}, u32[]{:S(2)}) %all-to-all-start.5) | async-done | bytes 1835040 | tf_op jit(solution)/shard_map/all_to_all | solution.py:36
  301.9 1.6 fusion.55
  303.5 1.5 convert.4
  304.9 1.5 convert.5
  (84 shorter events, 13.3 us)
Async XLA Ops:
  7.2 1.2 copy-start
  7.2 69.3 %reduce-scatter.2.cloned.1.call-start = ((), (), s32[]{:S(2)}) async-start(), calls=%async_computation.7 | async-start | bytes 4587520 | tf_op jit(solution)/shard_map/reduce_scatter | solution.py:90
  12.2 0.8 copy-start.11
  12.2 0.9 copy-start.9
  12.2 1.3 copy-start.12
  12.2 1.8 copy-start.7
  16.9 59.6 %copy-start.8 = (bf16[1,896,512]{2,1,0:T(8,128)(2,1)S(1)}, bf16[1,896,512]{2,1,0:T(8,128)(2,1)}, u32[]{:S(2)}) copy-start(bf16[1,896,512]{2,1,0:T(8,128)(2,1)} %param.15) | copy-start | bytes 2752516
  81.7 29.6 %all-to-all-start.1 = ((bf16[1,16,56,512]{3,2,0,1:T(8,128)(2,1)}), bf16[1,16,56,512]{3,2,0,1:T(8,128)(2,1)}, u32[]{:S(2)}, u32[]{:S(2)}) async-start(bf16[1,16,56,512]{3,2,0,1:T(8,128)(2,1)} %bitcast.18), calls=%async_computation.2 | async-start | bytes 1835008 | tf_op jit(solution)/shard_map/all_to_all | solution.py:34
  86.0 1.5 copy-start.2
  86.1 118.6 %all-gather.6.cloned.1.call-start = ((), (), s32[]{:S(2)}) async-start(), calls=%async_computation.9 | async-start | bytes 4276224 | tf_op jit(solution)/shard_map/all_gather | solution.py:109
  87.4 180.6 %all-gather.4.cloned.1.call-start = ((), (), s32[]{:S(2)}) async-start(), calls=%async_computation.8 | async-start | bytes 8257536 | tf_op jit(solution)/shard_map/all_gather | solution.py:114
  143.9 3.9 %copy-start.4 = (bf16[1,896,512]{2,1,0:T(8,128)(2,1)S(1)}, bf16[1,896,512]{2,1,0:T(8,128)(2,1)}, u32[]{:S(2)}) copy-start(bf16[1,896,512]{2,1,0:T(8,128)(2,1)} %get-tuple-element.31) | copy-start | bytes 2752516
  144.0 51.2 %all-to-all-start.3 = ((bf16[16,12,3712]{2,1,0:T(8,128)(2,1)}), bf16[16,12,3712]{2,1,0:T(8,128)(2,1)S(1)}, u32[]{:S(2)}, u32[]{:S(2)}) async-start(bf16[16,12,3712]{2,1,0:T(8,128)(2,1)} %get-tuple-element.25), calls=%async_computation.4 | async-start | bytes 3801088 | tf_op jit(solution)/shard_map/all_to_all | solution.py:103
  198.2 50.2 %all-to-all-start.4 = ((bf16[2,16,56,512]{3,2,0,1:T(8,128)(2,1)}), bf16[2,16,56,512]{3,2,0,1:T(8,128)(2,1)}, u32[]{:S(2)}, u32[]{:S(2)}) async-start(bf16[2,16,56,512]{3,2,0,1:T(8,128)(2,1)} %copy.74), calls=%async_computation.5 | async-start | bytes 3670016 | tf_op jit(solution)/shard_map/all_to_all | solution.py:34
  203.9 53.4 %collective-permute-start = (bf16[16,12,3712]{2,0,1:T(8,128)(2,1)}, bf16[16,12,3712]{2,0,1:T(8,128)(2,1)}, u32[]{:S(2)}, u32[]{:S(2)}) collective-permute-start(bf16[16,12,3712]{2,0,1:T(8,128)(2,1)} %copy.66), channel_id=1, source_target_pairs={{0,2},{2,0},{1,3},{3,1},{4,6},{6,4},{5,7},{7,5},{8,10},{10,8},{9,1... | collective-permute-start | bytes 4276232 | tf_op jit(solution)/shard_map/ppermute | solution.py:107
  251.8 50.1 %all-to-all-start.5 = ((bf16[2,16,56,512]{3,2,0,1:T(8,128)(2,1)}), bf16[2,16,56,512]{3,2,0,1:T(8,128)(2,1)}, u32[]{:S(2)}, u32[]{:S(2)}) async-start(bf16[2,16,56,512]{3,2,0,1:T(8,128)(2,1)} %bitcast.140), calls=%async_computation.6 | async-start | bytes 3670016 | tf_op jit(solution)/shard_map/all_to_all | solution.py:36
  268.0 4.7 %copy-start.6 = (bf16[384,3712]{1,0:T(8,128)(2,1)S(1)}, bf16[384,3712]{1,0:T(8,128)(2,1)}, u32[]{:S(2)}) copy-start(bf16[384,3712]{1,0:T(8,128)(2,1)} %reshape.221) | copy-start | bytes 8552452
  268.0 5.9 %copy-start.10 = (bf16[7168,512]{1,0:T(8,128)(2,1)S(1)}, bf16[7168,512]{1,0:T(8,128)(2,1)}, u32[]{:S(2)}) copy-start(bf16[7168,512]{1,0:T(8,128)(2,1)} %all-gather.4.cloned.1.call-done) | copy-start | bytes 22020100
  273.9 1.8 copy-start.5
  279.7 27.2 %collective-permute-start.1 = (bf16[2,384,256]{2,1,0:T(8,128)(2,1)S(1)}, bf16[2,384,256]{2,1,0:T(8,128)(2,1)S(1)}, u32[]{:S(2)}, u32[]{:S(2)}) collective-permute-start(bf16[2,384,256]{2,1,0:T(8,128)(2,1)S(1)} %get-tuple-element.38), channel_id=1, source_target_pairs={{0,1},{1,0},{2,3},{3,2},{4,5},{5,4},{6,7},{7,6},{8,9},{9,8},{10,11... | collective-permute-start | bytes 1179656 | tf_op jit(solution)/shard_map/ppermute | solution.py:132
  309.1 1.4 copy-start.3
  309.1 2.3 copy-start.1
Sparse Core Ops, SparseCore 0:
  12.3 46.2 reduce-scatter.1
  88.7 59.7 all-gather.5
  150.3 46.1 all-gather.3

commit v12 on v10

--- a/solution.py
+++ b/solution.py
@@ -107,19 +107,21 @@
     both = lax.all_gather(new_weight, ("xhi", "dp"), axis=0, tiled=True)
     both = both.reshape(2, -1, width)
     both = jnp.pad(both, ((0, 0), (0, SCALE_PAD), (0, 0)))
-    projected = jnp.stack(
-        [jnp.dot(near, both[k], preferred_element_type=jnp.float32) for k in range(2)]
-    )
     scaling = near[:, D].astype(jnp.float32)
-    result = (
-        jax.nn.silu(projected[:, :, :hidden_units])
-        * projected[:, :, hidden_units:]
-        * scaling[None, :, None]
-    ).astype(jnp.bfloat16)
     xhi = lax.axis_index("xhi")
-    own = lax.dynamic_index_in_dim(result, xhi, axis=0, keepdims=False)
-    other = lax.dynamic_index_in_dim(result, 1 - xhi, axis=0, keepdims=False)
+
+    def swiglu(weight_set):
+        projected = jnp.dot(near, weight_set, preferred_element_type=jnp.float32)
+        result = (
+            jax.nn.silu(projected[:, :hidden_units])
+            * projected[:, hidden_units:]
+            * scaling[:, None]
+        )
+        return result.astype(jnp.bfloat16)
+
+    other = swiglu(lax.dynamic_index_in_dim(both, 1 - xhi, axis=0, keepdims=False))
     for_partner = lax.ppermute(other, "xhi", perm=[(0, 1), (1, 0)])
+    own = swiglu(lax.dynamic_index_in_dim(both, xhi, axis=0, keepdims=False))
     mine = jnp.stack([own, for_partner]).reshape(2, 2, groups, capacity, hidden_units)
     flip = jnp.arange(2, dtype=jnp.int32)
     mine = jnp.take(mine, flip ^ xhi, axis=0)

time: 290 us -> 290 us (level)
  no operation moved by 1% of the time
where the time goes in v12:
time: 290 us; the launch traced here: 288 us
  blocking collectives  130 us (45%)
  waiting for transfers between devices  87.2 us (30%)
  local copies, waits for them, and re-layouts  14.9 us (5%)
  between operations  14.6 us (5%)
  matrix products  14.2 us (5%)
  starting transfers between devices  13.2 us (5%)
  other arithmetic  13.1 us (5%)
    all_to_all x1, blocking collectives, local(): lax.all_to_all(payload, 'grp', split_axis=0, concat_axis=0, tiled=True)  80.3 us
    all_to_all x1, blocking collectives, migrate(): lax.all_to_all(split, 'grp', split_axis=1, concat_axis=1, tiled=True)  50.2 us
    all_gather x1, waiting for transfers between devices, local(): both = lax.all_gather(new_weight, ('xhi', 'dp'), axis=0, tiled=True)  29.7 us
    all_to_all x2, waiting for transfers between devices, migrate(): lax.all_to_all(chosen, 'grp', split_axis=1, concat_axis=1, tiled=True)  26.5 us
    all_to_all x1, waiting for transfers between devices, migrate(): lax.all_to_all(split, 'grp', split_axis=1, concat_axis=1, tiled=True)  24.6 us
    dot_general x2, matrix products, swiglu(): projected = jnp.dot(near, weight_set, preferred_element_type=jnp.float32)  9.38 us
    all_to_all x2, starting transfers between devices, migrate(): lax.all_to_all(chosen, 'grp', split_axis=1, concat_axis=1, tiled=True)  7.56 us
    ppermute x1, waiting for transfers between devices, local(): for_partner = lax.ppermute(other, 'xhi', perm=[(0, 1), (1, 0)])  6.3 us
  transfers between devices with their start and end apart: 7, of which 5 were waited for; matrix products, arithmetic and copies ran while one was open for 10% of the time, Pallas kernels for 0%

profile of v12, /device:TPU:4, one launch (start us, length us, event | category | flops | bytes accessed | tf_op | source)
XLA Modules:
  0.0 287.8 jit_solution(16032511693016400014)
XLA Ops:
  7.2 1.1 copy-done
  8.3 3.8 %convolution_convert_fusion = bf16[3584,512]{1,0:T(8,128)(2,1)} fusion(bf16[1,1,128,3584]{3,2,1,0:T(8,128)(2,1)S(1)} %copy-done, bf16[1,1,128,512]{3,2,1,0:T(8,128)(2,1)} %param.14), kind=kOutput, calls=%fused_computation.6 | convolution fusion | flops 471597056 | bytes 4718592 | tf_op jit(solution)/shard_map/dot_general | solution.py:90
  14.5 0.9 convolution_convert_fusion.1
  15.6 80.3 %all_to_all.25 = bf16[16,24,3712]{2,1,0:T(8,128)(2,1)} all-to-all(bf16[16,24,3712]{2,1,0:T(8,128)(2,1)S(1)} %fusion.7), channel_id=1, replica_groups=mesh['dp'=4,'grp'=16,'ylo'=2,'xhi'=2] {'grp'}, dimensions={0} | all-to-all | bytes 5701632 | tf_op jit(solution)/shard_map/all_to_all | solution.py:87
  95.9 1.1 copy-done.5
  97.1 5.1 %fusion.10 = (bf16[896,512]{1,0:T(8,128)(2,1)}, bf16[1,896,512]{2,1,0:T(8,128)(2,1)S(1)}, bf16[1,896,512]{2,1,0:T(8,128)(2,1)}) fusion(bf16[1,896,512]{2,1,0:T(8,128)(2,1)S(1)} %copy-done.5, bf16[896,512]{1,0:T(8,128)(2,1)} %reduce-scatter.2.cloned.1.call-done, f32[1,896,512]{2,1,0:T(8,128)} %param.16, f32[1,896,512]{2,1,0:T(8,128)} %param.17), kind=kLoop, calls=%fused_computation.21 | loop fusion | flops 8257536 | bytes 8257536 | tf_op jit(solution)/shard_map/convert_element_type | solution.py:27
  102.2 3.8 %all-to-all-start.1 = ((bf16[1,16,56,512]{3,2,0,1:T(8,128)(2,1)}), bf16[1,16,56,512]{3,2,0,1:T(8,128)(2,1)S(1)}, u32[]{:S(2)}, u32[]{:S(2)}) async-start(bf16[1,16,56,512]{3,2,0,1:T(8,128)(2,1)} %bitcast.106), calls=%async_computation.2 | async-start | bytes 1835008 | tf_op jit(solution)/shard_map/all_to_all | solution.py:34
  106.1 0.7 gather_fusion
  106.8 24.6 %all-to-all-done.1 = bf16[1,16,56,512]{3,2,0,1:T(8,128)(2,1)S(1)} async-done(((bf16[1,16,56,512]{3,2,0,1:T(8,128)(2,1)}), bf16[1,16,56,512]{3,2,0,1:T(8,128)(2,1)S(1)}, u32[]{:S(2)}, u32[]{:S(2)}) %all-to-all-start.1) | async-done | bytes 917536 | tf_op jit(solution)/shard_map/all_to_all | solution.py:34
  131.4 1.5 gather_fusion.1
  132.9 3.8 %all-to-all-start.2 = ((bf16[1,16,56,512]{3,2,0,1:T(8,128)(2,1)}), bf16[1,16,56,512]{3,2,0,1:T(8,128)(2,1)S(1)}, u32[]{:S(2)}, u32[]{:S(2)}) async-start(bf16[1,16,56,512]{3,2,0,1:T(8,128)(2,1)} %bitcast.28), calls=%async_computation.3 | async-start | bytes 1835008 | tf_op jit(solution)/shard_map/all_to_all | solution.py:36
  136.8 2.6 pad_maximum_fusion
  139.4 24.7 %all-to-all-done.2 = bf16[1,16,56,512]{3,2,0,1:T(8,128)(2,1)S(1)} async-done(((bf16[1,16,56,512]{3,2,0,1:T(8,128)(2,1)}), bf16[1,16,56,512]{3,2,0,1:T(8,128)(2,1)S(1)}, u32[]{:S(2)}, u32[]{:S(2)}) %all-to-all-start.2) | async-done | bytes 917536 | tf_op jit(solution)/shard_map/all_to_all | solution.py:36
  164.1 0.9 copy-done.2
  165.0 1.7 copy.45
  166.8 50.2 %all_to_all.26 = bf16[2,16,56,512]{3,2,0,1:T(8,128)(2,1)S(1)} all-to-all(bf16[2,16,56,512]{3,2,0,1:T(8,128)(2,1)S(1)} %copy.45), channel_id=1, replica_groups=mesh['dp'=4,'grp'=16,'ylo'=2,'xhi'=2] {'grp'}, dimensions={1} | all-to-all | bytes 3670016 | tf_op jit(solution)/shard_map/all_to_all | solution.py:34
  216.9 1.9 gather_fusion.3
  218.8 3.7 %all-to-all-start.4 = ((bf16[2,16,56,512]{3,2,0,1:T(8,128)(2,1)}), bf16[2,16,56,512]{3,2,0,1:T(8,128)(2,1)S(1)}, u32[]{:S(2)}, u32[]{:S(2)}) async-start(bf16[2,16,56,512]{3,2,0,1:T(8,128)(2,1)} %bitcast.102), calls=%async_computation.5 | async-start | bytes 3670016 | tf_op jit(solution)/shard_map/all_to_all | solution.py:36
  222.6 0.9 slice.59
  223.7 29.7 %all-gather.4.cloned.1.call-done = bf16[7168,512]{1,0:T(8,128)(2,1)} async-done(((bf16[896,512]{1,0:T(8,128)(2,1)}), bf16[7168,512]{1,0:T(8,128)(2,1)}) %all-gather.4.cloned.1.call-update) | async-done | bytes 7340048 | tf_op jit(solution)/shard_map/all_gather | solution.py:107
  253.4 6.3 %fusion.5 = f32[768,512]{1,0:T(8,128)S(1)} fusion(bf16[768,3712]{1,0:T(8,128)(2,1)} %bitcast.112, s32[]{:T(128)S(6)} %select_n.74, bf16[2,3584,512]{2,1,0:T(8,128)(2,1)} %bitcast.116), kind=kOutput, calls=%fused_computation.13 | convolution fusion | flops 2919235584 | bytes 14614532 | tf_op jit(solution)/shard_map/dot_general | solution.py:114
  259.8 1.2 copy-done.8
  260.9 3.1 %fusion.2 = f32[768,512]{1,0:T(8,128)S(1)} fusion(bf16[768,3712]{1,0:T(8,128)(2,1)S(1)} %bitcast.113, s32[]{:T(128)S(6)} %select_n.73, bf16[2,3584,512]{2,1,0:T(8,128)(2,1)S(1)} %bitcast.117), kind=kOutput, calls=%fused_computation.11 | convolution fusion | flops 2919235584 | bytes 14614532 | tf_op jit(solution)/shard_map/dot_general | solution.py:114
  264.5 1.8 collective-permute-start
  266.2 1.8 all-to-all-done.4
  268.2 1.5 convert.5
  269.6 1.5 convert.6
  271.1 6.3 %collective-permute-done = bf16[768,256]{1,0:T(8,128)(2,1)} collective-permute-done((bf16[768,256]{1,0:T(8,128)(2,1)S(1)}, bf16[768,256]{1,0:T(8,128)(2,1)}, u32[]{:S(2)}, u32[]{:S(2)}) %collective-permute-start) | collective-permute-done | bytes 393248 | tf_op jit(solution)/shard_map/ppermute | solution.py:123
  277.4 1.1 pad_maximum_fusion.1
  278.5 0.6 gather_fusion.2
  279.3 1.0 copy.44
  280.3 0.9 copy.51
  (52 shorter events, 3.0 us)
Async XLA Ops:
  7.2 1.2 copy-start
  7.2 88.7 %reduce-scatter.2.cloned.1.call-start = ((), (), s32[]{:S(2)}) async-start(), calls=%async_computation.6 | async-start | bytes 4587520 | tf_op jit(solution)/shard_map/reduce_scatter | solution.py:89
  12.2 0.7 copy-start.9
  12.2 1.4 copy-start.7
  12.2 1.9 copy-start.10
  12.2 2.3 copy-start.4
  12.2 210.4 %all-gather.6.cloned.1.call-start = ((), (), s32[]{:S(2)}) async-start(), calls=%async_computation.8 | async-start | bytes 8552448 | tf_op jit(solution)/shard_map/all_gather | solution.py:99
  95.9 1.2 copy-start.5
  102.2 3.8 %copy-start.1 = (s32[16]{0:T(128)S(1)}, s32[16]{0:T(128)}, u32[]{:S(2)}) copy-start(s32[16]{0:T(128)} %param.22) | copy-start | bytes 196
  102.2 29.1 %all-to-all-start.1 = ((bf16[1,16,56,512]{3,2,0,1:T(8,128)(2,1)}), bf16[1,16,56,512]{3,2,0,1:T(8,128)(2,1)S(1)}, u32[]{:S(2)}, u32[]{:S(2)}) async-start(bf16[1,16,56,512]{3,2,0,1:T(8,128)(2,1)} %bitcast.106), calls=%async_computation.2 | async-start | bytes 1835008 | tf_op jit(solution)/shard_map/all_to_all | solution.py:34
  132.9 31.2 %all-to-all-start.2 = ((bf16[1,16,56,512]{3,2,0,1:T(8,128)(2,1)}), bf16[1,16,56,512]{3,2,0,1:T(8,128)(2,1)S(1)}, u32[]{:S(2)}, u32[]{:S(2)}) async-start(bf16[1,16,56,512]{3,2,0,1:T(8,128)(2,1)} %bitcast.28), calls=%async_computation.3 | async-start | bytes 1835008 | tf_op jit(solution)/shard_map/all_to_all | solution.py:36
  136.7 116.7 %all-gather.4.cloned.1.call-start = ((), (), s32[]{:S(2)}) async-start(), calls=%async_computation.7 | async-start | bytes 8257536 | tf_op jit(solution)/shard_map/all_gather | solution.py:107
  164.1 0.9 copy-start.2
  218.8 49.2 %all-to-all-start.4 = ((bf16[2,16,56,512]{3,2,0,1:T(8,128)(2,1)}), bf16[2,16,56,512]{3,2,0,1:T(8,128)(2,1)S(1)}, u32[]{:S(2)}, u32[]{:S(2)}) async-start(bf16[2,16,56,512]{3,2,0,1:T(8,128)(2,1)} %bitcast.102), calls=%async_computation.5 | async-start | bytes 3670016 | tf_op jit(solution)/shard_map/all_to_all | solution.py:36
  253.4 6.3 %copy-start.6 = (bf16[32,24,3712]{2,1,0:T(8,128)(2,1)S(1)}, bf16[32,24,3712]{2,1,0:T(8,128)(2,1)}, u32[]{:S(2)}) copy-start(bf16[32,24,3712]{2,1,0:T(8,128)(2,1)} %all-gather.6.cloned.1.call-done) | copy-start | bytes 17104900
  253.4 7.5 %copy-start.8 = (bf16[7168,512]{1,0:T(8,128)(2,1)S(1)}, bf16[7168,512]{1,0:T(8,128)(2,1)}, u32[]{:S(2)}) copy-start(bf16[7168,512]{1,0:T(8,128)(2,1)} %all-gather.4.cloned.1.call-done) | copy-start | bytes 22020100
  264.5 13.0 %collective-permute-start = (bf16[768,256]{1,0:T(8,128)(2,1)S(1)}, bf16[768,256]{1,0:T(8,128)(2,1)}, u32[]{:S(2)}, u32[]{:S(2)}) collective-permute-start(bf16[768,256]{1,0:T(8,128)(2,1)S(1)} %get-tuple-element.30), channel_id=1, source_target_pairs={{0,1},{1,0},{2,3},{3,2},{4,5},{5,4},{6,7},{7,6},{8,9},{9,8},{10,11... | collective-permute-start | bytes 1179656 | tf_op jit(solution)/shard_map/ppermute | solution.py:123
  279.1 1.2 copy-start.3
Sparse Core Ops, SparseCore 0:
  12.3 46.2 reduce-scatter.1
  96.1 106.2 all-gather.5
  204.8 48.6 all-gather.3

commit v13 on v10

--- a/solution.py
+++ b/solution.py
@@ -27,12 +27,12 @@
     return stepped.astype(jnp.bfloat16), first_next, second_next
 
 
-def migrate(state, group_source, groups):
+def migrate(state, group_source, groups, mode=None):
     layers, rows_dev, width = state.shape
     piece_rows = rows_dev // groups
     split = state.reshape(layers, groups, piece_rows, width)
     spread = lax.all_to_all(split, "grp", split_axis=1, concat_axis=1, tiled=True)
-    chosen = jnp.take(spread, group_source, axis=1, mode="clip", unique_indices=True)
+    chosen = jnp.take(spread, group_source, axis=1, mode=mode)
     home = lax.all_to_all(chosen, "grp", split_axis=1, concat_axis=1, tiled=True)
     return home.reshape(layers, rows_dev, width)
 
@@ -99,10 +99,11 @@
     near = lax.all_gather(by_group, "ylo", axis=0, tiled=False)
     near = near.reshape(2 * groups * capacity, D + SCALE_PAD)
     stepped, first_next, second_next = adamw(weights[0], first_moment[0], second_moment[0], grads)
-    new_weight = migrate(stepped[None], group_source, groups)[0]
+    weight_home = migrate(stepped[None], group_source, groups)
+    new_weight = weight_home[0]
     moments = jnp.stack([first_next.astype(jnp.bfloat16), second_next.astype(jnp.bfloat16)])
     moments, new_weight = lax.optimization_barrier((moments, new_weight))
-    moved = migrate(moments, group_source, groups)
+    moved = migrate(moments, group_source, groups, mode="clip")
 
     both = lax.all_gather(new_weight, ("xhi", "dp"), axis=0, tiled=True)
     both = both.reshape(2, -1, width)
@@ -126,7 +127,7 @@
     hidden = jnp.transpose(mine, (2, 1, 0, 3, 4)).reshape(1, 1, experts * capacity, hidden_units)
     return (
         hidden,
-        new_weight[None],
+        weight_home,
         moved[0].astype(jnp.float32)[None],
         moved[1].astype(jnp.float32)[None],
     )

time: 290 us -> 286 us (0.986)
  blocking collectives: 130 us -> 80.3 us
  waiting for transfers between devices: 87.2 us -> 128 us
  starting transfers between devices: 13.2 us -> 16.9 us
    all_to_all x1 -> x0, blocking collectives: 50.2 us -> none  [migrate(): lax.all_to_all(split, 'grp', split_axis=1, concat_axis=1, tiled=True)]
    all_to_all x1 -> x2, waiting for transfers between devices: 24.6 us -> 70.4 us  [migrate(): lax.all_to_all(split, 'grp', split_axis=1, concat_axis=1, tiled=True)]
    all_to_all x2, waiting for transfers between devices: 26.5 us -> 42.3 us  [migrate(): lax.all_to_all(chosen, 'grp', split_axis=1, concat_axis=1, tiled=True)]
    all_gather x1, waiting for transfers between devices: 29.7 us -> 14.7 us  [local(): both = lax.all_gather(new_weight, ('xhi', 'dp'), axis=0, tiled=True)]
    ppermute x1, waiting for transfers between devices: 6.35 us -> 0.01 us  [local(): for_partner = lax.ppermute(other, 'xhi', perm=[(0, 1), (1, 0)])]
    all_to_all x1 -> x2, starting transfers between devices: 3.78 us -> 7.5 us  [migrate(): lax.all_to_all(split, 'grp', split_axis=1, concat_axis=1, tiled=True)]
  transfers between devices with their start and end apart: 7 -> 8, of which waited for: 5 -> 5; matrix products, arithmetic and copies ran while one was open for 10% -> 12% of each run, Pallas kernels for 0% -> 0%
where the time goes in v13:
time: 286 us; the launch traced here: 285 us
  waiting for transfers between devices  128 us (45%)
  blocking collectives  80.3 us (28%)
  starting transfers between devices  16.9 us (6%)
  local copies, waits for them, and re-layouts  16.2 us (6%)
  other arithmetic  15.4 us (5%)
  between operations  14.7 us (5%)
  matrix products  14.2 us (5%)
    all_to_all x1, blocking collectives, local(): lax.all_to_all(payload, 'grp', split_axis=0, concat_axis=0, tiled=True)  80.3 us
    all_to_all x2, waiting for transfers between devices, migrate(): lax.all_to_all(split, 'grp', split_axis=1, concat_axis=1, tiled=True)  70.4 us
    all_to_all x2, waiting for transfers between devices, migrate(): lax.all_to_all(chosen, 'grp', split_axis=1, concat_axis=1, tiled=True)  42.3 us
    all_gather x1, waiting for transfers between devices, local(): both = lax.all_gather(new_weight, ('xhi', 'dp'), axis=0, tiled=True)  14.7 us
    dot_general x2, matrix products, local(): jnp.dot(near, both[k], preferred_element_type=jnp.float32)  9.38 us
    all_to_all x2, starting transfers between devices, migrate(): lax.all_to_all(chosen, 'grp', split_axis=1, concat_axis=1, tiled=True)  7.55 us
    all_to_all x2, starting transfers between devices, migrate(): lax.all_to_all(split, 'grp', split_axis=1, concat_axis=1, tiled=True)  7.5 us
    unnamed x24, local copies, waits for them, and re-layouts  6.1 us
  transfers between devices with their start and end apart: 8, of which 5 were waited for; matrix products, arithmetic and copies ran while one was open for 12% of the time, Pallas kernels for 0%

profile of v13, /device:TPU:4, one launch (start us, length us, event | category | flops | bytes accessed | tf_op | source)
XLA Modules:
  0.0 285.2 jit_solution(17586691552052428238)
XLA Ops:
  7.2 1.1 copy-done
  8.3 3.8 %convolution_convert_fusion = bf16[3584,512]{1,0:T(8,128)(2,1)} fusion(bf16[1,1,128,3584]{3,2,1,0:T(8,128)(2,1)S(1)} %copy-done, bf16[1,1,128,512]{3,2,1,0:T(8,128)(2,1)} %param.14), kind=kOutput, calls=%fused_computation.6 | convolution fusion | flops 471597056 | bytes 4718592 | tf_op jit(solution)/shard_map/dot_general | solution.py:90
  14.5 0.9 convolution_convert_fusion.1
  15.6 80.3 %all_to_all.25 = bf16[16,24,3712]{2,1,0:T(8,128)(2,1)} all-to-all(bf16[16,24,3712]{2,1,0:T(8,128)(2,1)S(1)} %fusion.7), channel_id=1, replica_groups=mesh['dp'=4,'grp'=16,'ylo'=2,'xhi'=2] {'grp'}, dimensions={0} | all-to-all | bytes 5701632 | tf_op jit(solution)/shard_map/all_to_all | solution.py:87
  96.0 1.1 copy-done.5
  97.1 5.1 %fusion.10 = (bf16[896,512]{1,0:T(8,128)(2,1)}, bf16[1,896,512]{2,1,0:T(8,128)(2,1)S(1)}, bf16[1,896,512]{2,1,0:T(8,128)(2,1)}) fusion(bf16[1,896,512]{2,1,0:T(8,128)(2,1)S(1)} %copy-done.5, bf16[896,512]{1,0:T(8,128)(2,1)} %reduce-scatter.2.cloned.1.call-done, f32[1,896,512]{2,1,0:T(8,128)} %param.16, f32[1,896,512]{2,1,0:T(8,128)} %param.17), kind=kLoop, calls=%fused_computation.23 | loop fusion | flops 8257536 | bytes 8257536 | tf_op jit(solution)/shard_map/convert_element_type | solution.py:27
  102.3 3.8 %all-to-all-start.1 = ((bf16[1,16,56,512]{3,2,0,1:T(8,128)(2,1)}), bf16[1,16,56,512]{3,2,0,1:T(8,128)(2,1)S(1)}, u32[]{:S(2)}, u32[]{:S(2)}) async-start(bf16[1,16,56,512]{3,2,0,1:T(8,128)(2,1)} %bitcast.127), calls=%async_computation.2 | async-start | bytes 1835008 | tf_op jit(solution)/shard_map/all_to_all | solution.py:34
  106.1 0.7 gather_fusion
  106.8 24.6 %all-to-all-done.1 = bf16[1,16,56,512]{3,2,0,1:T(8,128)(2,1)S(1)} async-done(((bf16[1,16,56,512]{3,2,0,1:T(8,128)(2,1)}), bf16[1,16,56,512]{3,2,0,1:T(8,128)(2,1)S(1)}, u32[]{:S(2)}, u32[]{:S(2)}) %all-to-all-start.1) | async-done | bytes 917536 | tf_op jit(solution)/shard_map/all_to_all | solution.py:34
  131.4 1.5 gather_fusion.1
  132.9 2.2 fusion.26
  135.2 3.8 %all-to-all-start.2 = ((bf16[1,16,56,512]{3,2,0,1:T(8,128)(2,1)}), bf16[1,16,56,512]{3,2,0,1:T(8,128)(2,1)S(1)}, u32[]{:S(2)}, u32[]{:S(2)}) async-start(bf16[1,16,56,512]{3,2,0,1:T(8,128)(2,1)} %fusion.26), calls=%async_computation.3 | async-start | bytes 1835008 | tf_op jit(solution)/shard_map/all_to_all | solution.py:36
  139.0 2.6 pad_maximum_fusion
  141.6 24.7 %all-to-all-done.2 = bf16[1,16,56,512]{3,2,0,1:T(8,128)(2,1)S(1)} async-done(((bf16[1,16,56,512]{3,2,0,1:T(8,128)(2,1)}), bf16[1,16,56,512]{3,2,0,1:T(8,128)(2,1)S(1)}, u32[]{:S(2)}, u32[]{:S(2)}) %all-to-all-start.2) | async-done | bytes 917536 | tf_op jit(solution)/shard_map/all_to_all | solution.py:36
  166.4 0.9 copy-done.2
  167.3 3.0 %copy.50 = bf16[2,16,56,512]{3,2,0,1:T(8,128)(2,1)} copy(bf16[2,16,56,512]{3,2,1,0:T(8,128)(2,1)} %bitcast.122) | data formatting | bytes 3670016 | tf_op jit(solution)/shard_map/reshape | solution.py:33
  170.3 3.7 %all-to-all-start.3 = ((bf16[2,16,56,512]{3,2,0,1:T(8,128)(2,1)}), bf16[2,16,56,512]{3,2,0,1:T(8,128)(2,1)S(1)}, u32[]{:S(2)}, u32[]{:S(2)}) async-start(bf16[2,16,56,512]{3,2,0,1:T(8,128)(2,1)} %copy.50), calls=%async_computation.4 | async-start | bytes 3670016 | tf_op jit(solution)/shard_map/all_to_all | solution.py:34
  174.0 45.8 %all-to-all-done.3 = bf16[2,16,56,512]{3,2,0,1:T(8,128)(2,1)S(1)} async-done(((bf16[2,16,56,512]{3,2,0,1:T(8,128)(2,1)}), bf16[2,16,56,512]{3,2,0,1:T(8,128)(2,1)S(1)}, u32[]{:S(2)}, u32[]{:S(2)}) %all-to-all-start.3) | async-done | bytes 1835040 | tf_op jit(solution)/shard_map/all_to_all | solution.py:34
  219.9 1.9 gather_fusion.3
  221.7 3.7 %all-to-all-start.4 = ((bf16[2,16,56,512]{3,2,0,1:T(8,128)(2,1)}), bf16[2,16,56,512]{3,2,0,1:T(8,128)(2,1)S(1)}, u32[]{:S(2)}, u32[]{:S(2)}) async-start(bf16[2,16,56,512]{3,2,0,1:T(8,128)(2,1)} %bitcast.123), calls=%async_computation.5 | async-start | bytes 3670016 | tf_op jit(solution)/shard_map/all_to_all | solution.py:36
  225.5 0.9 slice.59
  226.6 14.7 %all-gather.4.cloned.1.call-done = bf16[7168,512]{1,0:T(8,128)(2,1)} async-done(((bf16[896,512]{1,0:T(8,128)(2,1)}), bf16[7168,512]{1,0:T(8,128)(2,1)}) %all-gather.4.cloned.1.call-update) | async-done | bytes 7340048 | tf_op jit(solution)/shard_map/all_gather | solution.py:108
  241.4 6.3 %fusion.18 = f32[1,768,512]{2,1,0:T(8,128)S(1)} fusion(bf16[768,3712]{1,0:T(8,128)(2,1)} %bitcast.133, bf16[2,3584,512]{2,1,0:T(8,128)(2,1)} %bitcast.137), kind=kOutput, calls=%fused_computation.30 | convolution fusion | flops 2919235584 | bytes 14614528 | tf_op jit(solution)/shard_map/dot_general | solution.py:112
  247.7 1.2 copy-done.8
  248.9 3.1 %fusion.15 = f32[1,768,512]{2,1,0:T(8,128)S(1)} fusion(bf16[768,3712]{1,0:T(8,128)(2,1)S(1)} %bitcast.134, bf16[2,3584,512]{2,1,0:T(8,128)(2,1)S(1)} %bitcast.138), kind=kOutput, calls=%fused_computation.29 | convolution fusion | flops 2919235584 | bytes 14614528 | tf_op jit(solution)/shard_map/dot_general | solution.py:112
  252.5 1.8 collective-permute-start
  254.2 17.5 %all-to-all-done.4 = bf16[2,16,56,512]{3,2,0,1:T(8,128)(2,1)S(1)} async-done(((bf16[2,16,56,512]{3,2,0,1:T(8,128)(2,1)}), bf16[2,16,56,512]{3,2,0,1:T(8,128)(2,1)S(1)}, u32[]{:S(2)}, u32[]{:S(2)}) %all-to-all-start.4) | async-done | bytes 1835040 | tf_op jit(solution)/shard_map/all_to_all | solution.py:36
  271.9 1.5 convert.5
  273.4 1.5 convert.6
  274.8 1.1 pad_maximum_fusion.2
  276.7 1.0 copy.49
  277.8 0.9 copy.56
  (57 shorter events, 3.7 us)
Async XLA Ops:
  7.2 1.2 copy-start
  7.2 88.7 %reduce-scatter.2.cloned.1.call-start = ((), (), s32[]{:S(2)}) async-start(), calls=%async_computation.6 | async-start | bytes 4587520 | tf_op jit(solution)/shard_map/reduce_scatter | solution.py:89
  12.2 0.7 copy-start.9
  12.2 1.4 copy-start.7
  12.2 1.9 copy-start.10
  12.2 2.3 copy-start.4
  12.2 213.3 %all-gather.6.cloned.1.call-start = ((), (), s32[]{:S(2)}) async-start(), calls=%async_computation.8 | async-start | bytes 8552448 | tf_op jit(solution)/shard_map/all_gather | solution.py:99
  95.9 1.2 copy-start.5
  102.2 3.8 %copy-start.1 = (s32[16]{0:T(128)S(1)}, s32[16]{0:T(128)}, u32[]{:S(2)}) copy-start(s32[16]{0:T(128)} %param.22) | copy-start | bytes 196
  102.3 29.1 %all-to-all-start.1 = ((bf16[1,16,56,512]{3,2,0,1:T(8,128)(2,1)}), bf16[1,16,56,512]{3,2,0,1:T(8,128)(2,1)S(1)}, u32[]{:S(2)}, u32[]{:S(2)}) async-start(bf16[1,16,56,512]{3,2,0,1:T(8,128)(2,1)} %bitcast.127), calls=%async_computation.2 | async-start | bytes 1835008 | tf_op jit(solution)/shard_map/all_to_all | solution.py:34
  135.2 31.2 %all-to-all-start.2 = ((bf16[1,16,56,512]{3,2,0,1:T(8,128)(2,1)}), bf16[1,16,56,512]{3,2,0,1:T(8,128)(2,1)S(1)}, u32[]{:S(2)}, u32[]{:S(2)}) async-start(bf16[1,16,56,512]{3,2,0,1:T(8,128)(2,1)} %fusion.26), calls=%async_computation.3 | async-start | bytes 1835008 | tf_op jit(solution)/shard_map/all_to_all | solution.py:36
  139.0 102.4 %all-gather.4.cloned.1.call-start = ((), (), s32[]{:S(2)}) async-start(), calls=%async_computation.7 | async-start | bytes 8257536 | tf_op jit(solution)/shard_map/all_gather | solution.py:108
  166.4 0.9 copy-start.2
  170.3 49.6 %all-to-all-start.3 = ((bf16[2,16,56,512]{3,2,0,1:T(8,128)(2,1)}), bf16[2,16,56,512]{3,2,0,1:T(8,128)(2,1)S(1)}, u32[]{:S(2)}, u32[]{:S(2)}) async-start(bf16[2,16,56,512]{3,2,0,1:T(8,128)(2,1)} %copy.50), calls=%async_computation.4 | async-start | bytes 3670016 | tf_op jit(solution)/shard_map/all_to_all | solution.py:34
  221.7 50.0 %all-to-all-start.4 = ((bf16[2,16,56,512]{3,2,0,1:T(8,128)(2,1)}), bf16[2,16,56,512]{3,2,0,1:T(8,128)(2,1)S(1)}, u32[]{:S(2)}, u32[]{:S(2)}) async-start(bf16[2,16,56,512]{3,2,0,1:T(8,128)(2,1)} %bitcast.123), calls=%async_computation.5 | async-start | bytes 3670016 | tf_op jit(solution)/shard_map/all_to_all | solution.py:36
  241.4 6.3 %copy-start.6 = (bf16[32,24,3712]{2,1,0:T(8,128)(2,1)S(1)}, bf16[32,24,3712]{2,1,0:T(8,128)(2,1)}, u32[]{:S(2)}) copy-start(bf16[32,24,3712]{2,1,0:T(8,128)(2,1)} %all-gather.6.cloned.1.call-done) | copy-start | bytes 17104900
  241.4 7.5 %copy-start.8 = (bf16[7168,512]{1,0:T(8,128)(2,1)S(1)}, bf16[7168,512]{1,0:T(8,128)(2,1)}, u32[]{:S(2)}) copy-start(bf16[7168,512]{1,0:T(8,128)(2,1)} %all-gather.4.cloned.1.call-done) | copy-start | bytes 22020100
  252.5 22.4 %collective-permute-start = (bf16[768,256]{1,0:T(8,128)(2,1)S(1)}, bf16[768,256]{1,0:T(8,128)(2,1)}, u32[]{:S(2)}, u32[]{:S(2)}) collective-permute-start(bf16[768,256]{1,0:T(8,128)(2,1)S(1)} %get-tuple-element.30), channel_id=1, source_target_pairs={{0,1},{1,0},{2,3},{3,2},{4,5},{5,4},{6,7},{7,6},{8,9},{9,8},{10,11... | collective-permute-start | bytes 1179656 | tf_op jit(solution)/shard_map/ppermute | solution.py:123
  276.5 1.2 copy-start.3
Sparse Core Ops, SparseCore 0:
  12.3 46.2 reduce-scatter.1
  96.1 95.5 all-gather.5
  194.1 47.2 all-gather.3

commit v14 on v13

--- a/solution.py
+++ b/solution.py
@@ -121,9 +121,9 @@
     own = lax.dynamic_index_in_dim(result, xhi, axis=0, keepdims=False)
     other = lax.dynamic_index_in_dim(result, 1 - xhi, axis=0, keepdims=False)
     for_partner = lax.ppermute(other, "xhi", perm=[(0, 1), (1, 0)])
-    mine = jnp.stack([own, for_partner]).reshape(2, 2, groups, capacity, hidden_units)
-    flip = jnp.arange(2, dtype=jnp.int32)
-    mine = jnp.take(mine, flip ^ xhi, axis=0)
+    mine = jnp.where(
+        xhi == 0, jnp.stack([own, for_partner]), jnp.stack([for_partner, own])
+    ).reshape(2, 2, groups, capacity, hidden_units)
     hidden = jnp.transpose(mine, (2, 1, 0, 3, 4)).reshape(1, 1, experts * capacity, hidden_units)
     return (
         hidden,

time: 286 us -> 285 us (level)
  no operation moved by 1% of the time
where the time goes in v14:
time: 285 us
  waiting for transfers between devices  128 us (45%)
  blocking collectives  80.3 us (28%)
  starting transfers between devices  16.9 us (6%)
  local copies, waits for them, and re-layouts  15.5 us (5%)
  other arithmetic  15.4 us (5%)
  between operations  14.6 us (5%)
  matrix products  14.2 us (5%)
    all_to_all x1, blocking collectives, local(): lax.all_to_all(payload, 'grp', split_axis=0, concat_axis=0, tiled=True)  80.3 us
    all_to_all x2, waiting for transfers between devices, migrate(): lax.all_to_all(split, 'grp', split_axis=1, concat_axis=1, tiled=True)  70.4 us
    all_to_all x2, waiting for transfers between devices, migrate(): lax.all_to_all(chosen, 'grp', split_axis=1, concat_axis=1, tiled=True)  42.3 us
    all_gather x1, waiting for transfers between devices, local(): both = lax.all_gather(new_weight, ('xhi', 'dp'), axis=0, tiled=True)  14.8 us
    dot_general x2, matrix products, local(): jnp.dot(near, both[k], preferred_element_type=jnp.float32)  9.38 us
    all_to_all x2, starting transfers between devices, migrate(): lax.all_to_all(chosen, 'grp', split_axis=1, concat_axis=1, tiled=True)  7.55 us
    all_to_all x2, starting transfers between devices, migrate(): lax.all_to_all(split, 'grp', split_axis=1, concat_axis=1, tiled=True)  7.5 us
    unnamed x24, local copies, waits for them, and re-layouts  6 us
  transfers between devices with their start and end apart: 8, of which 5 were waited for; matrix products, arithmetic and copies ran while one was open for 12% of the time, Pallas kernels for 0%

profile of v14, /device:TPU:4, one launch (start us, length us, event | category | flops | bytes accessed | tf_op | source)
XLA Modules:
  0.0 284.6 jit_solution(10818399610023016619)
XLA Ops:
  7.2 1.1 copy-done
  8.3 3.8 %convolution_convert_fusion = bf16[3584,512]{1,0:T(8,128)(2,1)} fusion(bf16[1,1,128,3584]{3,2,1,0:T(8,128)(2,1)S(1)} %copy-done, bf16[1,1,128,512]{3,2,1,0:T(8,128)(2,1)} %param.14), kind=kOutput, calls=%fused_computation.5 | convolution fusion | flops 471597056 | bytes 4718592 | tf_op jit(solution)/shard_map/dot_general | solution.py:90
  14.5 0.9 convolution_convert_fusion.1
  15.6 80.3 %all_to_all.25 = bf16[16,24,3712]{2,1,0:T(8,128)(2,1)} all-to-all(bf16[16,24,3712]{2,1,0:T(8,128)(2,1)S(1)} %fusion.7), channel_id=1, replica_groups=mesh['dp'=4,'grp'=16,'ylo'=2,'xhi'=2] {'grp'}, dimensions={0} | all-to-all | bytes 5701632 | tf_op jit(solution)/shard_map/all_to_all | solution.py:87
  96.0 1.1 copy-done.5
  97.1 5.1 %fusion.10 = (bf16[896,512]{1,0:T(8,128)(2,1)}, bf16[1,896,512]{2,1,0:T(8,128)(2,1)S(1)}, bf16[1,896,512]{2,1,0:T(8,128)(2,1)}) fusion(bf16[1,896,512]{2,1,0:T(8,128)(2,1)S(1)} %copy-done.5, bf16[896,512]{1,0:T(8,128)(2,1)} %reduce-scatter.2.cloned.1.call-done, f32[1,896,512]{2,1,0:T(8,128)} %param.16, f32[1,896,512]{2,1,0:T(8,128)} %param.17), kind=kLoop, calls=%fused_computation.22 | loop fusion | flops 8257536 | bytes 8257536 | tf_op jit(solution)/shard_map/convert_element_type | solution.py:27
  102.3 3.8 %all-to-all-start.1 = ((bf16[1,16,56,512]{3,2,0,1:T(8,128)(2,1)}), bf16[1,16,56,512]{3,2,0,1:T(8,128)(2,1)S(1)}, u32[]{:S(2)}, u32[]{:S(2)}) async-start(bf16[1,16,56,512]{3,2,0,1:T(8,128)(2,1)} %bitcast.125), calls=%async_computation.2 | async-start | bytes 1835008 | tf_op jit(solution)/shard_map/all_to_all | solution.py:34
  106.1 0.7 gather_fusion
  106.8 24.6 %all-to-all-done.1 = bf16[1,16,56,512]{3,2,0,1:T(8,128)(2,1)S(1)} async-done(((bf16[1,16,56,512]{3,2,0,1:T(8,128)(2,1)}), bf16[1,16,56,512]{3,2,0,1:T(8,128)(2,1)S(1)}, u32[]{:S(2)}, u32[]{:S(2)}) %all-to-all-start.1) | async-done | bytes 917536 | tf_op jit(solution)/shard_map/all_to_all | solution.py:34
  131.4 1.5 gather_fusion.1
  132.9 2.2 fusion.26
  135.2 3.8 %all-to-all-start.2 = ((bf16[1,16,56,512]{3,2,0,1:T(8,128)(2,1)}), bf16[1,16,56,512]{3,2,0,1:T(8,128)(2,1)S(1)}, u32[]{:S(2)}, u32[]{:S(2)}) async-start(bf16[1,16,56,512]{3,2,0,1:T(8,128)(2,1)} %fusion.26), calls=%async_computation.3 | async-start | bytes 1835008 | tf_op jit(solution)/shard_map/all_to_all | solution.py:36
  139.0 2.6 pad_maximum_fusion
  141.6 24.7 %all-to-all-done.2 = bf16[1,16,56,512]{3,2,0,1:T(8,128)(2,1)S(1)} async-done(((bf16[1,16,56,512]{3,2,0,1:T(8,128)(2,1)}), bf16[1,16,56,512]{3,2,0,1:T(8,128)(2,1)S(1)}, u32[]{:S(2)}, u32[]{:S(2)}) %all-to-all-start.2) | async-done | bytes 917536 | tf_op jit(solution)/shard_map/all_to_all | solution.py:36
  166.4 0.9 copy-done.2
  167.3 3.0 %copy.50 = bf16[2,16,56,512]{3,2,0,1:T(8,128)(2,1)} copy(bf16[2,16,56,512]{3,2,1,0:T(8,128)(2,1)} %bitcast.120) | data formatting | bytes 3670016 | tf_op jit(solution)/shard_map/reshape | solution.py:33
  170.3 3.7 %all-to-all-start.3 = ((bf16[2,16,56,512]{3,2,0,1:T(8,128)(2,1)}), bf16[2,16,56,512]{3,2,0,1:T(8,128)(2,1)S(1)}, u32[]{:S(2)}, u32[]{:S(2)}) async-start(bf16[2,16,56,512]{3,2,0,1:T(8,128)(2,1)} %copy.50), calls=%async_computation.4 | async-start | bytes 3670016 | tf_op jit(solution)/shard_map/all_to_all | solution.py:34
  174.0 45.8 %all-to-all-done.3 = bf16[2,16,56,512]{3,2,0,1:T(8,128)(2,1)S(1)} async-done(((bf16[2,16,56,512]{3,2,0,1:T(8,128)(2,1)}), bf16[2,16,56,512]{3,2,0,1:T(8,128)(2,1)S(1)}, u32[]{:S(2)}, u32[]{:S(2)}) %all-to-all-start.3) | async-done | bytes 1835040 | tf_op jit(solution)/shard_map/all_to_all | solution.py:34
  219.9 1.9 gather_fusion.2
  221.7 3.7 %all-to-all-start.4 = ((bf16[2,16,56,512]{3,2,0,1:T(8,128)(2,1)}), bf16[2,16,56,512]{3,2,0,1:T(8,128)(2,1)S(1)}, u32[]{:S(2)}, u32[]{:S(2)}) async-start(bf16[2,16,56,512]{3,2,0,1:T(8,128)(2,1)} %bitcast.121), calls=%async_computation.5 | async-start | bytes 3670016 | tf_op jit(solution)/shard_map/all_to_all | solution.py:36
  225.5 0.9 slice.57
  226.6 14.8 %all-gather.4.cloned.1.call-done = bf16[7168,512]{1,0:T(8,128)(2,1)} async-done(((bf16[896,512]{1,0:T(8,128)(2,1)}), bf16[7168,512]{1,0:T(8,128)(2,1)}) %all-gather.4.cloned.1.call-update) | async-done | bytes 7340048 | tf_op jit(solution)/shard_map/all_gather | solution.py:108
  241.4 6.3 %fusion.15 = f32[1,768,512]{2,1,0:T(8,128)S(1)} fusion(bf16[768,3712]{1,0:T(8,128)(2,1)} %bitcast.131, bf16[2,3584,512]{2,1,0:T(8,128)(2,1)} %bitcast.135), kind=kOutput, calls=%fused_computation.28 | convolution fusion | flops 2919235584 | bytes 14614528 | tf_op jit(solution)/shard_map/dot_general | solution.py:112
  247.7 1.2 copy-done.8
  248.9 3.1 %fusion.18 = f32[1,768,512]{2,1,0:T(8,128)S(1)} fusion(bf16[768,3712]{1,0:T(8,128)(2,1)S(1)} %bitcast.132, bf16[2,3584,512]{2,1,0:T(8,128)(2,1)S(1)} %bitcast.136), kind=kOutput, calls=%fused_computation.29 | convolution fusion | flops 2919235584 | bytes 14614528 | tf_op jit(solution)/shard_map/dot_general | solution.py:112
  252.5 1.8 collective-permute-start
  254.2 17.5 %all-to-all-done.4 = bf16[2,16,56,512]{3,2,0,1:T(8,128)(2,1)S(1)} async-done(((bf16[2,16,56,512]{3,2,0,1:T(8,128)(2,1)}), bf16[2,16,56,512]{3,2,0,1:T(8,128)(2,1)S(1)}, u32[]{:S(2)}, u32[]{:S(2)}) %all-to-all-start.4) | async-done | bytes 1835040 | tf_op jit(solution)/shard_map/all_to_all | solution.py:36
  271.9 1.5 convert.5
  273.4 1.5 convert.6
  274.9 1.3 fusion.28
  276.2 1.0 copy.49
  277.1 0.9 copy.56
  (52 shorter events, 2.8 us)
Async XLA Ops:
  7.2 1.2 copy-start
  7.2 88.7 %reduce-scatter.2.cloned.1.call-start = ((), (), s32[]{:S(2)}) async-start(), calls=%async_computation.6 | async-start | bytes 4587520 | tf_op jit(solution)/shard_map/reduce_scatter | solution.py:89
  12.2 0.7 copy-start.9
  12.2 1.4 copy-start.7
  12.2 1.9 copy-start.10
  12.2 2.3 copy-start.4
  12.2 213.3 %all-gather.6.cloned.1.call-start = ((), (), s32[]{:S(2)}) async-start(), calls=%async_computation.8 | async-start | bytes 8552448 | tf_op jit(solution)/shard_map/all_gather | solution.py:99
  95.9 1.2 copy-start.5
  102.2 3.8 %copy-start.1 = (s32[16]{0:T(128)S(1)}, s32[16]{0:T(128)}, u32[]{:S(2)}) copy-start(s32[16]{0:T(128)} %param.22) | copy-start | bytes 196
  102.3 29.1 %all-to-all-start.1 = ((bf16[1,16,56,512]{3,2,0,1:T(8,128)(2,1)}), bf16[1,16,56,512]{3,2,0,1:T(8,128)(2,1)S(1)}, u32[]{:S(2)}, u32[]{:S(2)}) async-start(bf16[1,16,56,512]{3,2,0,1:T(8,128)(2,1)} %bitcast.125), calls=%async_computation.2 | async-start | bytes 1835008 | tf_op jit(solution)/shard_map/all_to_all | solution.py:34
  135.2 31.2 %all-to-all-start.2 = ((bf16[1,16,56,512]{3,2,0,1:T(8,128)(2,1)}), bf16[1,16,56,512]{3,2,0,1:T(8,128)(2,1)S(1)}, u32[]{:S(2)}, u32[]{:S(2)}) async-start(bf16[1,16,56,512]{3,2,0,1:T(8,128)(2,1)} %fusion.26), calls=%async_computation.3 | async-start | bytes 1835008 | tf_op jit(solution)/shard_map/all_to_all | solution.py:36
  139.0 102.4 %all-gather.4.cloned.1.call-start = ((), (), s32[]{:S(2)}) async-start(), calls=%async_computation.7 | async-start | bytes 8257536 | tf_op jit(solution)/shard_map/all_gather | solution.py:108
  166.4 0.9 copy-start.2
  170.3 49.6 %all-to-all-start.3 = ((bf16[2,16,56,512]{3,2,0,1:T(8,128)(2,1)}), bf16[2,16,56,512]{3,2,0,1:T(8,128)(2,1)S(1)}, u32[]{:S(2)}, u32[]{:S(2)}) async-start(bf16[2,16,56,512]{3,2,0,1:T(8,128)(2,1)} %copy.50), calls=%async_computation.4 | async-start | bytes 3670016 | tf_op jit(solution)/shard_map/all_to_all | solution.py:34
  221.7 50.0 %all-to-all-start.4 = ((bf16[2,16,56,512]{3,2,0,1:T(8,128)(2,1)}), bf16[2,16,56,512]{3,2,0,1:T(8,128)(2,1)S(1)}, u32[]{:S(2)}, u32[]{:S(2)}) async-start(bf16[2,16,56,512]{3,2,0,1:T(8,128)(2,1)} %bitcast.121), calls=%async_computation.5 | async-start | bytes 3670016 | tf_op jit(solution)/shard_map/all_to_all | solution.py:36
  241.4 6.3 %copy-start.6 = (bf16[32,24,3712]{2,1,0:T(8,128)(2,1)S(1)}, bf16[32,24,3712]{2,1,0:T(8,128)(2,1)}, u32[]{:S(2)}) copy-start(bf16[32,24,3712]{2,1,0:T(8,128)(2,1)} %all-gather.6.cloned.1.call-done) | copy-start | bytes 17104900
  241.4 7.5 %copy-start.8 = (bf16[7168,512]{1,0:T(8,128)(2,1)S(1)}, bf16[7168,512]{1,0:T(8,128)(2,1)}, u32[]{:S(2)}) copy-start(bf16[7168,512]{1,0:T(8,128)(2,1)} %all-gather.4.cloned.1.call-done) | copy-start | bytes 22020100
  252.5 22.4 %collective-permute-start = (bf16[768,256]{1,0:T(8,128)(2,1)S(1)}, bf16[768,256]{1,0:T(8,128)(2,1)}, u32[]{:S(2)}, u32[]{:S(2)}) collective-permute-start(bf16[768,256]{1,0:T(8,128)(2,1)S(1)} %get-tuple-element.30), channel_id=1, source_target_pairs={{0,1},{1,0},{2,3},{3,2},{4,5},{5,4},{6,7},{7,6},{8,9},{9,8},{10,11... | collective-permute-start | bytes 1179656 | tf_op jit(solution)/shard_map/ppermute | solution.py:123
  274.8 2.3 copy-start.3
Sparse Core Ops, SparseCore 0:
  12.3 46.2 reduce-scatter.1
  96.1 95.5 all-gather.5
  194.1 47.2 all-gather.3

commit v15 on v13

--- a/solution.py
+++ b/solution.py
@@ -99,7 +99,7 @@
     near = lax.all_gather(by_group, "ylo", axis=0, tiled=False)
     near = near.reshape(2 * groups * capacity, D + SCALE_PAD)
     stepped, first_next, second_next = adamw(weights[0], first_moment[0], second_moment[0], grads)
-    weight_home = migrate(stepped[None], group_source, groups)
+    weight_home = migrate(stepped[None], group_source, groups, mode="clip")
     new_weight = weight_home[0]
     moments = jnp.stack([first_next.astype(jnp.bfloat16), second_next.astype(jnp.bfloat16)])
     moments, new_weight = lax.optimization_barrier((moments, new_weight))

time: 286 us -> 290 us (1.014)
  blocking collectives: 80.3 us -> 130 us
  waiting for transfers between devices: 128 us -> 87.2 us
  starting transfers between devices: 16.9 us -> 13.2 us
    all_to_all x0 -> x1, blocking collectives: none -> 50.2 us  [migrate(): lax.all_to_all(split, 'grp', split_axis=1, concat_axis=1, tiled=True)]
    all_to_all x2 -> x1, waiting for transfers between devices: 70.4 us -> 24.6 us  [migrate(): lax.all_to_all(split, 'grp', split_axis=1, concat_axis=1, tiled=True)]
    all_to_all x2, waiting for transfers between devices: 42.3 us -> 26.5 us  [migrate(): lax.all_to_all(chosen, 'grp', split_axis=1, concat_axis=1, tiled=True)]
    all_gather x1, waiting for transfers between devices: 14.7 us -> 29.7 us  [local(): both = lax.all_gather(new_weight, ('xhi', 'dp'), axis=0, tiled=True)]
    ppermute x1, waiting for transfers between devices: 0.01 us -> 6.35 us  [local(): for_partner = lax.ppermute(other, 'xhi', perm=[(0, 1), (1, 0)])]
    all_to_all x2 -> x1, starting transfers between devices: 7.5 us -> 3.78 us  [migrate(): lax.all_to_all(split, 'grp', split_axis=1, concat_axis=1, tiled=True)]
  transfers between devices with their start and end apart: 8 -> 7, of which waited for: 5 -> 5; matrix products, arithmetic and copies ran while one was open for 12% -> 10% of each run, Pallas kernels for 0% -> 0%
where the time goes in v15:
time: 290 us; the launch traced here: 288 us
  blocking collectives  130 us (45%)
  waiting for transfers between devices  87.2 us (30%)
  local copies, waits for them, and re-layouts  14.9 us (5%)
  between operations  14.7 us (5%)
  matrix products  14.2 us (5%)
  starting transfers between devices  13.2 us (5%)
  other arithmetic  13.1 us (5%)
    all_to_all x1, blocking collectives, local(): lax.all_to_all(payload, 'grp', split_axis=0, concat_axis=0, tiled=True)  80.3 us
    all_to_all x1, blocking collectives, migrate(): lax.all_to_all(split, 'grp', split_axis=1, concat_axis=1, tiled=True)  50.2 us
    all_gather x1, waiting for transfers between devices, local(): both = lax.all_gather(new_weight, ('xhi', 'dp'), axis=0, tiled=True)  29.7 us
    all_to_all x2, waiting for transfers between devices, migrate(): lax.all_to_all(chosen, 'grp', split_axis=1, concat_axis=1, tiled=True)  26.5 us
    all_to_all x1, waiting for transfers between devices, migrate(): lax.all_to_all(split, 'grp', split_axis=1, concat_axis=1, tiled=True)  24.6 us
    dot_general x2, matrix products, local(): jnp.dot(near, both[k], preferred_element_type=jnp.float32)  9.38 us
    all_to_all x2, starting transfers between devices, migrate(): lax.all_to_all(chosen, 'grp', split_axis=1, concat_axis=1, tiled=True)  7.56 us
    ppermute x1, waiting for transfers between devices, local(): for_partner = lax.ppermute(other, 'xhi', perm=[(0, 1), (1, 0)])  6.35 us
  transfers between devices with their start and end apart: 7, of which 5 were waited for; matrix products, arithmetic and copies ran while one was open for 10% of the time, Pallas kernels for 0%

profile of v15, /device:TPU:4, one launch (start us, length us, event | category | flops | bytes accessed | tf_op | source)
XLA Modules:
  0.0 287.8 jit_solution(12718263698286540359)
XLA Ops:
  7.2 1.1 copy-done
  8.3 3.8 %convolution_convert_fusion = bf16[3584,512]{1,0:T(8,128)(2,1)} fusion(bf16[1,1,128,3584]{3,2,1,0:T(8,128)(2,1)S(1)} %copy-done, bf16[1,1,128,512]{3,2,1,0:T(8,128)(2,1)} %param.14), kind=kOutput, calls=%fused_computation.6 | convolution fusion | flops 471597056 | bytes 4718592 | tf_op jit(solution)/shard_map/dot_general | solution.py:90
  14.5 0.9 convolution_convert_fusion.1
  15.6 80.3 %all_to_all.25 = bf16[16,24,3712]{2,1,0:T(8,128)(2,1)} all-to-all(bf16[16,24,3712]{2,1,0:T(8,128)(2,1)S(1)} %fusion.7), channel_id=1, replica_groups=mesh['dp'=4,'grp'=16,'ylo'=2,'xhi'=2] {'grp'}, dimensions={0} | all-to-all | bytes 5701632 | tf_op jit(solution)/shard_map/all_to_all | solution.py:87
  95.9 1.1 copy-done.5
  97.1 5.1 %fusion.10 = (bf16[896,512]{1,0:T(8,128)(2,1)}, bf16[1,896,512]{2,1,0:T(8,128)(2,1)S(1)}, bf16[1,896,512]{2,1,0:T(8,128)(2,1)}) fusion(bf16[1,896,512]{2,1,0:T(8,128)(2,1)S(1)} %copy-done.5, bf16[896,512]{1,0:T(8,128)(2,1)} %reduce-scatter.2.cloned.1.call-done, f32[1,896,512]{2,1,0:T(8,128)} %param.16, f32[1,896,512]{2,1,0:T(8,128)} %param.17), kind=kLoop, calls=%fused_computation.23 | loop fusion | flops 8257536 | bytes 8257536 | tf_op jit(solution)/shard_map/convert_element_type | solution.py:27
  102.2 3.8 %all-to-all-start.1 = ((bf16[1,16,56,512]{3,2,0,1:T(8,128)(2,1)}), bf16[1,16,56,512]{3,2,0,1:T(8,128)(2,1)S(1)}, u32[]{:S(2)}, u32[]{:S(2)}) async-start(bf16[1,16,56,512]{3,2,0,1:T(8,128)(2,1)} %bitcast.116), calls=%async_computation.2 | async-start | bytes 1835008 | tf_op jit(solution)/shard_map/all_to_all | solution.py:34
  106.1 0.7 gather_fusion
  106.8 24.6 %all-to-all-done.1 = bf16[1,16,56,512]{3,2,0,1:T(8,128)(2,1)S(1)} async-done(((bf16[1,16,56,512]{3,2,0,1:T(8,128)(2,1)}), bf16[1,16,56,512]{3,2,0,1:T(8,128)(2,1)S(1)}, u32[]{:S(2)}, u32[]{:S(2)}) %all-to-all-start.1) | async-done | bytes 917536 | tf_op jit(solution)/shard_map/all_to_all | solution.py:34
  131.4 1.5 gather_fusion.1
  132.9 3.8 %all-to-all-start.2 = ((bf16[1,16,56,512]{3,2,0,1:T(8,128)(2,1)}), bf16[1,16,56,512]{3,2,0,1:T(8,128)(2,1)S(1)}, u32[]{:S(2)}, u32[]{:S(2)}) async-start(bf16[1,16,56,512]{3,2,0,1:T(8,128)(2,1)} %bitcast.28), calls=%async_computation.3 | async-start | bytes 1835008 | tf_op jit(solution)/shard_map/all_to_all | solution.py:36
  136.8 2.6 pad_maximum_fusion
  139.4 24.7 %all-to-all-done.2 = bf16[1,16,56,512]{3,2,0,1:T(8,128)(2,1)S(1)} async-done(((bf16[1,16,56,512]{3,2,0,1:T(8,128)(2,1)}), bf16[1,16,56,512]{3,2,0,1:T(8,128)(2,1)S(1)}, u32[]{:S(2)}, u32[]{:S(2)}) %all-to-all-start.2) | async-done | bytes 917536 | tf_op jit(solution)/shard_map/all_to_all | solution.py:36
  164.1 0.9 copy-done.2
  165.0 1.7 copy.50
  166.8 50.2 %all_to_all.26 = bf16[2,16,56,512]{3,2,0,1:T(8,128)(2,1)S(1)} all-to-all(bf16[2,16,56,512]{3,2,0,1:T(8,128)(2,1)S(1)} %copy.50), channel_id=1, replica_groups=mesh['dp'=4,'grp'=16,'ylo'=2,'xhi'=2] {'grp'}, dimensions={1} | all-to-all | bytes 3670016 | tf_op jit(solution)/shard_map/all_to_all | solution.py:34
  216.9 1.9 gather_fusion.3
  218.8 3.7 %all-to-all-start.4 = ((bf16[2,16,56,512]{3,2,0,1:T(8,128)(2,1)}), bf16[2,16,56,512]{3,2,0,1:T(8,128)(2,1)S(1)}, u32[]{:S(2)}, u32[]{:S(2)}) async-start(bf16[2,16,56,512]{3,2,0,1:T(8,128)(2,1)} %bitcast.112), calls=%async_computation.5 | async-start | bytes 3670016 | tf_op jit(solution)/shard_map/all_to_all | solution.py:36
  222.6 0.9 slice.59
  223.7 29.7 %all-gather.4.cloned.1.call-done = bf16[7168,512]{1,0:T(8,128)(2,1)} async-done(((bf16[896,512]{1,0:T(8,128)(2,1)}), bf16[7168,512]{1,0:T(8,128)(2,1)}) %all-gather.4.cloned.1.call-update) | async-done | bytes 7340048 | tf_op jit(solution)/shard_map/all_gather | solution.py:108
  253.4 6.3 %fusion.18 = f32[1,768,512]{2,1,0:T(8,128)S(1)} fusion(bf16[768,3712]{1,0:T(8,128)(2,1)} %bitcast.122, bf16[2,3584,512]{2,1,0:T(8,128)(2,1)} %bitcast.126), kind=kOutput, calls=%fused_computation.30 | convolution fusion | flops 2919235584 | bytes 14614528 | tf_op jit(solution)/shard_map/dot_general | solution.py:112
  259.7 1.2 copy-done.8
  260.9 3.1 %fusion.15 = f32[1,768,512]{2,1,0:T(8,128)S(1)} fusion(bf16[768,3712]{1,0:T(8,128)(2,1)S(1)} %bitcast.123, bf16[2,3584,512]{2,1,0:T(8,128)(2,1)S(1)} %bitcast.127), kind=kOutput, calls=%fused_computation.29 | convolution fusion | flops 2919235584 | bytes 14614528 | tf_op jit(solution)/shard_map/dot_general | solution.py:112
  264.5 1.8 collective-permute-start
  266.3 1.8 all-to-all-done.4
  268.2 1.5 convert.5
  269.6 1.5 convert.6
  271.1 6.3 %collective-permute-done = bf16[768,256]{1,0:T(8,128)(2,1)} collective-permute-done((bf16[768,256]{1,0:T(8,128)(2,1)S(1)}, bf16[768,256]{1,0:T(8,128)(2,1)}, u32[]{:S(2)}, u32[]{:S(2)}) %collective-permute-start) | collective-permute-done | bytes 393248 | tf_op jit(solution)/shard_map/ppermute | solution.py:123
  277.5 1.1 pad_maximum_fusion.2
  278.5 0.6 gather_fusion.2
  279.3 1.0 copy.49
  280.4 0.9 copy.56
  (53 shorter events, 3.0 us)
Async XLA Ops:
  7.2 1.2 copy-start
  7.2 88.7 %reduce-scatter.2.cloned.1.call-start = ((), (), s32[]{:S(2)}) async-start(), calls=%async_computation.6 | async-start | bytes 4587520 | tf_op jit(solution)/shard_map/reduce_scatter | solution.py:89
  12.2 0.7 copy-start.9
  12.2 1.4 copy-start.7
  12.2 1.9 copy-start.10
  12.2 2.3 copy-start.4
  12.2 210.4 %all-gather.6.cloned.1.call-start = ((), (), s32[]{:S(2)}) async-start(), calls=%async_computation.8 | async-start | bytes 8552448 | tf_op jit(solution)/shard_map/all_gather | solution.py:99
  95.9 1.2 copy-start.5
  102.2 3.8 %copy-start.1 = (s32[16]{0:T(128)S(1)}, s32[16]{0:T(128)}, u32[]{:S(2)}) copy-start(s32[16]{0:T(128)} %param.22) | copy-start | bytes 196
  102.2 29.1 %all-to-all-start.1 = ((bf16[1,16,56,512]{3,2,0,1:T(8,128)(2,1)}), bf16[1,16,56,512]{3,2,0,1:T(8,128)(2,1)S(1)}, u32[]{:S(2)}, u32[]{:S(2)}) async-start(bf16[1,16,56,512]{3,2,0,1:T(8,128)(2,1)} %bitcast.116), calls=%async_computation.2 | async-start | bytes 1835008 | tf_op jit(solution)/shard_map/all_to_all | solution.py:34
  132.9 31.2 %all-to-all-start.2 = ((bf16[1,16,56,512]{3,2,0,1:T(8,128)(2,1)}), bf16[1,16,56,512]{3,2,0,1:T(8,128)(2,1)S(1)}, u32[]{:S(2)}, u32[]{:S(2)}) async-start(bf16[1,16,56,512]{3,2,0,1:T(8,128)(2,1)} %bitcast.28), calls=%async_computation.3 | async-start | bytes 1835008 | tf_op jit(solution)/shard_map/all_to_all | solution.py:36
  136.7 116.7 %all-gather.4.cloned.1.call-start = ((), (), s32[]{:S(2)}) async-start(), calls=%async_computation.7 | async-start | bytes 8257536 | tf_op jit(solution)/shard_map/all_gather | solution.py:108
  164.1 0.9 copy-start.2
  218.8 49.2 %all-to-all-start.4 = ((bf16[2,16,56,512]{3,2,0,1:T(8,128)(2,1)}), bf16[2,16,56,512]{3,2,0,1:T(8,128)(2,1)S(1)}, u32[]{:S(2)}, u32[]{:S(2)}) async-start(bf16[2,16,56,512]{3,2,0,1:T(8,128)(2,1)} %bitcast.112), calls=%async_computation.5 | async-start | bytes 3670016 | tf_op jit(solution)/shard_map/all_to_all | solution.py:36
  253.4 6.3 %copy-start.6 = (bf16[32,24,3712]{2,1,0:T(8,128)(2,1)S(1)}, bf16[32,24,3712]{2,1,0:T(8,128)(2,1)}, u32[]{:S(2)}) copy-start(bf16[32,24,3712]{2,1,0:T(8,128)(2,1)} %all-gather.6.cloned.1.call-done) | copy-start | bytes 17104900
  253.4 7.5 %copy-start.8 = (bf16[7168,512]{1,0:T(8,128)(2,1)S(1)}, bf16[7168,512]{1,0:T(8,128)(2,1)}, u32[]{:S(2)}) copy-start(bf16[7168,512]{1,0:T(8,128)(2,1)} %all-gather.4.cloned.1.call-done) | copy-start | bytes 22020100
  264.5 13.0 %collective-permute-start = (bf16[768,256]{1,0:T(8,128)(2,1)S(1)}, bf16[768,256]{1,0:T(8,128)(2,1)}, u32[]{:S(2)}, u32[]{:S(2)}) collective-permute-start(bf16[768,256]{1,0:T(8,128)(2,1)S(1)} %get-tuple-element.30), channel_id=1, source_target_pairs={{0,1},{1,0},{2,3},{3,2},{4,5},{5,4},{6,7},{7,6},{8,9},{9,8},{10,11... | collective-permute-start | bytes 1179656 | tf_op jit(solution)/shard_map/ppermute | solution.py:123
  279.1 1.2 copy-start.3
Sparse Core Ops, SparseCore 0:
  12.3 46.2 reduce-scatter.1
  96.1 106.2 all-gather.5
  204.8 48.6 all-gather.3
